TPU v7x, 128 devices: a whole 4x4x4 slice. The times are simulated.
128 devices in a mesh: dp: 4 (over x), seq: 8 (over z, core), expert: 4 (over y).
Axes of the slice: x: 4, y: 4, z: 4, core: 2. Of those that a mesh axis runs over, the one named last changes fastest.
Arguments:
- x_in: bfloat16 [4096, 8192], P(('dp', 'seq'), 'expert'), parts along dimension 0, may hold values from -6 to 6
- z_in: bfloat16 [4096, 8192], P(('dp', 'seq'), 'expert'), parts along dimension 0, may hold values from -6 to 6
- step_raw: bfloat16 [4096, 8192], P(('dp', 'seq'), 'expert'), parts along dimension 0, may hold values from -4 to 4
- step_bias: float32 [8192], P('expert'), may hold values from -9 to -2
- decay_rate: float32 [16, 8192], P(None, 'expert'), may hold values from 0.5 to 4
- b_coef: bfloat16 [16, 4096], P(None, ('dp', 'seq')), parts along dimension 1, may hold values from -6 to 6
- c_coef: bfloat16 [16, 4096], P(None, ('dp', 'seq')), parts along dimension 1, may hold values from -6 to 6
- skip_gain: float32 [8192], P('expert'), may hold values from 0.5 to 1.5
- out_proj: bfloat16 [8192, 8192], P('expert', 'seq'), may hold values from -0.0625 to 0.0625
- residual: bfloat16 [4096, 8192], P(('dp', 'seq', 'expert')), parts along dimension 0, may hold values from -6 to 6
- norm_gain: float32 [8192], replicated, may hold values from 0.5 to 1.5
- router_weight: bfloat16 [8192, 16], replicated, may hold values from -0.0625 to 0.0625
- expert_ids: int32 [4096, 2], P(('dp', 'seq', 'expert')), parts along dimension 0, may hold values from 0 to 15, as said below
- gate_weight: bfloat16 [8192, 12288], P(None, ('seq', 'expert')), may hold values from -0.0625 to 0.0625
- up_weight: bfloat16 [8192, 12288], P(None, ('seq', 'expert')), may hold values from -0.0625 to 0.0625
- down_weight: bfloat16 [12288, 8192], P(('seq', 'expert')), may hold values from -0.0546875 to 0.0546875
Outputs:
- final: bfloat16 [4096, 8192], P(('dp', 'seq', 'expert')), parts along dimension 0
There are 4 independent parts, one for each index of `dp`. A program takes and returns all parts, laid end to end along the dimension named above; an argument that names none is the same for every part. Nothing has to cross between parts.
Inputs may be any that keep to these rules, and one draw needn't show every extreme that they name: `expert_ids`: each token names 2 different experts; among the 32 rows of one device at most 16 name expert 0 and at least one does; on some device exactly 16 do.
All inputs are finite; a program needn't handle non-finite values.
Results may differ from a plain program's by a relative error of at most 0.006.
Values may be sent and summed in bfloat16 or wider, within the bound.
No kernel may reach another device: no remote copies, remote signals or barrier semaphores. Data moves between devices by JAX's collectives and lax.ppermute only.
A program may use at most 192 MiB of HBM per device.

v0:
```python
import jax
import jax.numpy as jnp
from jax import lax
from jax.sharding import PartitionSpec as P

BLOCK = 128


def entering(value, axis, join, neutral):
    count, mine = (lax.axis_size(axis), lax.axis_index(axis))
    pieces = jax.tree.map(lambda part: lax.all_gather(part, axis), value)
    running = jax.tree.map(
        lambda part, zero: jnp.full_like(part, 0) + jnp.asarray(zero, part.dtype), value, neutral
    )

    def hop(position, running):
        longer = join(running, jax.tree.map(lambda part: part[position], pieces))
        return jax.tree.map(lambda new, old: jnp.where(position < mine, new, old), longer, running)

    return lax.fori_loop(0, count - 1, hop, running)


def pair_combine(early, later):
    return (early[0] * later[0], later[0] * early[1] + later[1])


def end_state(step_size, x_float, decay_rate, b_rows):

    def end_advance(state, inputs):
        step_now, x_now, b_now = inputs
        state = (
            jnp.exp(-step_now[None, :] * decay_rate) * state
            + (step_now * x_now)[None, :] * b_now[:, None]
        )
        return (state, None)

    start_state = jnp.zeros(decay_rate.shape, jnp.float32)
    final_state, _ = lax.scan(end_advance, start_state, (step_size, x_float, b_rows), unroll=8)
    return final_state


def scan_outputs(state_in, step_size, x_float, decay_rate, b_rows, c_rows, skip_gain):

    def scan_advance(state, inputs):
        step_now, x_now, b_now, c_now = inputs
        state = (
            jnp.exp(-step_now[None, :] * decay_rate) * state
            + (step_now * x_now)[None, :] * b_now[:, None]
        )
        y_now = jnp.sum(c_now[:, None] * state, axis=0) + skip_gain * x_now
        return (state, y_now)

    _, outputs = lax.scan(scan_advance, state_in, (step_size, x_float, b_rows, c_rows), unroll=8)
    return outputs


def on_device(
    x_in,
    z_in,
    step_raw,
    step_bias,
    decay_rate,
    b_coef,
    c_coef,
    skip_gain,
    out_proj,
    residual,
    norm_gain,
    router_weight,
    expert_ids,
    gate_weight,
    up_weight,
    down_weight,
):
    step_size = jax.nn.softplus(step_raw.astype(jnp.float32) + step_bias[None, :])
    x_float = x_in.astype(jnp.float32)
    b_rows = b_coef.astype(jnp.float32).T
    c_rows = c_coef.astype(jnp.float32).T
    state_end = end_state(step_size, x_float, decay_rate, b_rows)
    decay_end = jnp.exp(-decay_rate * jnp.sum(step_size, axis=0)[None, :])
    identity = (jnp.ones_like(decay_end), jnp.zeros_like(state_end))
    carried = entering((decay_end, state_end), "seq", pair_combine, identity)
    state_in = carried[1]
    scanned = scan_outputs(state_in, step_size, x_float, decay_rate, b_rows, c_rows, skip_gain)
    gated = (scanned * jax.nn.silu(z_in.astype(jnp.float32))).astype(jnp.bfloat16)
    column_part = jnp.dot(
        lax.all_gather(gated, "seq", axis=0, tiled=True),
        out_proj,
        preferred_element_type=jnp.float32,
    )
    seq_count = lax.axis_size("seq")
    expert_count = lax.axis_size("expert")
    rows = residual.shape[0]
    grouped = column_part.reshape(seq_count, expert_count, rows, column_part.shape[1])
    summed = lax.psum_scatter(grouped, "expert", scatter_dimension=1, tiled=True)
    arranged = jnp.transpose(summed[:, 0], (1, 0, 2))
    swapped = lax.all_to_all(arranged, "seq", split_axis=1, concat_axis=1, tiled=True)
    mamba_out = swapped.reshape(rows, -1)
    hidden = (residual.astype(jnp.float32) + mamba_out).astype(jnp.bfloat16)
    hidden_f = hidden.astype(jnp.float32)
    width_d = hidden.shape[1]
    scale_cols = width_d // BLOCK
    normed = (
        hidden_f
        * lax.rsqrt(jnp.mean(hidden_f * hidden_f, axis=-1, keepdims=True) + 1e-05)
        * norm_gain[None, :]
    )
    blocked = normed.reshape(rows, scale_cols, BLOCK)
    scales = (jnp.max(jnp.abs(blocked), axis=-1) / 448.0 + 1e-06).astype(jnp.bfloat16)
    quant = (blocked / scales.astype(jnp.float32)[..., None]).astype(jnp.bfloat16)
    restored = (
        (quant.astype(jnp.float32) * scales.astype(jnp.float32)[..., None])
        .astype(jnp.bfloat16)
        .reshape(rows, width_d)
    )
    experts = router_weight.shape[1]
    probs = jax.nn.sigmoid(jnp.dot(restored, router_weight, preferred_element_type=jnp.float32))
    picks = expert_ids[:, :, None] == jnp.arange(experts, dtype=jnp.int32)[None, None, :]
    chosen = jnp.sum(jnp.where(picks, probs[:, None, :], jnp.float32(0.0)), axis=-1)
    weights = chosen / jnp.sum(chosen, axis=-1, keepdims=True)
    coef = jnp.sum(jnp.where(expert_ids == 0, weights, jnp.float32(0.0)), axis=1)
    wanted = jnp.any(expert_ids == 0, axis=1)
    wanted_int = wanted.astype(jnp.int32)
    slot_pos = jnp.cumsum(wanted_int) - wanted_int
    capacity = rows // 2
    table = (
        (slot_pos[None, :] == jnp.arange(capacity, dtype=jnp.int32)[:, None]) & wanted[None, :]
    ).astype(jnp.bfloat16)
    send_quant = jnp.dot(
        table, quant.reshape(rows, width_d), preferred_element_type=jnp.float32
    ).astype(jnp.bfloat16)
    send_scale = jnp.dot(table, scales, preferred_element_type=jnp.float32).astype(jnp.bfloat16)
    all_quant, all_scale = (
        lax.all_gather(send_quant, ("seq", "expert"), axis=0, tiled=True),
        lax.all_gather(send_scale, ("seq", "expert"), axis=0, tiled=True),
    )
    slots = all_quant.shape[0]
    inputs = (
        (
            all_quant.reshape(slots, scale_cols, BLOCK).astype(jnp.float32)
            * all_scale.astype(jnp.float32)[..., None]
        )
        .astype(jnp.bfloat16)
        .reshape(slots, width_d)
    )
    gate_value = jnp.dot(inputs, gate_weight, preferred_element_type=jnp.float32)
    up_value = jnp.dot(inputs, up_weight, preferred_element_type=jnp.float32)
    active = (jax.nn.silu(gate_value) * up_value).astype(jnp.bfloat16)
    own_sum = lax.psum_scatter(
        jnp.dot(active, down_weight, preferred_element_type=jnp.float32).astype(jnp.bfloat16),
        ("seq", "expert"),
        scatter_dimension=0,
        tiled=True,
    )
    returned = jnp.dot(table.T, own_sum, preferred_element_type=jnp.float32)
    return (hidden_f + coef[:, None] * returned).astype(jnp.bfloat16)


def solution(mesh):
    return jax.shard_map(
        on_device,
        mesh=mesh,
        in_specs=(
            P(("dp", "seq"), "expert"),
            P(("dp", "seq"), "expert"),
            P(("dp", "seq"), "expert"),
            P("expert"),
            P(None, "expert"),
            P(None, ("dp", "seq")),
            P(None, ("dp", "seq")),
            P("expert"),
            P("expert", "seq"),
            P(("dp", "seq", "expert"), None),
            P(),
            P(),
            P(("dp", "seq", "expert"), None),
            P(None, ("seq", "expert")),
            P(None, ("seq", "expert")),
            P(("seq", "expert"), None),
        ),
        out_specs=P(("dp", "seq", "expert"), None),
        check_vma=False,
    )
```

profile of v0, /device:TPU:0, one launch (start us, length us, event | category | flops | bytes accessed | tf_op | source)
XLA Modules:
  0.0 533.8 jit_solution(4677953557653513335)
XLA Ops:
  8.5 1.7 fusion.67
  10.2 21.8 %while.38 = (s32[]{:T(128)}, f32[16,2048]{1,0:T(8,128)S(1)}, f32[16,8,2048]{2,1,0:T(8,128)S(1)}, f32[16,2048]{1,0:T(8,128)}, f32[16,8,2048]{2,1,0:T(8,128)S(1)},...) while((s32[]{:T(128)}, f32[16,2048]{1,0:T(8,128)S(1)}, ...), condition=%wide.region_2.3_spmd.clone, body=%wide.region_1.2_spmd.clone.sunk | while | flops 1114122 | bytes 789271 | solution.py:38
  32.8 1.6 multiply_exponential_fusion
  34.6 24.2 %all-gather.13.cloned.1.call-done = f32[128,2048]{1,0:T(8,128)} async-done(((f32[16,2048]{1,0:T(8,128)}), f32[128,2048]{1,0:T(8,128)}) %all-gather.13.cloned.1.call-update) | async-done | bytes 1048592 | tf_op jit(solution)/shard_map/all_gather | solution.py:11
  58.8 25.1 %all-gather.11.cloned.1.call-done = f32[128,2048]{1,0:T(8,128)} async-done(((f32[16,2048]{1,0:T(8,128)}), f32[128,2048]{1,0:T(8,128)}) %all-gather.11.cloned.1.call-update) | async-done | bytes 1048592 | tf_op jit(solution)/shard_map/all_gather | solution.py:11
  84.0 7.6 %while.39 = (s32[]{:T(128)}, f32[16,2048]{1,0:T(8,128)S(1)}, s32[]{:T(128)}, f32[8,16,2048]{2,1,0:T(8,128)}, f32[8,16,2048]{2,1,0:T(8,128)}, /*index=5*/s32[]{:T(128)}, s32[]{:T(128)}) while((s32[]{:T(128)}, f32[16,2048]{1,0:T(8,128)S(1)}, s32[]{:T(128)}, f32[8,16,2048]{2,1,0:T(8,128)}, f32[8,16,2048]{2,1,0:T(8,128)}, ...), condition=%wide.region_4.5_spmd.clone, body=%wide.region_3.4_spmd.clone.sunk | while | flops 131076 | bytes 524397 | solution.py:20
  91.6 71.2 %while.37 = (s32[]{:T(128)}, f32[16,2048]{1,0:T(8,128)S(1)}, f32[16,8,2048]{2,1,0:T(8,128)}, f32[16,8,2048]{2,1,0:T(8,128)S(1)}, f32[16,2048]{1,0:T(8,128)}, /*i...) while((s32[]{:T(128)}, f32[16,2048]{1,0:T(8,128)S(1)}, ...), condition=%wide.region_14.15_spmd, body=%wide.region_5.14_spmd.sunk | while | flops 2408457 | bytes 2078409 | solution.py:53
  97.3 1.2 multiply_reduce_fusion.11
  106.2 1.2 multiply_reduce_fusion.11
  110.7 1.2 multiply_reduce_fusion.11
  162.8 2.3 fusion.66
  165.2 32.3 %all-gather.7.cloned.1.call-done = bf16[1024,2048]{1,0:T(8,128)(2,1)} async-done(((bf16[128,2048]{1,0:T(8,128)(2,1)}), bf16[1024,2048]{1,0:T(8,128)(2,1)}) %all-gather.7.cloned.1.call-update) | async-done | bytes 4194320 | tf_op jit(solution)/shard_map/all_gather | solution.py:87
  197.5 9.9 %fusion.91 = f32[1024,1024]{1,0:T(8,128)} fusion(bf16[1024,2048]{1,0:T(8,128)(2,1)} %all-gather.7.cloned.1.call-done, bf16[2048,1024]{1,0:T(8,128)(2,1)} %param.30), kind=kOutput, calls=%fused_computation.200 | convolution fusion | flops 4294967296 | bytes 12582912 | tf_op jit(solution)/shard_map/dot_general | solution.py:86
  208.0 92.1 %all-reduce.3.cloned.1.call-done = f32[8,4,32,1024]{3,2,1,0:T(8,128)} async-done(((f32[8,4,32,1024]{3,2,1,0:T(8,128)}), f32[8,4,32,1024]{3,2,1,0:T(8,128)}) %all-reduce.3.cloned.1.call-update) | async-done | bytes 4194320
  300.2 3.0 dynamic-slice_bitcast_fusion
  303.1 4.4 all-to-all-start
  307.9 15.6 %all-to-all-done = f32[32,8,1024]{2,0,1:T(8,128)S(1)} async-done(((f32[32,8,1024]{2,0,1:T(8,128)}), f32[32,8,1024]{2,0,1:T(8,128)S(1)}, u32[]{:S(2)}, u32[]{:S(2)}) %all-to-all-start) | async-done | bytes 1048608 | tf_op jit(solution)/shard_map/all_to_all | solution.py:97
  326.7 38.1 %all_gather.27 = bf16[512,64]{1,0:T(8,128)(2,1)S(1)} all-gather(bf16[16,64]{1,0:T(8,128)(2,1)S(1)} %convolution_convert_fusion.2), channel_id=1, replica_groups=mesh['dp'=4,'seq'=8,'expert'=4] {'seq','expert'}, dimensions={0}, use_global_device_ids=true | all-gather | bytes 67584 | tf_op jit(solution)/shard_map/all_gather | solution.py:135
  364.9 12.8 %all-gather.9.cloned.1.call-done = bf16[512,8192]{1,0:T(8,128)(2,1)} async-done(((bf16[16,8192]{1,0:T(8,128)(2,1)}), bf16[512,8192]{1,0:T(8,128)(2,1)}) %all-gather.9.cloned.1.call-update) | async-done | bytes 8388624 | tf_op jit(solution)/shard_map/all_gather | solution.py:134
  377.7 8.0 %mul.821 = f32[512,64,128]{2,1,0:T(8,128)} broadcast(bf16[512,64]{1,0:T(8,128)(2,1)S(1)} %all_gather.27), dimensions={0,1} | broadcast | bytes 16842752 | tf_op jit(solution)/shard_map/mul | solution.py:140
  385.6 18.4 %fusion.89 = f32[512,384]{1,0:T(8,128)S(1)} fusion(bf16[8192,384]{1,0:T(8,128)(2,1)} %param.35, f32[64,8,64,128]{3,2,1,0:T(8,128)} %bitcast.286, bf16[512,8192]{1,0:T(8,128)(2,1)S(1)} %copy-done.1), kind=kOutput, calls=%fused_computation.199 | convolution fusion | flops 3233808384 | bytes 32243712 | tf_op jit(solution)/shard_map/dot_general | solution.py:146
  404.0 28.3 %convolution_convert_fusion = bf16[512,8192]{1,0:T(8,128)(2,1)} fusion(bf16[384,8192]{1,0:T(8,128)(2,1)} %param.37, bf16[8192,384]{1,0:T(8,128)(2,1)} %param.36, f32[512,384]{1,0:T(8,128)S(1)} %fusion.89, f32[64,8,64,128]{3,2,1,0:T(8,128)} %bitcast.287, bf16[512,8192]{1,0:T(8,128)(2,1)} %all-gather.9.cloned.1.call-done), kind=kOutput, calls=%fused_computation.137 | convolution fusion | flops 6460407808 | bytes 46923776 | tf_op jit(solution)/shard_map/dot_general | solution.py:150
  433.2 91.7 %reduce-scatter.5.cloned.1.call-done = bf16[16,8192]{1,0:T(8,128)(2,1)} async-done(((bf16[512,8192]{1,0:T(8,128)(2,1)}), bf16[16,8192]{1,0:T(8,128)(2,1)}) %reduce-scatter.5.cloned.1.call-update) | async-done | bytes 262160 | tf_op jit(solution)/shard_map/reduce_scatter | solution.py:149
  524.9 2.1 fusion.50
  (289 shorter events, 103.5 us)
Async XLA Ops:
  6.5 425.8 %copy-start = (bf16[8192,16]{0,1:T(8,128)(2,1)S(1)}, bf16[8192,16]{0,1:T(8,128)(2,1)}, u32[]{:S(2)}) copy-start(bf16[8192,16]{0,1:T(8,128)(2,1)} %param.33) | copy-start | bytes 786436
  6.5 27.9 %copy-start.7 = (bf16[16,128]{1,0:T(8,128)(2,1)S(1)}, bf16[16,128]{1,0:T(8,128)(2,1)}, u32[]{:S(2)}) copy-start(bf16[16,128]{1,0:T(8,128)(2,1)} %param.28) | copy-start | bytes 12292
  6.5 85.0 %copy-start.5 = (f32[2048]{0:T(1024)S(1)}, f32[2048]{0:T(1024)}, u32[]{:S(2)}) copy-start(f32[2048]{0:T(1024)} %param.29) | copy-start | bytes 24580
  6.5 52.3 %all-gather.13.cloned.1.call-start = ((), (), s32[]{:S(2)}) async-start(), calls=%async_computation.6 | async-start | bytes 1179648 | tf_op jit(solution)/shard_map/all_gather | solution.py:11
  32.1 0.6 copy-start.2
  32.1 130.7 %copy-start.4 = (bf16[128,2048]{1,0:T(8,128)(2,1)S(1)}, bf16[128,2048]{1,0:T(8,128)(2,1)}, u32[]{:S(2)}) copy-start(bf16[128,2048]{1,0:T(8,128)(2,1)} %param.23) | copy-start | bytes 1572868
  32.7 51.2 %all-gather.11.cloned.1.call-start = ((), (), s32[]{:S(2)}) async-start(), calls=%async_computation.5 | async-start | bytes 1179648 | tf_op jit(solution)/shard_map/all_gather | solution.py:11
  34.4 163.1 %all-gather.7.cloned.1.call-start = ((), (), s32[]{:S(2)}) async-start(), calls=%async_computation.2 | async-start | bytes 4718592 | tf_op jit(solution)/shard_map/all_gather | solution.py:87
  165.1 42.3 %copy-start.9 = (u32[128]{0:T(128)S(1)}, u32[128]{0:T(128)}, u32[]{:S(2)}) copy-start(u32[128]{0:T(128)} %constant.87) | copy-start | bytes 1540
  165.2 135.0 %all-reduce.3.cloned.1.call-start = ((), (), s32[]{:S(2)}) async-start(), calls=%async_computation.7 | async-start | bytes 8388608
  207.4 100.2 %copy-start.8 = (s32[32,2]{0,1:T(2,128)S(1)}, s32[32,2]{0,1:T(2,128)}, u32[]{:S(2)}) copy-start(s32[32,2]{0,1:T(2,128)} %param.34) | copy-start | bytes 772
  207.4 116.2 %copy-start.3 = (bf16[32,8192]{1,0:T(8,128)(2,1)S(1)}, bf16[32,8192]{1,0:T(8,128)(2,1)}, u32[]{:S(2)}) copy-start(bf16[32,8192]{1,0:T(8,128)(2,1)} %param.31) | copy-start | bytes 1572868
  207.4 116.5 %copy-start.6 = (f32[8192]{0:T(1024)S(1)}, f32[8192]{0:T(1024)}, u32[]{:S(2)}) copy-start(f32[8192]{0:T(1024)} %param.32) | copy-start | bytes 98308
  303.1 20.4 %all-to-all-start = ((f32[32,8,1024]{2,0,1:T(8,128)}), f32[32,8,1024]{2,0,1:T(8,128)S(1)}, u32[]{:S(2)}, u32[]{:S(2)}) async-start(f32[32,8,1024]{2,0,1:T(8,128)} %dynamic-slice_bitcast_fusion), calls=%async_computation | async-start | bytes 2097152 | tf_op jit(solution)/shard_map/all_to_all | solution.py:97
  307.5 70.1 %all-gather.9.cloned.1.call-start = ((), (), s32[]{:S(2)}) async-start(), calls=%async_computation.3 | async-start | bytes 8650752 | tf_op jit(solution)/shard_map/all_gather | solution.py:134
  326.6 198.3 %reduce-scatter.5.cloned.1.call-start = ((), (), s32[]{:S(2)}) async-start(), calls=%async_computation.4 | async-start | bytes 8650752 | tf_op jit(solution)/shard_map/reduce_scatter | solution.py:149
  377.7 8.0 %copy-start.1 = (bf16[512,8192]{1,0:T(8,128)(2,1)S(1)}, bf16[512,8192]{1,0:T(8,128)(2,1)}, u32[]{:S(2)}) copy-start(bf16[512,8192]{1,0:T(8,128)(2,1)} %all-gather.9.cloned.1.call-done) | copy-start | bytes 25165828
Sparse Core Ops, SparseCore 0:
  32.9 25.9 all-gather.12
  60.5 23.3 all-gather.10
  165.3 32.1 all-gather.6
  207.6 92.5 all-reduce.2
  326.7 50.9 all-gather.8
  432.5 92.3 reduce-scatter.4
where the time goes:
time: 535 us; the launch traced here: 534 us
  waiting for transfers between devices  294 us (55%)
  other arithmetic  96.1 us (18%)
  matrix products  60.5 us (11%)
  blocking collectives  38.1 us (7%)
  local copies, waits for them, and re-layouts  25.5 us (5%)
  between operations  13.7 us (3%)
    unnamed x7, waiting for transfers between devices  92.2 us
    reduce_scatter x1, waiting for transfers between devices, on_device(): lax.psum_scatter(jnp.dot(active, down_weight, preferred_element_type=jnp....  91.7 us
    reduce_sum x48, other arithmetic, scan_advance(): y_now = jnp.sum(c_now[:, None] * state, axis=0) + skip_gain * x_now  54.8 us
    all_gather x2, waiting for transfers between devices, entering(): pieces = jax.tree.map(lambda part: lax.all_gather(part, axis), value)  49.4 us
    all_gather x1, blocking collectives, on_device(): lax.all_gather(send_scale, ('seq', 'expert'), axis=0, tiled=True)  38.1 us
    all_gather x1, waiting for transfers between devices, on_device(): lax.all_gather(gated, 'seq', axis=0, tiled=True)  32.3 us
    dot_general x1, matrix products, on_device(): jnp.dot(active, down_weight, preferred_element_type=jnp.float32)  28.3 us
    add x16, other arithmetic, end_advance(): jnp.exp(-step_now[None, :] * decay_rate) * state  18.7 us
  transfers between devices with their start and end apart: 7, of which 7 were waited for; matrix products, arithmetic and copies ran while one was open for 1% of the time, Pallas kernels for 0%

commit v1 on v0

--- a/solution.py
+++ b/solution.py
@@ -8,16 +8,12 @@
 
 def entering(value, axis, join, neutral):
     count, mine = (lax.axis_size(axis), lax.axis_index(axis))
-    pieces = jax.tree.map(lambda part: lax.all_gather(part, axis), value)
-    running = jax.tree.map(
-        lambda part, zero: jnp.full_like(part, 0) + jnp.asarray(zero, part.dtype), value, neutral
-    )
-
-    def hop(position, running):
-        longer = join(running, jax.tree.map(lambda part: part[position], pieces))
-        return jax.tree.map(lambda new, old: jnp.where(position < mine, new, old), longer, running)
-
-    return lax.fori_loop(0, count - 1, hop, running)
+    stacked = lax.all_gather(jnp.stack(value), axis)
+    running = tuple(jnp.full_like(part, zero) for part, zero in zip(value, neutral))
+    for position in range(count - 1):
+        longer = join(running, (stacked[position, 0], stacked[position, 1]))
+        running = tuple(jnp.where(position < mine, new, old) for new, old in zip(longer, running))
+    return running
 
 
 def pair_combine(early, later):
@@ -78,24 +74,22 @@
     c_rows = c_coef.astype(jnp.float32).T
     state_end = end_state(step_size, x_float, decay_rate, b_rows)
     decay_end = jnp.exp(-decay_rate * jnp.sum(step_size, axis=0)[None, :])
-    identity = (jnp.ones_like(decay_end), jnp.zeros_like(state_end))
+    identity = (1.0, 0.0)
     carried = entering((decay_end, state_end), "seq", pair_combine, identity)
     state_in = carried[1]
     scanned = scan_outputs(state_in, step_size, x_float, decay_rate, b_rows, c_rows, skip_gain)
     gated = (scanned * jax.nn.silu(z_in.astype(jnp.float32))).astype(jnp.bfloat16)
-    column_part = jnp.dot(
-        lax.all_gather(gated, "seq", axis=0, tiled=True),
-        out_proj,
-        preferred_element_type=jnp.float32,
-    )
     seq_count = lax.axis_size("seq")
     expert_count = lax.axis_size("expert")
     rows = residual.shape[0]
-    grouped = column_part.reshape(seq_count, expert_count, rows, column_part.shape[1])
-    summed = lax.psum_scatter(grouped, "expert", scatter_dimension=1, tiled=True)
-    arranged = jnp.transpose(summed[:, 0], (1, 0, 2))
-    swapped = lax.all_to_all(arranged, "seq", split_axis=1, concat_axis=1, tiled=True)
-    mamba_out = swapped.reshape(rows, -1)
+    gathered = lax.all_gather(gated, "seq", axis=0, tiled=True)
+    gathered = gathered.reshape(seq_count, expert_count, rows, gated.shape[1])
+    gathered = jnp.transpose(gathered, (1, 0, 2, 3)).reshape(-1, gated.shape[1])
+    column_part = jnp.dot(gathered, out_proj, preferred_element_type=jnp.float32)
+    summed = lax.psum_scatter(column_part, "expert", scatter_dimension=0, tiled=True)
+    summed = summed.reshape(seq_count, rows, column_part.shape[1])
+    swapped = lax.all_to_all(summed, "seq", split_axis=0, concat_axis=0, tiled=True)
+    mamba_out = jnp.transpose(swapped, (1, 0, 2)).reshape(rows, -1)
     hidden = (residual.astype(jnp.float32) + mamba_out).astype(jnp.bfloat16)
     hidden_f = hidden.astype(jnp.float32)
     width_d = hidden.shape[1]
@@ -126,23 +120,8 @@
     table = (
         (slot_pos[None, :] == jnp.arange(capacity, dtype=jnp.int32)[:, None]) & wanted[None, :]
     ).astype(jnp.bfloat16)
-    send_quant = jnp.dot(
-        table, quant.reshape(rows, width_d), preferred_element_type=jnp.float32
-    ).astype(jnp.bfloat16)
-    send_scale = jnp.dot(table, scales, preferred_element_type=jnp.float32).astype(jnp.bfloat16)
-    all_quant, all_scale = (
-        lax.all_gather(send_quant, ("seq", "expert"), axis=0, tiled=True),
-        lax.all_gather(send_scale, ("seq", "expert"), axis=0, tiled=True),
-    )
-    slots = all_quant.shape[0]
-    inputs = (
-        (
-            all_quant.reshape(slots, scale_cols, BLOCK).astype(jnp.float32)
-            * all_scale.astype(jnp.float32)[..., None]
-        )
-        .astype(jnp.bfloat16)
-        .reshape(slots, width_d)
-    )
+    send_rows = jnp.dot(table, restored, preferred_element_type=jnp.float32).astype(jnp.bfloat16)
+    inputs = lax.all_gather(send_rows, ("seq", "expert"), axis=0, tiled=True)
     gate_value = jnp.dot(inputs, gate_weight, preferred_element_type=jnp.float32)
     up_value = jnp.dot(inputs, up_weight, preferred_element_type=jnp.float32)
     active = (jax.nn.silu(gate_value) * up_value).astype(jnp.bfloat16)

time: 535 us -> 429 us (0.80)
  blocking collectives: 38.1 us -> 0 us
  waiting for transfers between devices: 294 us -> 266 us
  matrix products: 60.5 us -> 35.2 us
  local copies, waits for them, and re-layouts: 25.5 us -> 16.7 us
  other arithmetic: 96.1 us -> 90.4 us
    unnamed x7 -> x5, waiting for transfers between devices: 92.2 us -> 0.08 us
    reduce_scatter x0 -> x1, waiting for transfers between devices: none -> 46.8 us  [on_device(): lax.psum_scatter(column_part, 'expert', scatter_dimension=0, tiled=True)]
    all_gather x1 -> x0, blocking collectives: 38.1 us -> none  [on_device(): lax.all_gather(send_scale, ('seq', 'expert'), axis=0, tiled=True)]
    all_gather x4 -> x3, waiting for transfers between devices: 94.4 us -> 111 us  [the longest x1 50.5 us: on_device(): inputs = lax.all_gather(send_rows, ('seq', 'expert'), axis=0, tiled=True)]
    dot_general x1, matrix products: 28.3 us -> 17.1 us  [on_device(): jnp.dot(active, down_weight, preferred_element_type=jnp.float32)]
    dot_general x1, matrix products: 18.4 us -> 8.78 us  [on_device(): jnp.dot(inputs, gate_weight, preferred_element_type=jnp.float32)]
    mul x1 -> x0, local copies, waits for them, and re-layouts: 7.97 us -> none  [on_device(): all_quant.reshape(slots, scale_cols, BLOCK).astype(jnp.float32)]
    select_n x7 -> x1, other arithmetic: 7.49 us -> 1.62 us  [entering(): jnp.where(position < mine, new, old)]
  transfers between devices with their start and end apart: 7 -> 6, of which waited for: 7 -> 6; matrix products, arithmetic and copies ran while one was open for 1% -> 0% of each run, Pallas kernels for 0% -> 0%
where the time goes in v1:
time: 429 us; the launch traced here: 427 us
  waiting for transfers between devices  266 us (62%)
  other arithmetic  90.4 us (21%)
  matrix products  35.2 us (8%)
  local copies, waits for them, and re-layouts  16.7 us (4%)
  between operations  13.3 us (3%)
  starting transfers between devices  4.79 us (1%)
    reduce_scatter x1, waiting for transfers between devices, on_device(): lax.psum_scatter(jnp.dot(active, down_weight, preferred_element_type=jnp....  92.3 us
    reduce_sum x48, other arithmetic, scan_advance(): y_now = jnp.sum(c_now[:, None] * state, axis=0) + skip_gain * x_now  54.9 us
    all_gather x1, waiting for transfers between devices, on_device(): inputs = lax.all_gather(send_rows, ('seq', 'expert'), axis=0, tiled=True)  50.5 us
    reduce_scatter x1, waiting for transfers between devices, on_device(): lax.psum_scatter(column_part, 'expert', scatter_dimension=0, tiled=True)  46.8 us
    all_gather x1, waiting for transfers between devices, on_device(): gathered = lax.all_gather(gated, 'seq', axis=0, tiled=True)  32.6 us
    all_gather x1, waiting for transfers between devices, entering(): stacked = lax.all_gather(jnp.stack(value), axis)  28 us
    add x16, other arithmetic, end_advance(): jnp.exp(-step_now[None, :] * decay_rate) * state  18.6 us
    dot_general x1, matrix products, on_device(): jnp.dot(active, down_weight, preferred_element_type=jnp.float32)  17.1 us
  transfers between devices with their start and end apart: 6, of which 6 were waited for; matrix products, arithmetic and copies ran while one was open for 0% of the time, Pallas kernels for 0%

profile of v1, /device:TPU:0, one launch (start us, length us, event | category | flops | bytes accessed | tf_op | source)
XLA Modules:
  0.0 427.4 jit_solution(3741020597015307561)
XLA Ops:
  8.5 1.7 fusion.66
  10.2 21.7 %while.24 = (s32[]{:T(128)}, f32[16,2048]{1,0:T(8,128)S(1)}, f32[16,8,2048]{2,1,0:T(8,128)S(1)}, f32[16,2048]{1,0:T(8,128)}, f32[16,8,2048]{2,1,0:T(8,128)S(1)},...) while((s32[]{:T(128)}, f32[16,2048]{1,0:T(8,128)S(1)}, ...), condition=%wide.region_2.3_spmd.clone, body=%wide.region_1.2_spmd.clone.sunk | while | flops 1114122 | bytes 789271 | solution.py:34
  33.9 28.0 %all-gather.9.cloned.1.call-done = f32[16,16,2048]{2,1,0:T(8,128)} async-done(((f32[2,16,2048]{2,1,0:T(8,128)}), f32[16,16,2048]{2,1,0:T(8,128)}) %all-gather.9.cloned.1.call-update) | async-done | bytes 2097168 | tf_op jit(solution)/shard_map/all_gather | solution.py:11
  61.8 1.6 fusion.69
  63.5 71.3 %while.23 = (s32[]{:T(128)}, f32[16,2048]{1,0:T(8,128)S(1)}, f32[16,8,2048]{2,1,0:T(8,128)}, f32[16,8,2048]{2,1,0:T(8,128)S(1)}, f32[16,2048]{1,0:T(8,128)}, /*i...) while((s32[]{:T(128)}, f32[16,2048]{1,0:T(8,128)S(1)}, ...), condition=%wide.region_12.13_spmd, body=%wide.region_3.12_spmd.sunk | while | flops 2408457 | bytes 2078409 | solution.py:49
  69.2 1.2 multiply_reduce_fusion.11
  78.1 1.2 multiply_reduce_fusion.11
  82.6 1.2 multiply_reduce_fusion.11
  87.0 1.2 multiply_reduce_fusion.11
  91.5 1.2 multiply_reduce_fusion.11
  95.9 1.2 multiply_reduce_fusion.11
  100.4 1.2 multiply_reduce_fusion.11
  134.8 2.3 fusion.64
  137.2 32.6 %all-gather.5.cloned.1.call-done = bf16[1024,2048]{1,0:T(8,128)(2,1)} async-done(((bf16[128,2048]{1,0:T(8,128)(2,1)}), bf16[1024,2048]{1,0:T(8,128)(2,1)}) %all-gather.5.cloned.1.call-update) | async-done | bytes 4194320 | tf_op jit(solution)/shard_map/all_gather | solution.py:85
  169.8 2.7 copy.45
  173.2 6.0 %fusion.99 = f32[1024,1024]{1,0:T(8,128)} fusion(bf16[1024,2048]{1,0:T(8,128)(2,1)S(1)} %bitcast.416, bf16[2048,1024]{1,0:T(8,128)(2,1)S(1)} %copy-done.7), kind=kOutput, calls=%fused_computation.223 | convolution fusion | flops 4294967296 | bytes 12582912 | tf_op jit(solution)/shard_map/dot_general | solution.py:88
  179.3 46.8 %reduce-scatter.3.cloned.1.call-done = f32[256,1024]{1,0:T(8,128)} async-done(((f32[1024,1024]{1,0:T(8,128)}), f32[256,1024]{1,0:T(8,128)}) %reduce-scatter.3.cloned.1.call-update) | async-done | bytes 1048592 | tf_op jit(solution)/shard_map/reduce_scatter | solution.py:89
  226.1 4.4 %all-to-all-start = ((f32[8,32,1024]{2,1,0:T(8,128)}), f32[8,32,1024]{2,1,0:T(8,128)S(1)}, u32[]{:S(2)}, u32[]{:S(2)}) async-start(f32[8,32,1024]{2,1,0:T(8,128)} %bitcast.444), calls=%async_computation.1 | async-start | bytes 2097152 | tf_op jit(solution)/shard_map/all_to_all | solution.py:91
  230.9 15.6 %all-to-all-done = f32[8,32,1024]{2,1,0:T(8,128)S(1)} async-done(((f32[8,32,1024]{2,1,0:T(8,128)}), f32[8,32,1024]{2,1,0:T(8,128)S(1)}, u32[]{:S(2)}, u32[]{:S(2)}) %all-to-all-start) | async-done | bytes 1048608 | tf_op jit(solution)/shard_map/all_to_all | solution.py:91
  249.8 50.5 %all-gather.7.cloned.1.call-done = bf16[512,8192]{1,0:T(8,128)(2,1)} async-done(((bf16[16,8192]{1,0:T(8,128)(2,1)}), bf16[512,8192]{1,0:T(8,128)(2,1)}) %all-gather.7.cloned.1.call-update) | async-done | bytes 8388624 | tf_op jit(solution)/shard_map/all_gather | solution.py:124
  300.3 8.8 %fusion.100 = f32[512,384]{1,0:T(8,128)S(1)} fusion(bf16[512,8192]{1,0:T(8,128)(2,1)} %all-gather.7.cloned.1.call-done, bf16[8192,384]{1,0:T(8,128)(2,1)} %param.33), kind=kOutput, calls=%fused_computation.224 | convolution fusion | flops 3221225472 | bytes 15466496 | tf_op jit(solution)/shard_map/dot_general | solution.py:125
  309.1 17.1 %convolution_convert_fusion = bf16[512,8192]{1,0:T(8,128)(2,1)} fusion(bf16[384,8192]{1,0:T(8,128)(2,1)} %param.35, bf16[512,8192]{1,0:T(8,128)(2,1)} %all-gather.7.cloned.1.call-done, bf16[8192,384]{1,0:T(8,128)(2,1)} %param.34, f32[512,384]{1,0:T(8,128)S(1)} %fusion.100), kind=kOutput, calls=%fused_computation.132 | convolution fusion | flops 6447824896 | bytes 30146560 | tf_op jit(solution)/shard_map/dot_general | solution.py:129
  326.5 92.3 %reduce-scatter.5.cloned.1.call-done = bf16[16,8192]{1,0:T(8,128)(2,1)} async-done(((bf16[512,8192]{1,0:T(8,128)(2,1)}), bf16[16,8192]{1,0:T(8,128)(2,1)}) %reduce-scatter.5.cloned.1.call-update) | async-done | bytes 262160 | tf_op jit(solution)/shard_map/reduce_scatter | solution.py:128
  418.8 2.1 fusion.48
  (271 shorter events, 91.9 us)
Async XLA Ops:
  6.5 319.7 %copy-start = (bf16[8192,16]{0,1:T(8,128)(2,1)S(1)}, bf16[8192,16]{0,1:T(8,128)(2,1)}, u32[]{:S(2)}) copy-start(bf16[8192,16]{0,1:T(8,128)(2,1)} %param.31) | copy-start | bytes 786436
  6.5 27.2 %copy-start.5 = (bf16[16,128]{1,0:T(8,128)(2,1)S(1)}, bf16[16,128]{1,0:T(8,128)(2,1)}, u32[]{:S(2)}) copy-start(bf16[16,128]{1,0:T(8,128)(2,1)} %param.26) | copy-start | bytes 12292
  6.5 56.9 %copy-start.3 = (f32[2048]{0:T(1024)S(1)}, f32[2048]{0:T(1024)}, u32[]{:S(2)}) copy-start(f32[2048]{0:T(1024)} %param.27) | copy-start | bytes 24580
  6.5 55.3 %all-gather.9.cloned.1.call-start = ((), (), s32[]{:S(2)}) async-start(), calls=%async_computation.7 | async-start | bytes 2359296 | tf_op jit(solution)/shard_map/all_gather | solution.py:11
  33.7 136.1 %all-gather.5.cloned.1.call-start = ((), (), s32[]{:S(2)}) async-start(), calls=%async_computation.3 | async-start | bytes 4718592 | tf_op jit(solution)/shard_map/all_gather | solution.py:85
  63.5 71.3 %copy-start.2 = (bf16[128,2048]{1,0:T(8,128)(2,1)S(1)}, bf16[128,2048]{1,0:T(8,128)(2,1)}, u32[]{:S(2)}) copy-start(bf16[128,2048]{1,0:T(8,128)(2,1)} %param.21) | copy-start | bytes 1572868
  137.1 89.0 %reduce-scatter.3.cloned.1.call-start = ((), (), s32[]{:S(2)}) async-start(), calls=%async_computation.4 | async-start | bytes 5242880 | tf_op jit(solution)/shard_map/reduce_scatter | solution.py:89
  169.8 3.4 copy-start.7
  179.2 51.3 %copy-start.6 = (s32[32,2]{0,1:T(2,128)S(1)}, s32[32,2]{0,1:T(2,128)}, u32[]{:S(2)}) copy-start(s32[32,2]{0,1:T(2,128)} %param.32) | copy-start | bytes 772
  179.2 67.3 %copy-start.1 = (bf16[32,8192]{1,0:T(8,128)(2,1)S(1)}, bf16[32,8192]{1,0:T(8,128)(2,1)}, u32[]{:S(2)}) copy-start(bf16[32,8192]{1,0:T(8,128)(2,1)} %param.29) | copy-start | bytes 1572868
  179.2 67.6 %copy-start.4 = (f32[8192]{0:T(1024)S(1)}, f32[8192]{0:T(1024)}, u32[]{:S(2)}) copy-start(f32[8192]{0:T(1024)} %param.30) | copy-start | bytes 98308
  226.1 20.4 %all-to-all-start = ((f32[8,32,1024]{2,1,0:T(8,128)}), f32[8,32,1024]{2,1,0:T(8,128)S(1)}, u32[]{:S(2)}, u32[]{:S(2)}) async-start(f32[8,32,1024]{2,1,0:T(8,128)} %bitcast.444), calls=%async_computation.1 | async-start | bytes 2097152 | tf_op jit(solution)/shard_map/all_to_all | solution.py:91
  230.5 69.8 %all-gather.7.cloned.1.call-start = ((), (), s32[]{:S(2)}) async-start(), calls=%async_computation.5 | async-start | bytes 8650752 | tf_op jit(solution)/shard_map/all_gather | solution.py:124
  249.5 169.3 %reduce-scatter.5.cloned.1.call-start = ((), (), s32[]{:S(2)}) async-start(), calls=%async_computation.6 | async-start | bytes 8650752 | tf_op jit(solution)/shard_map/reduce_scatter | solution.py:128
Sparse Core Ops, SparseCore 0:
  33.8 27.9 all-gather.8
  137.2 32.4 all-gather.4
  179.4 46.6 reduce-scatter.2
  249.7 50.5 all-gather.6
  326.3 92.4 reduce-scatter.4

commit v2 on v1

--- a/solution.py
+++ b/solution.py
@@ -1,9 +1,111 @@
 import jax
 import jax.numpy as jnp
 from jax import lax
+from jax.experimental import pallas as pl
+from jax.experimental.pallas import tpu as pltpu
 from jax.sharding import PartitionSpec as P
 
 BLOCK = 128
+LANES = 128
+ROWS_PER_LOAD = 16
+
+
+def _lane_tile(col, width):
+    return jnp.concatenate([col] * (width // LANES), axis=1) if width > LANES else col
+
+
+def _end_kernel(step_ref, x_ref, decay_ref, b_ref, state_ref):
+    steps, width = step_ref.shape
+    rate = decay_ref[...]
+
+    def body(k, state):
+        base = pl.multiple_of(k * ROWS_PER_LOAD, ROWS_PER_LOAD)
+        s_blk = step_ref[pl.ds(base, ROWS_PER_LOAD), :]
+        x_blk = x_ref[pl.ds(base, ROWS_PER_LOAD), :].astype(jnp.float32)
+        for i in range(ROWS_PER_LOAD):
+            s_now = s_blk[i : i + 1]
+            b_now = _lane_tile(b_ref[base + i], width)
+            state = jnp.exp(-s_now * rate) * state + (s_now * x_blk[i : i + 1]) * b_now
+        return state
+
+    zero = jnp.zeros(rate.shape, jnp.float32)
+    state_ref[...] = lax.fori_loop(0, steps // ROWS_PER_LOAD, body, zero)
+
+
+def _out_kernel(state_in_ref, step_ref, x_ref, z_ref, decay_ref, b_ref, c_ref, skip_ref, gated_ref, y_ref):
+    steps, width = step_ref.shape
+    rate = decay_ref[...]
+    skip = skip_ref[...]
+
+    def body(k, state):
+        base = pl.multiple_of(k * ROWS_PER_LOAD, ROWS_PER_LOAD)
+        s_blk = step_ref[pl.ds(base, ROWS_PER_LOAD), :]
+        x_blk = x_ref[pl.ds(base, ROWS_PER_LOAD), :].astype(jnp.float32)
+        for i in range(ROWS_PER_LOAD):
+            s_now = s_blk[i : i + 1]
+            x_now = x_blk[i : i + 1]
+            b_now = _lane_tile(b_ref[base + i], width)
+            c_now = _lane_tile(c_ref[base + i], width)
+            state = jnp.exp(-s_now * rate) * state + (s_now * x_now) * b_now
+            y_ref[pl.ds(base + i, 1), :] = jnp.sum(c_now * state, axis=0, keepdims=True) + skip * x_now
+        return state
+
+    lax.fori_loop(0, steps // ROWS_PER_LOAD, body, state_in_ref[...])
+    z = z_ref[...].astype(jnp.float32)
+    gated_ref[...] = (y_ref[...] * (z * jax.nn.sigmoid(z))).astype(gated_ref.dtype)
+
+
+def _columns(b_coef):
+    rows = b_coef.astype(jnp.float32).T
+    return jnp.broadcast_to(rows[:, :, None], rows.shape + (LANES,))
+
+
+def scan_end(step_size, x_in, decay_rate, b_coef, width=512):
+    steps, chans = step_size.shape
+    states = decay_rate.shape[0]
+    grid = (chans // width,)
+    return pl.pallas_call(
+        _end_kernel,
+        grid=grid,
+        in_specs=[
+            pl.BlockSpec((steps, width), lambda j: (0, j)),
+            pl.BlockSpec((steps, width), lambda j: (0, j)),
+            pl.BlockSpec((states, width), lambda j: (0, j)),
+            pl.BlockSpec((steps, states, LANES), lambda j: (0, 0, 0)),
+        ],
+        out_specs=pl.BlockSpec((states, width), lambda j: (0, j)),
+        out_shape=jax.ShapeDtypeStruct((states, chans), jnp.float32),
+        cost_estimate=pl.CostEstimate(
+            flops=6 * steps * states * chans, transcendentals=steps * states * chans,
+            bytes_accessed=steps * chans * 6 + states * chans * 8),
+    )(step_size, x_in, decay_rate, _columns(b_coef))
+
+
+def scan_gated(state_in, step_size, x_in, z_in, decay_rate, b_coef, c_coef, skip_gain, width=512):
+    steps, chans = step_size.shape
+    states = decay_rate.shape[0]
+    grid = (chans // width,)
+    col = lambda j: (0, j)
+    return pl.pallas_call(
+        _out_kernel,
+        grid=grid,
+        in_specs=[
+            pl.BlockSpec((states, width), col),
+            pl.BlockSpec((steps, width), col),
+            pl.BlockSpec((steps, width), col),
+            pl.BlockSpec((steps, width), col),
+            pl.BlockSpec((states, width), col),
+            pl.BlockSpec((steps, states, LANES), lambda j: (0, 0, 0)),
+            pl.BlockSpec((steps, states, LANES), lambda j: (0, 0, 0)),
+            pl.BlockSpec((1, width), col),
+        ],
+        out_specs=pl.BlockSpec((steps, width), col),
+        out_shape=jax.ShapeDtypeStruct((steps, chans), jnp.bfloat16),
+        scratch_shapes=[pltpu.VMEM((steps, width), jnp.float32)],
+        cost_estimate=pl.CostEstimate(
+            flops=9 * steps * states * chans, transcendentals=steps * states * chans + steps * chans,
+            bytes_accessed=steps * chans * 10 + states * chans * 8),
+    )(state_in, step_size, x_in, z_in, decay_rate, _columns(b_coef), _columns(c_coef), skip_gain[None, :])
 
 
 def entering(value, axis, join, neutral):
@@ -70,15 +172,12 @@
 ):
     step_size = jax.nn.softplus(step_raw.astype(jnp.float32) + step_bias[None, :])
     x_float = x_in.astype(jnp.float32)
-    b_rows = b_coef.astype(jnp.float32).T
-    c_rows = c_coef.astype(jnp.float32).T
-    state_end = end_state(step_size, x_float, decay_rate, b_rows)
+    state_end = scan_end(step_size, x_in, decay_rate, b_coef)
     decay_end = jnp.exp(-decay_rate * jnp.sum(step_size, axis=0)[None, :])
     identity = (1.0, 0.0)
     carried = entering((decay_end, state_end), "seq", pair_combine, identity)
     state_in = carried[1]
-    scanned = scan_outputs(state_in, step_size, x_float, decay_rate, b_rows, c_rows, skip_gain)
-    gated = (scanned * jax.nn.silu(z_in.astype(jnp.float32))).astype(jnp.bfloat16)
+    gated = scan_gated(state_in, step_size, x_in, z_in, decay_rate, b_coef, c_coef, skip_gain)
     seq_count = lax.axis_size("seq")
     expert_count = lax.axis_size("expert")
     rows = residual.shape[0]

time: 429 us -> 354 us (0.83)
  other arithmetic: 90.4 us -> 10 us
  Pallas kernels: 0 us -> 17.1 us
  local copies, waits for them, and re-layouts: 16.7 us -> 7.01 us
    reduce_sum x48 -> x0, other arithmetic: 54.9 us -> none  [scan_advance(): y_now = jnp.sum(c_now[:, None] * state, axis=0) + skip_gain * x_now]
    add x32 -> x0, other arithmetic: 20.3 us -> none  [the longest x16 18.6 us: end_advance(): jnp.exp(-step_now[None, :] * decay_rate) * state]
    pallas_call x0 -> x2, Pallas kernels: none -> 17.1 us  [the longest x1 10.9 us: scan_gated(): pl.pallas_call(_out_kernel, grid=grid, in_specs=[pl.BlockSpec((states, wi...]
    dynamic_update_slice x16 -> x0, local copies, waits for them, and re-layouts: 10 us -> none  [scan_outputs(): lax.scan(scan_advance, state_in, (step_size, x_float, b_rows, c_rows), un...]
where the time goes in v2:
time: 354 us; the launch traced here: 353 us
  waiting for transfers between devices  266 us (75%)
  matrix products  35.2 us (10%)
  Pallas kernels  17.1 us (5%)
  between operations  13.3 us (4%)
  other arithmetic  10 us (3%)
  local copies, waits for them, and re-layouts  7.01 us (2%)
  starting transfers between devices  4.79 us (1%)
    reduce_scatter x1, waiting for transfers between devices, on_device(): lax.psum_scatter(jnp.dot(active, down_weight, preferred_element_type=jnp....  92.3 us
    all_gather x1, waiting for transfers between devices, on_device(): inputs = lax.all_gather(send_rows, ('seq', 'expert'), axis=0, tiled=True)  50.5 us
    reduce_scatter x1, waiting for transfers between devices, on_device(): lax.psum_scatter(column_part, 'expert', scatter_dimension=0, tiled=True)  46.8 us
    all_gather x1, waiting for transfers between devices, on_device(): gathered = lax.all_gather(gated, 'seq', axis=0, tiled=True)  32.6 us
    all_gather x1, waiting for transfers between devices, entering(): stacked = lax.all_gather(jnp.stack(value), axis)  28 us
    dot_general x1, matrix products, on_device(): jnp.dot(active, down_weight, preferred_element_type=jnp.float32)  17.1 us
    all_to_all x1, waiting for transfers between devices, on_device(): lax.all_to_all(summed, 'seq', split_axis=0, concat_axis=0, tiled=True)  15.6 us
    pallas_call x1, Pallas kernels, scan_gated(): pl.pallas_call(_out_kernel, grid=grid, in_specs=[pl.BlockSpec((states, wi...  10.9 us
  transfers between devices with their start and end apart: 6, of which 6 were waited for; matrix products, arithmetic and copies ran while one was open for 0% of the time, Pallas kernels for 0%

profile of v2, /device:TPU:0, one launch (start us, length us, event | category | flops | bytes accessed | tf_op | source)
XLA Modules:
  0.0 353.2 jit_solution(1550610798099290021)
XLA Ops:
  6.5 0.7 convert_bitcast_fusion.1
  7.4 2.7 fusion.45
  10.1 0.9 exponential_bitcast_fusion
  11.0 1.3 broadcast_in_dim.19.b_ref
  12.3 6.2 %shard_map.154 = f32[16,2048]{1,0:T(8,128)} custom-call(f32[128,2048]{1,0:T(8,128)} %get-tuple-element.10.step_ref, bf16[128,2048]{1,0:T(8,128)(2,1)} %x_ref.3, f32[16,2048]{1,0:T(8,128)} %decay_ref.3, f32[128,16,128]{2,1,0:T(8,128)} %broadcast_in_dim.19.b_ref), custom_call_target="tpu_custom_call" | custom-call | flops 25165824 | bytes 1835008 | tf_op jit(solution)/shard_map/pallas_call | solution.py:67
  18.6 1.6 pad_maximum_fusion
  20.4 28.0 %all-gather.9.cloned.1.call-done = f32[16,16,2048]{2,1,0:T(8,128)} async-done(((f32[2,16,2048]{2,1,0:T(8,128)}), f32[16,16,2048]{2,1,0:T(8,128)}) %all-gather.9.cloned.1.call-update) | async-done | bytes 2097168 | tf_op jit(solution)/shard_map/all_gather | solution.py:113
  48.4 2.3 fusion.15.state_in_ref
  50.7 1.3 broadcast_in_dim.21.c_ref
  52.0 10.9 %shard_map.155 = bf16[128,2048]{1,0:T(8,128)(2,1)} custom-call(f32[16,2048]{1,0:T(8,128)} %fusion.15.state_in_ref, f32[128,2048]{1,0:T(8,128)} %get-tuple-element.10.step_ref, bf16[128,2048]{1,0:T(8,128)(2,1)} %x_ref.3, bf16[128,2048]{1,0:T(8,128)(2,1)} %z_ref.1, f32[16,2048]{1,0:T(8,128)} %decay_ref.3, f32[128,16,128]{2,1,0:T(8,128)} %broadcast_in_dim.19.b_ref, ...), custom_call_target="tpu_custom_call" | custom-call | flops 37748736 | bytes 2883584 | tf_op jit(solution)/shard_map/pallas_call | solution.py:89
  63.0 32.6 %all-gather.5.cloned.1.call-done = bf16[1024,2048]{1,0:T(8,128)(2,1)} async-done(((bf16[128,2048]{1,0:T(8,128)(2,1)}), bf16[1024,2048]{1,0:T(8,128)(2,1)}) %all-gather.5.cloned.1.call-update) | async-done | bytes 4194320 | tf_op jit(solution)/shard_map/all_gather | solution.py:184
  95.6 2.7 copy.39
  98.2 0.8 copy-done.5
  99.0 6.0 %fusion.46 = f32[1024,1024]{1,0:T(8,128)} fusion(bf16[1024,2048]{1,0:T(8,128)(2,1)S(1)} %bitcast.190, bf16[2048,1024]{1,0:T(8,128)(2,1)S(1)} %copy-done.5), kind=kOutput, calls=%fused_computation.82 | convolution fusion | flops 4294967296 | bytes 12582912 | tf_op jit(solution)/shard_map/dot_general | solution.py:187
  105.1 46.8 %reduce-scatter.3.cloned.1.call-done = f32[256,1024]{1,0:T(8,128)} async-done(((f32[1024,1024]{1,0:T(8,128)}), f32[256,1024]{1,0:T(8,128)}) %reduce-scatter.3.cloned.1.call-update) | async-done | bytes 1048592 | tf_op jit(solution)/shard_map/reduce_scatter | solution.py:188
  151.9 4.4 %all-to-all-start = ((f32[8,32,1024]{2,1,0:T(8,128)}), f32[8,32,1024]{2,1,0:T(8,128)S(1)}, u32[]{:S(2)}, u32[]{:S(2)}) async-start(f32[8,32,1024]{2,1,0:T(8,128)} %bitcast.194), calls=%async_computation.1 | async-start | bytes 2097152 | tf_op jit(solution)/shard_map/all_to_all | solution.py:190
  156.7 15.6 %all-to-all-done = f32[8,32,1024]{2,1,0:T(8,128)S(1)} async-done(((f32[8,32,1024]{2,1,0:T(8,128)}), f32[8,32,1024]{2,1,0:T(8,128)S(1)}, u32[]{:S(2)}, u32[]{:S(2)}) %all-to-all-start) | async-done | bytes 1048608 | tf_op jit(solution)/shard_map/all_to_all | solution.py:190
  173.8 0.6 fusion.12
  174.4 0.9 convolution_convert_fusion.1
  175.6 50.5 %all-gather.7.cloned.1.call-done = bf16[512,8192]{1,0:T(8,128)(2,1)} async-done(((bf16[16,8192]{1,0:T(8,128)(2,1)}), bf16[512,8192]{1,0:T(8,128)(2,1)}) %all-gather.7.cloned.1.call-update) | async-done | bytes 8388624 | tf_op jit(solution)/shard_map/all_gather | solution.py:223
  226.1 8.8 %fusion.47 = f32[512,384]{1,0:T(8,128)S(1)} fusion(bf16[512,8192]{1,0:T(8,128)(2,1)} %all-gather.7.cloned.1.call-done, bf16[8192,384]{1,0:T(8,128)(2,1)} %param.29), kind=kOutput, calls=%fused_computation.83 | convolution fusion | flops 3221225472 | bytes 15466496 | tf_op jit(solution)/shard_map/dot_general | solution.py:224
  234.9 17.1 %convolution_convert_fusion = bf16[512,8192]{1,0:T(8,128)(2,1)} fusion(bf16[384,8192]{1,0:T(8,128)(2,1)} %param.31, bf16[512,8192]{1,0:T(8,128)(2,1)} %all-gather.7.cloned.1.call-done, bf16[8192,384]{1,0:T(8,128)(2,1)} %param.30, f32[512,384]{1,0:T(8,128)S(1)} %fusion.47), kind=kOutput, calls=%fused_computation | convolution fusion | flops 6447824896 | bytes 30146560 | tf_op jit(solution)/shard_map/dot_general | solution.py:228
  252.3 92.3 %reduce-scatter.5.cloned.1.call-done = bf16[16,8192]{1,0:T(8,128)(2,1)} async-done(((bf16[512,8192]{1,0:T(8,128)(2,1)}), bf16[16,8192]{1,0:T(8,128)(2,1)}) %reduce-scatter.5.cloned.1.call-update) | async-done | bytes 262160 | tf_op jit(solution)/shard_map/reduce_scatter | solution.py:227
  344.6 2.1 fusion.1
  (41 shorter events, 2.7 us)
Async XLA Ops:
  6.5 245.5 %copy-start = (bf16[8192,16]{0,1:T(8,128)(2,1)S(1)}, bf16[8192,16]{0,1:T(8,128)(2,1)}, u32[]{:S(2)}) copy-start(bf16[8192,16]{0,1:T(8,128)(2,1)} %param.27) | copy-start | bytes 786436
  6.5 13.8 %copy-start.3 = (bf16[16,128]{1,0:T(8,128)(2,1)S(1)}, bf16[16,128]{1,0:T(8,128)(2,1)}, u32[]{:S(2)}) copy-start(bf16[16,128]{1,0:T(8,128)(2,1)} %param.22) | copy-start | bytes 12292
  6.5 41.8 %all-gather.9.cloned.1.call-start = ((), (), s32[]{:S(2)}) async-start(), calls=%async_computation.7 | async-start | bytes 2359296 | tf_op jit(solution)/shard_map/all_gather | solution.py:113
  20.2 75.3 %all-gather.5.cloned.1.call-start = ((), (), s32[]{:S(2)}) async-start(), calls=%async_computation.3 | async-start | bytes 4718592 | tf_op jit(solution)/shard_map/all_gather | solution.py:184
  62.9 89.0 %reduce-scatter.3.cloned.1.call-start = ((), (), s32[]{:S(2)}) async-start(), calls=%async_computation.4 | async-start | bytes 5242880 | tf_op jit(solution)/shard_map/reduce_scatter | solution.py:188
  95.6 3.4 copy-start.5
  105.0 51.3 %copy-start.4 = (s32[32,2]{0,1:T(2,128)S(1)}, s32[32,2]{0,1:T(2,128)}, u32[]{:S(2)}) copy-start(s32[32,2]{0,1:T(2,128)} %param.28) | copy-start | bytes 772
  105.1 67.3 %copy-start.1 = (bf16[32,8192]{1,0:T(8,128)(2,1)S(1)}, bf16[32,8192]{1,0:T(8,128)(2,1)}, u32[]{:S(2)}) copy-start(bf16[32,8192]{1,0:T(8,128)(2,1)} %param.25) | copy-start | bytes 1572868
  105.1 67.6 %copy-start.2 = (f32[8192]{0:T(1024)S(1)}, f32[8192]{0:T(1024)}, u32[]{:S(2)}) copy-start(f32[8192]{0:T(1024)} %param.26) | copy-start | bytes 98308
  151.9 20.4 %all-to-all-start = ((f32[8,32,1024]{2,1,0:T(8,128)}), f32[8,32,1024]{2,1,0:T(8,128)S(1)}, u32[]{:S(2)}, u32[]{:S(2)}) async-start(f32[8,32,1024]{2,1,0:T(8,128)} %bitcast.194), calls=%async_computation.1 | async-start | bytes 2097152 | tf_op jit(solution)/shard_map/all_to_all | solution.py:190
  156.3 69.8 %all-gather.7.cloned.1.call-start = ((), (), s32[]{:S(2)}) async-start(), calls=%async_computation.5 | async-start | bytes 8650752 | tf_op jit(solution)/shard_map/all_gather | solution.py:223
  175.3 169.3 %reduce-scatter.5.cloned.1.call-start = ((), (), s32[]{:S(2)}) async-start(), calls=%async_computation.6 | async-start | bytes 8650752 | tf_op jit(solution)/shard_map/reduce_scatter | solution.py:227
Sparse Core Ops, SparseCore 0:
  20.3 27.9 all-gather.8
  63.0 32.4 all-gather.4
  105.2 46.6 reduce-scatter.2
  175.5 50.5 all-gather.6
  252.1 92.4 reduce-scatter.4

commit v3 on v2

--- a/solution.py
+++ b/solution.py
@@ -108,48 +108,15 @@
     )(state_in, step_size, x_in, z_in, decay_rate, _columns(b_coef), _columns(c_coef), skip_gain[None, :])
 
 
-def entering(value, axis, join, neutral):
+def entering_state(state_end, step_total, decay_rate, axis):
     count, mine = (lax.axis_size(axis), lax.axis_index(axis))
-    stacked = lax.all_gather(jnp.stack(value), axis)
-    running = tuple(jnp.full_like(part, zero) for part, zero in zip(value, neutral))
+    stacked = lax.all_gather(jnp.concatenate([state_end, step_total[None, :]], axis=0), axis)
+    running = jnp.zeros_like(state_end)
     for position in range(count - 1):
-        longer = join(running, (stacked[position, 0], stacked[position, 1]))
-        running = tuple(jnp.where(position < mine, new, old) for new, old in zip(longer, running))
+        decay_then = jnp.exp(-decay_rate * stacked[position, -1][None, :])
+        longer = decay_then * running + stacked[position, :-1]
+        running = jnp.where(position < mine, longer, running)
     return running
-
-
-def pair_combine(early, later):
-    return (early[0] * later[0], later[0] * early[1] + later[1])
-
-
-def end_state(step_size, x_float, decay_rate, b_rows):
-
-    def end_advance(state, inputs):
-        step_now, x_now, b_now = inputs
-        state = (
-            jnp.exp(-step_now[None, :] * decay_rate) * state
-            + (step_now * x_now)[None, :] * b_now[:, None]
-        )
-        return (state, None)
-
-    start_state = jnp.zeros(decay_rate.shape, jnp.float32)
-    final_state, _ = lax.scan(end_advance, start_state, (step_size, x_float, b_rows), unroll=8)
-    return final_state
-
-
-def scan_outputs(state_in, step_size, x_float, decay_rate, b_rows, c_rows, skip_gain):
-
-    def scan_advance(state, inputs):
-        step_now, x_now, b_now, c_now = inputs
-        state = (
-            jnp.exp(-step_now[None, :] * decay_rate) * state
-            + (step_now * x_now)[None, :] * b_now[:, None]
-        )
-        y_now = jnp.sum(c_now[:, None] * state, axis=0) + skip_gain * x_now
-        return (state, y_now)
-
-    _, outputs = lax.scan(scan_advance, state_in, (step_size, x_float, b_rows, c_rows), unroll=8)
-    return outputs
 
 
 def on_device(
@@ -171,12 +138,8 @@
     down_weight,
 ):
     step_size = jax.nn.softplus(step_raw.astype(jnp.float32) + step_bias[None, :])
-    x_float = x_in.astype(jnp.float32)
     state_end = scan_end(step_size, x_in, decay_rate, b_coef)
-    decay_end = jnp.exp(-decay_rate * jnp.sum(step_size, axis=0)[None, :])
-    identity = (1.0, 0.0)
-    carried = entering((decay_end, state_end), "seq", pair_combine, identity)
-    state_in = carried[1]
+    state_in = entering_state(state_end, jnp.sum(step_size, axis=0), decay_rate, "seq")
     gated = scan_gated(state_in, step_size, x_in, z_in, decay_rate, b_coef, c_coef, skip_gain)
     seq_count = lax.axis_size("seq")
     expert_count = lax.axis_size("expert")
@@ -184,7 +147,7 @@
     gathered = lax.all_gather(gated, "seq", axis=0, tiled=True)
     gathered = gathered.reshape(seq_count, expert_count, rows, gated.shape[1])
     gathered = jnp.transpose(gathered, (1, 0, 2, 3)).reshape(-1, gated.shape[1])
-    column_part = jnp.dot(gathered, out_proj, preferred_element_type=jnp.float32)
+    column_part = jnp.dot(gathered, out_proj, preferred_element_type=jnp.float32).astype(jnp.bfloat16)
     summed = lax.psum_scatter(column_part, "expert", scatter_dimension=0, tiled=True)
     summed = summed.reshape(seq_count, rows, column_part.shape[1])
     swapped = lax.all_to_all(summed, "seq", split_axis=0, concat_axis=0, tiled=True)

time: 354 us -> 329 us (0.929)
  waiting for transfers between devices: 266 us -> 242 us
    reduce_scatter x1, waiting for transfers between devices: 46.8 us -> 29.7 us  [on_device(): lax.psum_scatter(column_part, 'expert', scatter_dimension=0, tiled=True)]
    all_to_all x1, waiting for transfers between devices: 15.6 us -> 9.96 us  [on_device(): lax.all_to_all(summed, 'seq', split_axis=0, concat_axis=0, tiled=True)]
where the time goes in v3:
time: 329 us
  waiting for transfers between devices  242 us (74%)
  matrix products  34.9 us (11%)
  Pallas kernels  17.1 us (5%)
  between operations  13.3 us (4%)
  other arithmetic  8.94 us (3%)
  local copies, waits for them, and re-layouts  8.05 us (2%)
  starting transfers between devices  4.76 us (1%)
    reduce_scatter x1, waiting for transfers between devices, on_device(): lax.psum_scatter(jnp.dot(active, down_weight, preferred_element_type=jnp....  92.3 us
    all_gather x1, waiting for transfers between devices, on_device(): inputs = lax.all_gather(send_rows, ('seq', 'expert'), axis=0, tiled=True)  50.5 us
    all_gather x1, waiting for transfers between devices, on_device(): gathered = lax.all_gather(gated, 'seq', axis=0, tiled=True)  32.3 us
    reduce_scatter x1, waiting for transfers between devices, on_device(): lax.psum_scatter(column_part, 'expert', scatter_dimension=0, tiled=True)  29.7 us
    all_gather x1, waiting for transfers between devices, entering_state(): lax.all_gather(jnp.concatenate([state_end, step_total[None, :]], axis=0),...  27.1 us
    dot_general x1, matrix products, on_device(): jnp.dot(active, down_weight, preferred_element_type=jnp.float32)  17.1 us
    pallas_call x1, Pallas kernels, scan_gated(): pl.pallas_call(_out_kernel, grid=grid, in_specs=[pl.BlockSpec((states, wi...  10.9 us
    all_to_all x1, waiting for transfers between devices, on_device(): lax.all_to_all(summed, 'seq', split_axis=0, concat_axis=0, tiled=True)  9.96 us
  transfers between devices with their start and end apart: 6, of which 6 were waited for; matrix products, arithmetic and copies ran while one was open for 0% of the time, Pallas kernels for 0%

profile of v3, /device:TPU:0, one launch (start us, length us, event | category | flops | bytes accessed | tf_op | source)
XLA Modules:
  0.0 329.0 jit_solution(6996495638037577613)
XLA Ops:
  6.5 0.7 convert_bitcast_fusion.2
  7.4 2.7 compare_select_fusion
  10.1 1.3 broadcast_in_dim.21.b_ref
  11.4 6.2 %shard_map.154 = f32[16,2048]{1,0:T(8,128)} custom-call(f32[128,2048]{1,0:T(8,128)} %get-tuple-element.16.step_ref, bf16[128,2048]{1,0:T(8,128)(2,1)} %x_ref.3, f32[16,2048]{1,0:T(8,128)} %decay_ref.3, f32[128,16,128]{2,1,0:T(8,128)} %broadcast_in_dim.21.b_ref), custom_call_target="tpu_custom_call" | custom-call | flops 25165824 | bytes 1835008 | tf_op jit(solution)/shard_map/pallas_call | solution.py:67
  17.6 1.6 maximum_bitcast_fusion
  19.4 27.1 %all-gather.10.cloned.1.call-done = f32[8,17,2048]{2,1,0:T(8,128)} async-done(((f32[1,17,2048]{2,1,0:T(8,128)}), f32[8,17,2048]{2,1,0:T(8,128)}) %all-gather.10.cloned.1.call-update) | async-done | bytes 1114128 | tf_op jit(solution)/shard_map/all_gather | solution.py:113
  46.5 1.1 fusion.40
  47.6 2.1 fusion.15.state_in_ref
  49.7 1.3 broadcast_in_dim.24.c_ref
  51.0 10.9 %shard_map.155 = bf16[128,2048]{1,0:T(8,128)(2,1)} custom-call(f32[16,2048]{1,0:T(8,128)} %fusion.15.state_in_ref, f32[128,2048]{1,0:T(8,128)} %get-tuple-element.16.step_ref, bf16[128,2048]{1,0:T(8,128)(2,1)} %x_ref.3, bf16[128,2048]{1,0:T(8,128)(2,1)} %z_ref.1, f32[16,2048]{1,0:T(8,128)} %decay_ref.3, f32[128,16,128]{2,1,0:T(8,128)} %broadcast_in_dim.21.b_ref, ...), custom_call_target="tpu_custom_call" | custom-call | flops 37748736 | bytes 2883584 | tf_op jit(solution)/shard_map/pallas_call | solution.py:89
  62.0 32.3 %all-gather.6.cloned.1.call-done = bf16[1024,2048]{1,0:T(8,128)(2,1)} async-done(((bf16[128,2048]{1,0:T(8,128)(2,1)}), bf16[1024,2048]{1,0:T(8,128)(2,1)}) %all-gather.6.cloned.1.call-update) | async-done | bytes 4194320 | tf_op jit(solution)/shard_map/all_gather | solution.py:147
  94.3 2.7 copy.39
  96.9 0.8 copy-done.6
  97.7 5.7 %convolution_convert_fusion.2 = bf16[1024,1024]{1,0:T(8,128)(2,1)} fusion(bf16[1024,2048]{1,0:T(8,128)(2,1)S(1)} %bitcast.105, bf16[2048,1024]{1,0:T(8,128)(2,1)S(1)} %copy-done.6), kind=kOutput, calls=%fused_computation.6 | convolution fusion | flops 4296015872 | bytes 10485760 | tf_op jit(solution)/shard_map/dot_general | solution.py:150
  103.5 29.7 %reduce-scatter.3.cloned.1.call-done = bf16[256,1024]{1,0:T(8,128)(2,1)} async-done(((bf16[1024,1024]{1,0:T(8,128)(2,1)}), bf16[256,1024]{1,0:T(8,128)(2,1)}) %reduce-scatter.3.cloned.1.call-update) | async-done | bytes 524304 | tf_op jit(solution)/shard_map/reduce_scatter | solution.py:151
  133.2 4.4 %all-to-all-start = ((bf16[8,32,1024]{2,1,0:T(8,128)(2,1)}), bf16[8,32,1024]{2,1,0:T(8,128)(2,1)S(1)}, u32[]{:S(2)}, u32[]{:S(2)}) async-start(bf16[8,32,1024]{2,1,0:T(8,128)(2,1)} %bitcast.107), calls=%async_computation.1 | async-start | bytes 1048576 | tf_op jit(solution)/shard_map/all_to_all | solution.py:153
  137.9 10.0 %all-to-all-done = bf16[8,32,1024]{2,1,0:T(8,128)(2,1)S(1)} async-done(((bf16[8,32,1024]{2,1,0:T(8,128)(2,1)}), bf16[8,32,1024]{2,1,0:T(8,128)(2,1)S(1)}, u32[]{:S(2)}, u32[]{:S(2)}) %all-to-all-start) | async-done | bytes 524320 | tf_op jit(solution)/shard_map/all_to_all | solution.py:153
  149.5 0.6 fusion.12
  150.1 0.9 convolution_convert_fusion.1
  151.3 50.5 %all-gather.8.cloned.1.call-done = bf16[512,8192]{1,0:T(8,128)(2,1)} async-done(((bf16[16,8192]{1,0:T(8,128)(2,1)}), bf16[512,8192]{1,0:T(8,128)(2,1)}) %all-gather.8.cloned.1.call-update) | async-done | bytes 8388624 | tf_op jit(solution)/shard_map/all_gather | solution.py:186
  201.8 8.8 %fusion.41 = f32[512,384]{1,0:T(8,128)S(1)} fusion(bf16[512,8192]{1,0:T(8,128)(2,1)} %all-gather.8.cloned.1.call-done, bf16[8192,384]{1,0:T(8,128)(2,1)} %param.29), kind=kOutput, calls=%fused_computation.71 | convolution fusion | flops 3221225472 | bytes 15466496 | tf_op jit(solution)/shard_map/dot_general | solution.py:187
  210.6 17.1 %convolution_convert_fusion = bf16[512,8192]{1,0:T(8,128)(2,1)} fusion(bf16[384,8192]{1,0:T(8,128)(2,1)} %param.31, bf16[512,8192]{1,0:T(8,128)(2,1)} %all-gather.8.cloned.1.call-done, bf16[8192,384]{1,0:T(8,128)(2,1)} %param.30, f32[512,384]{1,0:T(8,128)S(1)} %fusion.41), kind=kOutput, calls=%fused_computation | convolution fusion | flops 6447824896 | bytes 30146560 | tf_op jit(solution)/shard_map/dot_general | solution.py:191
  228.1 92.3 %reduce-scatter.5.cloned.1.call-done = bf16[16,8192]{1,0:T(8,128)(2,1)} async-done(((bf16[512,8192]{1,0:T(8,128)(2,1)}), bf16[16,8192]{1,0:T(8,128)(2,1)}) %reduce-scatter.5.cloned.1.call-update) | async-done | bytes 262160 | tf_op jit(solution)/shard_map/reduce_scatter | solution.py:190
  320.4 2.1 fusion.1
  (44 shorter events, 2.8 us)
Async XLA Ops:
  6.5 221.2 %copy-start = (bf16[8192,16]{0,1:T(8,128)(2,1)S(1)}, bf16[8192,16]{0,1:T(8,128)(2,1)}, u32[]{:S(2)}) copy-start(bf16[8192,16]{0,1:T(8,128)(2,1)} %param.27) | copy-start | bytes 786436
  6.5 41.1 %copy-start.3 = (f32[16,2048]{1,0:T(8,128)S(1)}, f32[16,2048]{1,0:T(8,128)}, u32[]{:S(2)}) copy-start(f32[16,2048]{1,0:T(8,128)} %decay_ref.3) | copy-start | bytes 393220
  6.5 12.8 %copy-start.4 = (bf16[16,128]{1,0:T(8,128)(2,1)S(1)}, bf16[16,128]{1,0:T(8,128)(2,1)}, u32[]{:S(2)}) copy-start(bf16[16,128]{1,0:T(8,128)(2,1)} %param.22) | copy-start | bytes 12292
  6.5 40.0 %all-gather.10.cloned.1.call-start = ((), (), s32[]{:S(2)}) async-start(), calls=%async_computation.7 | async-start | bytes 1769472 | tf_op jit(solution)/shard_map/all_gather | solution.py:113
  19.2 75.0 %all-gather.6.cloned.1.call-start = ((), (), s32[]{:S(2)}) async-start(), calls=%async_computation.3 | async-start | bytes 4718592 | tf_op jit(solution)/shard_map/all_gather | solution.py:147
  62.0 71.2 %reduce-scatter.3.cloned.1.call-start = ((), (), s32[]{:S(2)}) async-start(), calls=%async_computation.4 | async-start | bytes 2621440 | tf_op jit(solution)/shard_map/reduce_scatter | solution.py:151
  94.3 3.4 %copy-start.6 = (bf16[2048,1024]{1,0:T(8,128)(2,1)S(1)}, bf16[2048,1024]{1,0:T(8,128)(2,1)}, u32[]{:S(2)}) copy-start(bf16[2048,1024]{1,0:T(8,128)(2,1)} %param.24) | copy-start | bytes 12582916
  97.7 39.9 %copy-start.5 = (s32[32,2]{0,1:T(2,128)S(1)}, s32[32,2]{0,1:T(2,128)}, u32[]{:S(2)}) copy-start(s32[32,2]{0,1:T(2,128)} %param.28) | copy-start | bytes 772
  103.5 44.6 %copy-start.1 = (bf16[32,8192]{1,0:T(8,128)(2,1)S(1)}, bf16[32,8192]{1,0:T(8,128)(2,1)}, u32[]{:S(2)}) copy-start(bf16[32,8192]{1,0:T(8,128)(2,1)} %param.25) | copy-start | bytes 1572868
  103.5 44.9 %copy-start.2 = (f32[8192]{0:T(1024)S(1)}, f32[8192]{0:T(1024)}, u32[]{:S(2)}) copy-start(f32[8192]{0:T(1024)} %param.26) | copy-start | bytes 98308
  133.2 14.7 %all-to-all-start = ((bf16[8,32,1024]{2,1,0:T(8,128)(2,1)}), bf16[8,32,1024]{2,1,0:T(8,128)(2,1)S(1)}, u32[]{:S(2)}, u32[]{:S(2)}) async-start(bf16[8,32,1024]{2,1,0:T(8,128)(2,1)} %bitcast.107), calls=%async_computation.1 | async-start | bytes 1048576 | tf_op jit(solution)/shard_map/all_to_all | solution.py:153
  137.6 64.3 %all-gather.8.cloned.1.call-start = ((), (), s32[]{:S(2)}) async-start(), calls=%async_computation.5 | async-start | bytes 8650752 | tf_op jit(solution)/shard_map/all_gather | solution.py:186
  151.1 169.3 %reduce-scatter.5.cloned.1.call-start = ((), (), s32[]{:S(2)}) async-start(), calls=%async_computation.6 | async-start | bytes 8650752 | tf_op jit(solution)/shard_map/reduce_scatter | solution.py:190
Sparse Core Ops, SparseCore 0:
  19.4 27.1 all-gather.9
  62.1 32.1 all-gather.5
  103.6 29.5 reduce-scatter.2
  151.2 50.6 all-gather.7
  227.9 92.4 reduce-scatter.4

commit v4 on v3

--- a/solution.py
+++ b/solution.py
@@ -145,13 +145,12 @@
     expert_count = lax.axis_size("expert")
     rows = residual.shape[0]
     gathered = lax.all_gather(gated, "seq", axis=0, tiled=True)
-    gathered = gathered.reshape(seq_count, expert_count, rows, gated.shape[1])
-    gathered = jnp.transpose(gathered, (1, 0, 2, 3)).reshape(-1, gated.shape[1])
     column_part = jnp.dot(gathered, out_proj, preferred_element_type=jnp.float32).astype(jnp.bfloat16)
-    summed = lax.psum_scatter(column_part, "expert", scatter_dimension=0, tiled=True)
-    summed = summed.reshape(seq_count, rows, column_part.shape[1])
-    swapped = lax.all_to_all(summed, "seq", split_axis=0, concat_axis=0, tiled=True)
-    mamba_out = jnp.transpose(swapped, (1, 0, 2)).reshape(rows, -1)
+    column_part = column_part.reshape(seq_count * expert_count, rows, column_part.shape[1])
+    swapped = lax.all_to_all(column_part, ("seq", "expert"), split_axis=0, concat_axis=0, tiled=True)
+    swapped = swapped.reshape(seq_count, expert_count, rows, column_part.shape[2])
+    summed = jnp.sum(swapped.astype(jnp.float32), axis=1)
+    mamba_out = jnp.transpose(summed, (1, 0, 2)).reshape(rows, -1)
     hidden = (residual.astype(jnp.float32) + mamba_out).astype(jnp.bfloat16)
     hidden_f = hidden.astype(jnp.float32)
     width_d = hidden.shape[1]

time: 329 us -> 320 us (0.973)
  waiting for transfers between devices: 242 us -> 231 us
  matrix products: 34.9 us -> 38.4 us
  local copies, waits for them, and re-layouts: 8.05 us -> 4.61 us
    reduce_scatter x1 -> x0, waiting for transfers between devices: 29.7 us -> none  [on_device(): lax.psum_scatter(column_part, 'expert', scatter_dimension=0, tiled=True)]
    all_to_all x1, waiting for transfers between devices: 9.96 us -> 27.3 us  [on_device(): lax.all_to_all(column_part, ('seq', 'expert'), split_axis=0, concat_axis=...]
    dot_general x1, matrix products: 5.74 us -> 9.28 us  [on_device(): jnp.dot(gathered, out_proj, preferred_element_type=jnp.float32)]
  transfers between devices with their start and end apart: 6 -> 5, of which waited for: 6 -> 5; matrix products, arithmetic and copies ran while one was open for 0% -> 0% of each run, Pallas kernels for 0% -> 0%
where the time goes in v4:
time: 320 us; the launch traced here: 319 us
  waiting for transfers between devices  231 us (72%)
  matrix products  38.4 us (12%)
  Pallas kernels  17.1 us (5%)
  between operations  13.3 us (4%)
  other arithmetic  9.22 us (3%)
  starting transfers between devices  6.24 us (2%)
  local copies, waits for them, and re-layouts  4.61 us (1%)
    reduce_scatter x1, waiting for transfers between devices, on_device(): lax.psum_scatter(jnp.dot(active, down_weight, preferred_element_type=jnp....  92.3 us
    all_gather x1, waiting for transfers between devices, on_device(): inputs = lax.all_gather(send_rows, ('seq', 'expert'), axis=0, tiled=True)  51.5 us
    all_gather x1, waiting for transfers between devices, on_device(): gathered = lax.all_gather(gated, 'seq', axis=0, tiled=True)  32.3 us
    all_to_all x1, waiting for transfers between devices, on_device(): lax.all_to_all(column_part, ('seq', 'expert'), split_axis=0, concat_axis=...  27.3 us
    all_gather x1, waiting for transfers between devices, entering_state(): lax.all_gather(jnp.concatenate([state_end, step_total[None, :]], axis=0),...  27.1 us
    dot_general x1, matrix products, on_device(): jnp.dot(active, down_weight, preferred_element_type=jnp.float32)  17.1 us
    pallas_call x1, Pallas kernels, scan_gated(): pl.pallas_call(_out_kernel, grid=grid, in_specs=[pl.BlockSpec((states, wi...  10.9 us
    dot_general x1, matrix products, on_device(): jnp.dot(gathered, out_proj, preferred_element_type=jnp.float32)  9.28 us
  transfers between devices with their start and end apart: 5, of which 5 were waited for; matrix products, arithmetic and copies ran while one was open for 0% of the time, Pallas kernels for 0%

profile of v4, /device:TPU:0, one launch (start us, length us, event | category | flops | bytes accessed | tf_op | source)
XLA Modules:
  0.0 319.4 jit_solution(8060728264373921183)
XLA Ops:
  6.5 0.7 convert_bitcast_fusion.1
  7.4 2.7 compare_select_fusion
  10.1 1.3 broadcast_in_dim.21.b_ref
  11.4 6.2 %shard_map.154 = f32[16,2048]{1,0:T(8,128)} custom-call(f32[128,2048]{1,0:T(8,128)} %get-tuple-element.16.step_ref, bf16[128,2048]{1,0:T(8,128)(2,1)} %x_ref.3, f32[16,2048]{1,0:T(8,128)} %decay_ref.3, f32[128,16,128]{2,1,0:T(8,128)} %broadcast_in_dim.21.b_ref), custom_call_target="tpu_custom_call" | custom-call | flops 25165824 | bytes 1835008 | tf_op jit(solution)/shard_map/pallas_call | solution.py:67
  17.6 1.6 maximum_bitcast_fusion
  19.4 27.1 %all-gather.10.cloned.1.call-done = f32[8,17,2048]{2,1,0:T(8,128)} async-done(((f32[1,17,2048]{2,1,0:T(8,128)}), f32[8,17,2048]{2,1,0:T(8,128)}) %all-gather.10.cloned.1.call-update) | async-done | bytes 1114128 | tf_op jit(solution)/shard_map/all_gather | solution.py:113
  46.5 1.1 fusion.40
  47.6 2.1 fusion.15.state_in_ref
  49.7 1.3 broadcast_in_dim.24.c_ref
  51.0 10.9 %shard_map.155 = bf16[128,2048]{1,0:T(8,128)(2,1)} custom-call(f32[16,2048]{1,0:T(8,128)} %fusion.15.state_in_ref, f32[128,2048]{1,0:T(8,128)} %get-tuple-element.16.step_ref, bf16[128,2048]{1,0:T(8,128)(2,1)} %x_ref.3, bf16[128,2048]{1,0:T(8,128)(2,1)} %z_ref.1, f32[16,2048]{1,0:T(8,128)} %decay_ref.3, f32[128,16,128]{2,1,0:T(8,128)} %broadcast_in_dim.21.b_ref, ...), custom_call_target="tpu_custom_call" | custom-call | flops 37748736 | bytes 2883584 | tf_op jit(solution)/shard_map/pallas_call | solution.py:89
  62.0 32.3 %all-gather.6.cloned.1.call-done = bf16[1024,2048]{1,0:T(8,128)(2,1)} async-done(((bf16[128,2048]{1,0:T(8,128)(2,1)}), bf16[1024,2048]{1,0:T(8,128)(2,1)}) %all-gather.6.cloned.1.call-update) | async-done | bytes 4194320 | tf_op jit(solution)/shard_map/all_gather | solution.py:147
  94.3 9.3 %convolution_convert_fusion.2 = bf16[1024,1024]{1,0:T(8,128)(2,1)} fusion(bf16[1024,2048]{1,0:T(8,128)(2,1)} %all-gather.6.cloned.1.call-done, bf16[2048,1024]{1,0:T(8,128)(2,1)} %param.24), kind=kOutput, calls=%fused_computation.7 | convolution fusion | flops 4296015872 | bytes 10485760 | tf_op jit(solution)/shard_map/dot_general | solution.py:148
  103.6 5.9 %all-to-all-start = ((bf16[32,32,1024]{2,1,0:T(8,128)(2,1)}), bf16[32,32,1024]{2,1,0:T(8,128)(2,1)S(1)}, u32[]{:S(2)}, u32[]{:S(2)}) async-start(bf16[32,32,1024]{2,1,0:T(8,128)(2,1)} %bitcast.104), calls=%async_computation | async-start | bytes 4194304 | tf_op jit(solution)/shard_map/all_to_all | solution.py:150
  109.8 27.3 %all-to-all-done = bf16[32,32,1024]{2,1,0:T(8,128)(2,1)S(1)} async-done(((bf16[32,32,1024]{2,1,0:T(8,128)(2,1)}), bf16[32,32,1024]{2,1,0:T(8,128)(2,1)S(1)}, u32[]{:S(2)}, u32[]{:S(2)}) %all-to-all-start) | async-done | bytes 2097184 | tf_op jit(solution)/shard_map/all_to_all | solution.py:150
  137.2 0.4 convert_reduce_fusion
  138.3 0.3 reduce_max.9
  138.7 0.3 div.42
  139.0 0.6 fusion.12
  139.7 0.9 convolution_convert_fusion.1
  140.9 51.5 %all-gather.8.cloned.1.call-done = bf16[512,8192]{1,0:T(8,128)(2,1)} async-done(((bf16[16,8192]{1,0:T(8,128)(2,1)}), bf16[512,8192]{1,0:T(8,128)(2,1)}) %all-gather.8.cloned.1.call-update) | async-done | bytes 8388624 | tf_op jit(solution)/shard_map/all_gather | solution.py:185
  192.3 8.8 %fusion.41 = f32[512,384]{1,0:T(8,128)S(1)} fusion(bf16[512,8192]{1,0:T(8,128)(2,1)} %all-gather.8.cloned.1.call-done, bf16[8192,384]{1,0:T(8,128)(2,1)} %param.29), kind=kOutput, calls=%fused_computation.71 | convolution fusion | flops 3221225472 | bytes 15466496 | tf_op jit(solution)/shard_map/dot_general | solution.py:186
  201.1 17.1 %convolution_convert_fusion = bf16[512,8192]{1,0:T(8,128)(2,1)} fusion(bf16[384,8192]{1,0:T(8,128)(2,1)} %param.31, bf16[512,8192]{1,0:T(8,128)(2,1)} %all-gather.8.cloned.1.call-done, bf16[8192,384]{1,0:T(8,128)(2,1)} %param.30, f32[512,384]{1,0:T(8,128)S(1)} %fusion.41), kind=kOutput, calls=%fused_computation | convolution fusion | flops 6447824896 | bytes 30146560 | tf_op jit(solution)/shard_map/dot_general | solution.py:190
  218.6 92.3 %reduce-scatter.2.cloned.1.call-done = bf16[16,8192]{1,0:T(8,128)(2,1)} async-done(((bf16[512,8192]{1,0:T(8,128)(2,1)}), bf16[16,8192]{1,0:T(8,128)(2,1)}) %reduce-scatter.2.cloned.1.call-update) | async-done | bytes 262160 | tf_op jit(solution)/shard_map/reduce_scatter | solution.py:189
  310.8 2.1 fusion.1
  (38 shorter events, 2.0 us)
Async XLA Ops:
  6.5 211.7 %copy-start = (bf16[8192,16]{0,1:T(8,128)(2,1)S(1)}, bf16[8192,16]{0,1:T(8,128)(2,1)}, u32[]{:S(2)}) copy-start(bf16[8192,16]{0,1:T(8,128)(2,1)} %param.27) | copy-start | bytes 786436
  6.5 41.1 %copy-start.3 = (f32[16,2048]{1,0:T(8,128)S(1)}, f32[16,2048]{1,0:T(8,128)}, u32[]{:S(2)}) copy-start(f32[16,2048]{1,0:T(8,128)} %decay_ref.3) | copy-start | bytes 393220
  6.5 12.8 %copy-start.4 = (bf16[16,128]{1,0:T(8,128)(2,1)S(1)}, bf16[16,128]{1,0:T(8,128)(2,1)}, u32[]{:S(2)}) copy-start(bf16[16,128]{1,0:T(8,128)(2,1)} %param.22) | copy-start | bytes 12292
  6.5 40.0 %all-gather.10.cloned.1.call-start = ((), (), s32[]{:S(2)}) async-start(), calls=%async_computation.5 | async-start | bytes 1769472 | tf_op jit(solution)/shard_map/all_gather | solution.py:113
  19.2 75.0 %all-gather.6.cloned.1.call-start = ((), (), s32[]{:S(2)}) async-start(), calls=%async_computation.2 | async-start | bytes 4718592 | tf_op jit(solution)/shard_map/all_gather | solution.py:147
  62.0 47.6 %copy-start.5 = (s32[32,2]{0,1:T(2,128)S(1)}, s32[32,2]{0,1:T(2,128)}, u32[]{:S(2)}) copy-start(s32[32,2]{0,1:T(2,128)} %param.28) | copy-start | bytes 772
  103.5 34.1 %copy-start.1 = (bf16[32,8192]{1,0:T(8,128)(2,1)S(1)}, bf16[32,8192]{1,0:T(8,128)(2,1)}, u32[]{:S(2)}) copy-start(bf16[32,8192]{1,0:T(8,128)(2,1)} %param.25) | copy-start | bytes 1572868
  103.6 34.4 %copy-start.2 = (f32[8192]{0:T(1024)S(1)}, f32[8192]{0:T(1024)}, u32[]{:S(2)}) copy-start(f32[8192]{0:T(1024)} %param.26) | copy-start | bytes 98308
  103.6 33.6 %all-to-all-start = ((bf16[32,32,1024]{2,1,0:T(8,128)(2,1)}), bf16[32,32,1024]{2,1,0:T(8,128)(2,1)S(1)}, u32[]{:S(2)}, u32[]{:S(2)}) async-start(bf16[32,32,1024]{2,1,0:T(8,128)(2,1)} %bitcast.104), calls=%async_computation | async-start | bytes 4194304 | tf_op jit(solution)/shard_map/all_to_all | solution.py:150
  109.5 82.8 %all-gather.8.cloned.1.call-start = ((), (), s32[]{:S(2)}) async-start(), calls=%async_computation.3 | async-start | bytes 8650752 | tf_op jit(solution)/shard_map/all_gather | solution.py:185
  140.6 170.2 %reduce-scatter.2.cloned.1.call-start = ((), (), s32[]{:S(2)}) async-start(), calls=%async_computation.4 | async-start | bytes 8650752 | tf_op jit(solution)/shard_map/reduce_scatter | solution.py:189
Sparse Core Ops, SparseCore 0:
  19.4 27.1 all-gather.9
  62.1 32.1 all-gather.5
  140.8 51.5 all-gather.7
  218.4 92.4 reduce-scatter.1

commit v5 on v4

--- a/solution.py
+++ b/solution.py
@@ -8,6 +8,68 @@
 BLOCK = 128
 LANES = 128
 ROWS_PER_LOAD = 16
+
+EXPERT_TILE = 2048
+
+
+def _expert_kernel(nk, rows_ref, gate_ref, up_ref, down_ref, out_ref, acc_g, acc_u, active):
+    i = pl.program_id(0)
+
+    @pl.when(i == 0)
+    def _():
+        acc_g[...] = jnp.zeros_like(acc_g)
+        acc_u[...] = jnp.zeros_like(acc_u)
+
+    @pl.when(i < nk)
+    def _():
+        x = rows_ref[...]
+        acc_g[...] += jnp.dot(x, gate_ref[...], preferred_element_type=jnp.float32)
+        acc_u[...] += jnp.dot(x, up_ref[...], preferred_element_type=jnp.float32)
+
+    @pl.when(i == nk - 1)
+    def _():
+        g = acc_g[...]
+        active[...] = (g * jax.nn.sigmoid(g) * acc_u[...]).astype(active.dtype)
+
+    @pl.when(i >= nk)
+    def _():
+        out_ref[...] = jnp.dot(active[...], down_ref[...], preferred_element_type=jnp.float32).astype(
+            out_ref.dtype
+        )
+
+
+def expert_partial(inputs, gate_weight, up_weight, down_weight):
+    slots, width = inputs.shape
+    hidden = gate_weight.shape[1]
+    tile = EXPERT_TILE
+    nk, nn = width // tile, down_weight.shape[1] // tile
+    k_of = lambda i: jnp.minimum(i, nk - 1)
+    n_of = lambda i: jnp.maximum(i - nk, 0)
+    return pl.pallas_call(
+        lambda *refs: _expert_kernel(nk, *refs),
+        grid=(nk + nn,),
+        in_specs=[
+            pl.BlockSpec((slots, tile), lambda i: (0, k_of(i))),
+            pl.BlockSpec((tile, hidden), lambda i: (k_of(i), 0)),
+            pl.BlockSpec((tile, hidden), lambda i: (k_of(i), 0)),
+            pl.BlockSpec((hidden, tile), lambda i: (0, n_of(i))),
+        ],
+        out_specs=pl.BlockSpec((slots, tile), lambda i: (0, n_of(i))),
+        out_shape=jax.ShapeDtypeStruct((slots, down_weight.shape[1]), jnp.bfloat16),
+        scratch_shapes=[
+            pltpu.VMEM((slots, hidden), jnp.float32),
+            pltpu.VMEM((slots, hidden), jnp.float32),
+            pltpu.VMEM((slots, hidden), jnp.bfloat16),
+        ],
+        compiler_params=pltpu.CompilerParams(
+            dimension_semantics=("arbitrary",), vmem_limit_bytes=48 * 1024 * 1024
+        ),
+        cost_estimate=pl.CostEstimate(
+            flops=6 * slots * width * hidden,
+            transcendentals=slots * hidden,
+            bytes_accessed=2 * (2 * slots * width + 3 * width * hidden),
+        ),
+    )(inputs, gate_weight, up_weight, down_weight)
 
 
 def _lane_tile(col, width):
@@ -183,11 +245,8 @@
     ).astype(jnp.bfloat16)
     send_rows = jnp.dot(table, restored, preferred_element_type=jnp.float32).astype(jnp.bfloat16)
     inputs = lax.all_gather(send_rows, ("seq", "expert"), axis=0, tiled=True)
-    gate_value = jnp.dot(inputs, gate_weight, preferred_element_type=jnp.float32)
-    up_value = jnp.dot(inputs, up_weight, preferred_element_type=jnp.float32)
-    active = (jax.nn.silu(gate_value) * up_value).astype(jnp.bfloat16)
     own_sum = lax.psum_scatter(
-        jnp.dot(active, down_weight, preferred_element_type=jnp.float32).astype(jnp.bfloat16),
+        expert_partial(inputs, gate_weight, up_weight, down_weight),
         ("seq", "expert"),
         scatter_dimension=0,
         tiled=True,

time: 320 us -> 315 us (0.984)
  matrix products: 38.4 us -> 12.5 us
  Pallas kernels: 17.1 us -> 37.6 us
    dot_general x2 -> x0, matrix products: 25.9 us -> none  [the longest x1 17.1 us: on_device(): jnp.dot(active, down_weight, preferred_element_type=jnp.float32)]
    pallas_call x0 -> x1, Pallas kernels: none -> 20.4 us  [expert_partial(): pl.pallas_call(lambda *refs: _expert_kernel(nk, *refs), grid=(nk + nn,),...]
where the time goes in v5:
time: 315 us; the launch traced here: 314 us
  waiting for transfers between devices  231 us (73%)
  Pallas kernels  37.6 us (12%)
  between operations  13.3 us (4%)
  matrix products  12.5 us (4%)
  other arithmetic  9.24 us (3%)
  starting transfers between devices  6.24 us (2%)
  local copies, waits for them, and re-layouts  4.61 us (1%)
    reduce_scatter x1, waiting for transfers between devices, on_device(): lax.psum_scatter(expert_partial(inputs, gate_weight, up_weight, down_weig...  92.3 us
    all_gather x1, waiting for transfers between devices, on_device(): inputs = lax.all_gather(send_rows, ('seq', 'expert'), axis=0, tiled=True)  51.5 us
    all_gather x1, waiting for transfers between devices, on_device(): gathered = lax.all_gather(gated, 'seq', axis=0, tiled=True)  32.3 us
    all_to_all x1, waiting for transfers between devices, on_device(): lax.all_to_all(column_part, ('seq', 'expert'), split_axis=0, concat_axis=...  27.3 us
    all_gather x1, waiting for transfers between devices, entering_state(): lax.all_gather(jnp.concatenate([state_end, step_total[None, :]], axis=0),...  27.1 us
    pallas_call x1, Pallas kernels, expert_partial(): pl.pallas_call(lambda *refs: _expert_kernel(nk, *refs), grid=(nk + nn,),...  20.4 us
    pallas_call x1, Pallas kernels, scan_gated(): pl.pallas_call(_out_kernel, grid=grid, in_specs=[pl.BlockSpec((states, wi...  10.9 us
    dot_general x1, matrix products, on_device(): jnp.dot(gathered, out_proj, preferred_element_type=jnp.float32)  9.28 us
  transfers between devices with their start and end apart: 5, of which 5 were waited for; matrix products, arithmetic and copies ran while one was open for 0% of the time, Pallas kernels for 0%

profile of v5, /device:TPU:0, one launch (start us, length us, event | category | flops | bytes accessed | tf_op | source)
XLA Modules:
  0.0 314.1 jit_solution(11360546840826465491)
XLA Ops:
  6.5 0.7 convert_bitcast_fusion.1
  7.4 2.7 compare_select_fusion
  10.0 1.3 broadcast_in_dim.21.b_ref
  11.4 6.3 %shard_map.154 = f32[16,2048]{1,0:T(8,128)} custom-call(f32[128,2048]{1,0:T(8,128)} %get-tuple-element.16.step_ref, bf16[128,2048]{1,0:T(8,128)(2,1)} %x_ref.3, f32[16,2048]{1,0:T(8,128)} %decay_ref.3, f32[128,16,128]{2,1,0:T(8,128)} %broadcast_in_dim.21.b_ref), custom_call_target="tpu_custom_call" | custom-call | flops 25165824 | bytes 1835008 | tf_op jit(solution)/shard_map/pallas_call | solution.py:129
  17.7 1.6 maximum_bitcast_fusion
  19.5 27.1 %all-gather.10.cloned.1.call-done = f32[8,17,2048]{2,1,0:T(8,128)} async-done(((f32[1,17,2048]{2,1,0:T(8,128)}), f32[8,17,2048]{2,1,0:T(8,128)}) %all-gather.10.cloned.1.call-update) | async-done | bytes 1114128 | tf_op jit(solution)/shard_map/all_gather | solution.py:175
  46.6 1.1 fusion.37
  47.6 2.1 fusion.13.state_in_ref
  49.7 1.3 broadcast_in_dim.24.c_ref
  51.1 10.9 %shard_map.155 = bf16[128,2048]{1,0:T(8,128)(2,1)} custom-call(f32[16,2048]{1,0:T(8,128)} %fusion.13.state_in_ref, f32[128,2048]{1,0:T(8,128)} %get-tuple-element.16.step_ref, bf16[128,2048]{1,0:T(8,128)(2,1)} %x_ref.3, bf16[128,2048]{1,0:T(8,128)(2,1)} %z_ref.1, f32[16,2048]{1,0:T(8,128)} %decay_ref.3, f32[128,16,128]{2,1,0:T(8,128)} %broadcast_in_dim.21.b_ref, ...), custom_call_target="tpu_custom_call" | custom-call | flops 37748736 | bytes 2883584 | tf_op jit(solution)/shard_map/pallas_call | solution.py:151
  62.0 32.3 %all-gather.6.cloned.1.call-done = bf16[1024,2048]{1,0:T(8,128)(2,1)} async-done(((bf16[128,2048]{1,0:T(8,128)(2,1)}), bf16[1024,2048]{1,0:T(8,128)(2,1)}) %all-gather.6.cloned.1.call-update) | async-done | bytes 4194320 | tf_op jit(solution)/shard_map/all_gather | solution.py:209
  94.3 9.3 %convolution_convert_fusion.1 = bf16[1024,1024]{1,0:T(8,128)(2,1)} fusion(bf16[1024,2048]{1,0:T(8,128)(2,1)} %all-gather.6.cloned.1.call-done, bf16[2048,1024]{1,0:T(8,128)(2,1)} %param.24), kind=kOutput, calls=%fused_computation.6 | convolution fusion | flops 4296015872 | bytes 10485760 | tf_op jit(solution)/shard_map/dot_general | solution.py:210
  103.6 5.9 %all-to-all-start = ((bf16[32,32,1024]{2,1,0:T(8,128)(2,1)}), bf16[32,32,1024]{2,1,0:T(8,128)(2,1)S(1)}, u32[]{:S(2)}, u32[]{:S(2)}) async-start(bf16[32,32,1024]{2,1,0:T(8,128)(2,1)} %bitcast.99), calls=%async_computation | async-start | bytes 4194304 | tf_op jit(solution)/shard_map/all_to_all | solution.py:212
  109.9 27.3 %all-to-all-done = bf16[32,32,1024]{2,1,0:T(8,128)(2,1)S(1)} async-done(((bf16[32,32,1024]{2,1,0:T(8,128)(2,1)}), bf16[32,32,1024]{2,1,0:T(8,128)(2,1)S(1)}, u32[]{:S(2)}, u32[]{:S(2)}) %all-to-all-start) | async-done | bytes 2097184 | tf_op jit(solution)/shard_map/all_to_all | solution.py:212
  137.2 0.4 convert_reduce_fusion
  137.7 0.3 fusion.5
  138.4 0.3 reduce_max.9
  138.8 0.3 div.38
  139.1 0.7 fusion.11
  139.8 0.9 convolution_convert_fusion
  140.9 51.5 %all-gather.8.cloned.1.call-done.refs_0_ = bf16[512,8192]{1,0:T(8,128)(2,1)} async-done(((bf16[16,8192]{1,0:T(8,128)(2,1)}), bf16[512,8192]{1,0:T(8,128)(2,1)}) %all-gather.8.cloned.1.call-update) | async-done | bytes 8388624 | tf_op jit(solution)/shard_map/all_gather | solution.py:247
  192.4 20.4 %shard_map.156 = bf16[512,8192]{1,0:T(8,128)(2,1)} custom-call(bf16[512,8192]{1,0:T(8,128)(2,1)} %all-gather.8.cloned.1.call-done.refs_0_, bf16[8192,384]{1,0:T(8,128)(2,1)} %refs_1_.1, bf16[8192,384]{1,0:T(8,128)(2,1)} %refs_2_.1, bf16[384,8192]{1,0:T(8,128)(2,1)} %refs_3_.1), custom_call_target="tpu_custom_call" | custom-call | flops 9663676416 | bytes 35651584 | tf_op jit(solution)/shard_map/pallas_call | solution.py:48
  213.2 92.3 %reduce-scatter.2.cloned.1.call-done = bf16[16,8192]{1,0:T(8,128)(2,1)} async-done(((bf16[512,8192]{1,0:T(8,128)(2,1)}), bf16[16,8192]{1,0:T(8,128)(2,1)}) %reduce-scatter.2.cloned.1.call-update) | async-done | bytes 262160 | tf_op jit(solution)/shard_map/reduce_scatter | solution.py:248
  305.5 2.1 fusion.1
  (37 shorter events, 1.7 us)
Async XLA Ops:
  6.5 206.3 %copy-start = (bf16[8192,16]{0,1:T(8,128)(2,1)S(1)}, bf16[8192,16]{0,1:T(8,128)(2,1)}, u32[]{:S(2)}) copy-start(bf16[8192,16]{0,1:T(8,128)(2,1)} %param.27) | copy-start | bytes 786436
  6.5 40.0 %all-gather.10.cloned.1.call-start = ((), (), s32[]{:S(2)}) async-start(), calls=%async_computation.5 | async-start | bytes 1769472 | tf_op jit(solution)/shard_map/all_gather | solution.py:175
  11.4 8.0 %copy-start.4 = (bf16[16,128]{1,0:T(8,128)(2,1)S(1)}, bf16[16,128]{1,0:T(8,128)(2,1)}, u32[]{:S(2)}) copy-start(bf16[16,128]{1,0:T(8,128)(2,1)} %param.22) | copy-start | bytes 12292
  11.4 36.3 %copy-start.3 = (f32[16,2048]{1,0:T(8,128)S(1)}, f32[16,2048]{1,0:T(8,128)}, u32[]{:S(2)}) copy-start(f32[16,2048]{1,0:T(8,128)} %decay_ref.3) | copy-start | bytes 393220
  19.3 75.0 %all-gather.6.cloned.1.call-start = ((), (), s32[]{:S(2)}) async-start(), calls=%async_computation.2 | async-start | bytes 4718592 | tf_op jit(solution)/shard_map/all_gather | solution.py:209
  103.6 6.0 %copy-start.5 = (s32[32,2]{0,1:T(2,128)S(1)}, s32[32,2]{0,1:T(2,128)}, u32[]{:S(2)}) copy-start(s32[32,2]{0,1:T(2,128)} %param.28) | copy-start | bytes 772
  103.6 34.1 %copy-start.1 = (bf16[32,8192]{1,0:T(8,128)(2,1)S(1)}, bf16[32,8192]{1,0:T(8,128)(2,1)}, u32[]{:S(2)}) copy-start(bf16[32,8192]{1,0:T(8,128)(2,1)} %param.25) | copy-start | bytes 1572868
  103.6 33.6 %all-to-all-start = ((bf16[32,32,1024]{2,1,0:T(8,128)(2,1)}), bf16[32,32,1024]{2,1,0:T(8,128)(2,1)S(1)}, u32[]{:S(2)}, u32[]{:S(2)}) async-start(bf16[32,32,1024]{2,1,0:T(8,128)(2,1)} %bitcast.99), calls=%async_computation | async-start | bytes 4194304 | tf_op jit(solution)/shard_map/all_to_all | solution.py:212
  109.5 28.5 %copy-start.2 = (f32[8192]{0:T(1024)S(1)}, f32[8192]{0:T(1024)}, u32[]{:S(2)}) copy-start(f32[8192]{0:T(1024)} %param.26) | copy-start | bytes 98308
  109.5 82.9 %all-gather.8.cloned.1.call-start = ((), (), s32[]{:S(2)}) async-start(), calls=%async_computation.3 | async-start | bytes 8650752 | tf_op jit(solution)/shard_map/all_gather | solution.py:247
  140.7 164.8 %reduce-scatter.2.cloned.1.call-start = ((), (), s32[]{:S(2)}) async-start(), calls=%async_computation.4 | async-start | bytes 8650752 | tf_op jit(solution)/shard_map/reduce_scatter | solution.py:248
Sparse Core Ops, SparseCore 0:
  19.4 27.1 all-gather.9
  62.1 32.1 all-gather.5
  140.8 51.5 all-gather.7
  213.0 92.4 reduce-scatter.1

commit v6 on v5

--- a/solution.py
+++ b/solution.py
@@ -78,6 +78,7 @@
 
 def _end_kernel(step_ref, x_ref, decay_ref, b_ref, state_ref):
     steps, width = step_ref.shape
+    states = decay_ref.shape[0]
     rate = decay_ref[...]
 
     def body(k, state):
@@ -91,13 +92,24 @@
         return state
 
     zero = jnp.zeros(rate.shape, jnp.float32)
-    state_ref[...] = lax.fori_loop(0, steps // ROWS_PER_LOAD, body, zero)
-
-
-def _out_kernel(state_in_ref, step_ref, x_ref, z_ref, decay_ref, b_ref, c_ref, skip_ref, gated_ref, y_ref):
+    state_ref[:states] = lax.fori_loop(0, steps // ROWS_PER_LOAD, body, zero)
+    state_ref[states:] = jnp.sum(step_ref[...], axis=0, keepdims=True)
+
+
+def _out_kernel(
+    mine_ref, stacked_ref, step_ref, x_ref, z_ref, decay_ref, b_ref, c_ref, skip_ref, gated_ref, y_ref
+):
     steps, width = step_ref.shape
+    states = decay_ref.shape[0]
     rate = decay_ref[...]
     skip = skip_ref[...]
+    mine = mine_ref[0]
+
+    running = jnp.zeros(rate.shape, jnp.float32)
+    for position in range(stacked_ref.shape[0] - 1):
+        piece = stacked_ref[position]
+        longer = jnp.exp(-rate * piece[states:]) * running + piece[:states]
+        running = jnp.where(position < mine, longer, running)
 
     def body(k, state):
         base = pl.multiple_of(k * ROWS_PER_LOAD, ROWS_PER_LOAD)
@@ -112,53 +124,57 @@
             y_ref[pl.ds(base + i, 1), :] = jnp.sum(c_now * state, axis=0, keepdims=True) + skip * x_now
         return state
 
-    lax.fori_loop(0, steps // ROWS_PER_LOAD, body, state_in_ref[...])
+    lax.fori_loop(0, steps // ROWS_PER_LOAD, body, running)
     z = z_ref[...].astype(jnp.float32)
     gated_ref[...] = (y_ref[...] * (z * jax.nn.sigmoid(z))).astype(gated_ref.dtype)
 
 
-def _columns(b_coef):
-    rows = b_coef.astype(jnp.float32).T
-    return jnp.broadcast_to(rows[:, :, None], rows.shape + (LANES,))
-
-
-def scan_end(step_size, x_in, decay_rate, b_coef, width=512):
+def _columns(b_coef, c_coef):
+    rows = jnp.transpose(jnp.stack([b_coef, c_coef]).astype(jnp.float32), (0, 2, 1))
+    return jnp.broadcast_to(rows[..., None], rows.shape + (LANES,))
+
+
+def _coef_spec(steps, states, which):
+    return pl.BlockSpec((None, steps, states, LANES), lambda j: (which, 0, 0, 0))
+
+
+def scan_end(step_size, x_in, decay_rate, columns, width=512):
     steps, chans = step_size.shape
     states = decay_rate.shape[0]
-    grid = (chans // width,)
     return pl.pallas_call(
         _end_kernel,
-        grid=grid,
+        grid=(chans // width,),
         in_specs=[
             pl.BlockSpec((steps, width), lambda j: (0, j)),
             pl.BlockSpec((steps, width), lambda j: (0, j)),
             pl.BlockSpec((states, width), lambda j: (0, j)),
-            pl.BlockSpec((steps, states, LANES), lambda j: (0, 0, 0)),
-        ],
-        out_specs=pl.BlockSpec((states, width), lambda j: (0, j)),
-        out_shape=jax.ShapeDtypeStruct((states, chans), jnp.float32),
+            _coef_spec(steps, states, 0),
+        ],
+        out_specs=pl.BlockSpec((states + 1, width), lambda j: (0, j)),
+        out_shape=jax.ShapeDtypeStruct((states + 1, chans), jnp.float32),
         cost_estimate=pl.CostEstimate(
             flops=6 * steps * states * chans, transcendentals=steps * states * chans,
             bytes_accessed=steps * chans * 6 + states * chans * 8),
-    )(step_size, x_in, decay_rate, _columns(b_coef))
-
-
-def scan_gated(state_in, step_size, x_in, z_in, decay_rate, b_coef, c_coef, skip_gain, width=512):
+    )(step_size, x_in, decay_rate, columns)
+
+
+def scan_gated(mine, stacked, step_size, x_in, z_in, decay_rate, columns, skip_gain, width=512):
     steps, chans = step_size.shape
     states = decay_rate.shape[0]
-    grid = (chans // width,)
+    count = stacked.shape[0]
     col = lambda j: (0, j)
     return pl.pallas_call(
         _out_kernel,
-        grid=grid,
+        grid=(chans // width,),
         in_specs=[
-            pl.BlockSpec((states, width), col),
+            pl.BlockSpec(memory_space=pltpu.SMEM),
+            pl.BlockSpec((count, states + 1, width), lambda j: (0, 0, j)),
             pl.BlockSpec((steps, width), col),
             pl.BlockSpec((steps, width), col),
             pl.BlockSpec((steps, width), col),
             pl.BlockSpec((states, width), col),
-            pl.BlockSpec((steps, states, LANES), lambda j: (0, 0, 0)),
-            pl.BlockSpec((steps, states, LANES), lambda j: (0, 0, 0)),
+            _coef_spec(steps, states, 0),
+            _coef_spec(steps, states, 1),
             pl.BlockSpec((1, width), col),
         ],
         out_specs=pl.BlockSpec((steps, width), col),
@@ -166,19 +182,8 @@
         scratch_shapes=[pltpu.VMEM((steps, width), jnp.float32)],
         cost_estimate=pl.CostEstimate(
             flops=9 * steps * states * chans, transcendentals=steps * states * chans + steps * chans,
-            bytes_accessed=steps * chans * 10 + states * chans * 8),
-    )(state_in, step_size, x_in, z_in, decay_rate, _columns(b_coef), _columns(c_coef), skip_gain[None, :])
-
-
-def entering_state(state_end, step_total, decay_rate, axis):
-    count, mine = (lax.axis_size(axis), lax.axis_index(axis))
-    stacked = lax.all_gather(jnp.concatenate([state_end, step_total[None, :]], axis=0), axis)
-    running = jnp.zeros_like(state_end)
-    for position in range(count - 1):
-        decay_then = jnp.exp(-decay_rate * stacked[position, -1][None, :])
-        longer = decay_then * running + stacked[position, :-1]
-        running = jnp.where(position < mine, longer, running)
-    return running
+            bytes_accessed=steps * chans * 10 + count * states * chans * 4),
+    )(mine, stacked, step_size, x_in, z_in, decay_rate, columns, columns, skip_gain[None, :])
 
 
 def on_device(
@@ -200,9 +205,11 @@
     down_weight,
 ):
     step_size = jax.nn.softplus(step_raw.astype(jnp.float32) + step_bias[None, :])
-    state_end = scan_end(step_size, x_in, decay_rate, b_coef)
-    state_in = entering_state(state_end, jnp.sum(step_size, axis=0), decay_rate, "seq")
-    gated = scan_gated(state_in, step_size, x_in, z_in, decay_rate, b_coef, c_coef, skip_gain)
+    columns = _columns(b_coef, c_coef)
+    state_end = scan_end(step_size, x_in, decay_rate, columns)
+    stacked = lax.all_gather(state_end, "seq")
+    mine = lax.axis_index("seq").astype(jnp.int32).reshape(1)
+    gated = scan_gated(mine, stacked, step_size, x_in, z_in, decay_rate, columns, skip_gain)
     seq_count = lax.axis_size("seq")
     expert_count = lax.axis_size("expert")
     rows = residual.shape[0]

time: 315 us -> 309 us (0.981)
  other arithmetic: 9.24 us -> 5.54 us
where the time goes in v6:
time: 309 us
  waiting for transfers between devices  231 us (75%)
  Pallas kernels  38 us (12%)
  between operations  13.2 us (4%)
  matrix products  12.6 us (4%)
  starting transfers between devices  6.05 us (2%)
  other arithmetic  5.54 us (2%)
    reduce_scatter x1, waiting for transfers between devices, on_device(): lax.psum_scatter(expert_partial(inputs, gate_weight, up_weight, down_weig...  92.3 us
    all_gather x1, waiting for transfers between devices, on_device(): inputs = lax.all_gather(send_rows, ('seq', 'expert'), axis=0, tiled=True)  51.6 us
    all_gather x1, waiting for transfers between devices, on_device(): gathered = lax.all_gather(gated, 'seq', axis=0, tiled=True)  32.3 us
    all_to_all x1, waiting for transfers between devices, on_device(): lax.all_to_all(column_part, ('seq', 'expert'), split_axis=0, concat_axis=...  27.3 us
    all_gather x1, waiting for transfers between devices, on_device(): stacked = lax.all_gather(state_end, 'seq')  27.2 us
    pallas_call x1, Pallas kernels, expert_partial(): pl.pallas_call(lambda *refs: _expert_kernel(nk, *refs), grid=(nk + nn,),...  20.4 us
    pallas_call x1, Pallas kernels, scan_gated(): pl.pallas_call(_out_kernel, grid=(chans // width,), in_specs=[pl.BlockSpe...  11.2 us
    dot_general x1, matrix products, on_device(): jnp.dot(gathered, out_proj, preferred_element_type=jnp.float32)  9.28 us
  transfers between devices with their start and end apart: 5, of which 5 were waited for; matrix products, arithmetic and copies ran while one was open for 0% of the time, Pallas kernels for 0%

profile of v6, /device:TPU:0, one launch (start us, length us, event | category | flops | bytes accessed | tf_op | source)
XLA Modules:
  0.0 308.9 jit_solution(2598727403829445109)
XLA Ops:
  6.5 0.7 convert_bitcast_fusion
  7.4 2.6 compare_select_fusion.step_ref
  10.0 2.0 broadcast_in_dim.15.b_ref.c_ref
  12.0 6.4 %shard_map.154 = f32[17,2048]{1,0:T(8,128)} custom-call(f32[128,2048]{1,0:T(8,128)} %compare_select_fusion.step_ref, bf16[128,2048]{1,0:T(8,128)(2,1)} %x_ref.3, f32[16,2048]{1,0:T(8,128)} %decay_ref.3, f32[2,128,16,128]{3,2,1,0:T(8,128)} %broadcast_in_dim.15.b_ref.c_ref), custom_call_target="tpu_custom_call" | custom-call | flops 25165824 | bytes 1835008 | tf_op jit(solution)/shard_map/pallas_call | solution.py:144
  18.4 27.2 %all-gather.10.cloned.1.call-done.stacked_ref = f32[8,17,2048]{2,1,0:T(8,128)} async-done(((f32[1,17,2048]{2,1,0:T(8,128)}), f32[8,17,2048]{2,1,0:T(8,128)}) %all-gather.10.cloned.1.call-update) | async-done | bytes 1114128 | tf_op jit(solution)/shard_map/all_gather | solution.py:210
  45.6 11.2 %shard_map.155 = bf16[128,2048]{1,0:T(8,128)(2,1)} custom-call(s32[1]{0:T(128)} %bitcast.mine_ref, f32[8,17,2048]{2,1,0:T(8,128)} %all-gather.10.cloned.1.call-done.stacked_ref, f32[128,2048]{1,0:T(8,128)} %compare_select_fusion.step_ref, bf16[128,2048]{1,0:T(8,128)(2,1)} %x_ref.3, bf16[128,2048]{1,0:T(8,128)(2,1)} %z_ref.1, f32[16,2048]{1,0:T(8,128)} %decay_ref.3, ...), custom_call_target="tpu_custom_call" | custom-call | flops 37748736 | bytes 3670016 | tf_op jit(solution)/shard_map/pallas_call | solution.py:166
  56.9 32.3 %all-gather.6.cloned.1.call-done = bf16[1024,2048]{1,0:T(8,128)(2,1)} async-done(((bf16[128,2048]{1,0:T(8,128)(2,1)}), bf16[1024,2048]{1,0:T(8,128)(2,1)}) %all-gather.6.cloned.1.call-update) | async-done | bytes 4194320 | tf_op jit(solution)/shard_map/all_gather | solution.py:216
  89.2 9.3 %convolution_convert_fusion.1 = bf16[1024,1024]{1,0:T(8,128)(2,1)} fusion(bf16[1024,2048]{1,0:T(8,128)(2,1)} %all-gather.6.cloned.1.call-done, bf16[2048,1024]{1,0:T(8,128)(2,1)} %param.24), kind=kOutput, calls=%fused_computation.6 | convolution fusion | flops 4296015872 | bytes 10485760 | tf_op jit(solution)/shard_map/dot_general | solution.py:217
  98.4 5.9 %all-to-all-start = ((bf16[32,32,1024]{2,1,0:T(8,128)(2,1)}), bf16[32,32,1024]{2,1,0:T(8,128)(2,1)S(1)}, u32[]{:S(2)}, u32[]{:S(2)}) async-start(bf16[32,32,1024]{2,1,0:T(8,128)(2,1)} %bitcast.37), calls=%async_computation | async-start | bytes 4194304 | tf_op jit(solution)/shard_map/all_to_all | solution.py:219
  104.6 0.1 reduce.1
  104.8 27.3 %all-to-all-done = bf16[32,32,1024]{2,1,0:T(8,128)(2,1)S(1)} async-done(((bf16[32,32,1024]{2,1,0:T(8,128)(2,1)}), bf16[32,32,1024]{2,1,0:T(8,128)(2,1)S(1)}, u32[]{:S(2)}, u32[]{:S(2)}) %all-to-all-start) | async-done | bytes 2097184 | tf_op jit(solution)/shard_map/all_to_all | solution.py:219
  132.1 0.4 convert_reduce_fusion
  132.6 0.3 fusion.5
  132.9 0.2 fusion.9
  133.1 0.2 copy.34
  133.3 0.3 reduce_max.9
  133.6 0.3 div.38
  134.0 0.7 fusion.11
  134.6 0.9 convolution_convert_fusion
  135.6 51.6 %all-gather.8.cloned.1.call-done.refs_0_ = bf16[512,8192]{1,0:T(8,128)(2,1)} async-done(((bf16[16,8192]{1,0:T(8,128)(2,1)}), bf16[512,8192]{1,0:T(8,128)(2,1)}) %all-gather.8.cloned.1.call-update) | async-done | bytes 8388624 | tf_op jit(solution)/shard_map/all_gather | solution.py:254
  187.3 20.4 %shard_map.156 = bf16[512,8192]{1,0:T(8,128)(2,1)} custom-call(bf16[512,8192]{1,0:T(8,128)(2,1)} %all-gather.8.cloned.1.call-done.refs_0_, bf16[8192,384]{1,0:T(8,128)(2,1)} %refs_1_.1, bf16[8192,384]{1,0:T(8,128)(2,1)} %refs_2_.1, bf16[384,8192]{1,0:T(8,128)(2,1)} %refs_3_.1), custom_call_target="tpu_custom_call" | custom-call | flops 9663676416 | bytes 35651584 | tf_op jit(solution)/shard_map/pallas_call | solution.py:48
  207.7 0.3 fusion.4
  208.1 92.3 %reduce-scatter.2.cloned.1.call-done = bf16[16,8192]{1,0:T(8,128)(2,1)} async-done(((bf16[512,8192]{1,0:T(8,128)(2,1)}), bf16[16,8192]{1,0:T(8,128)(2,1)}) %reduce-scatter.2.cloned.1.call-update) | async-done | bytes 262160 | tf_op jit(solution)/shard_map/reduce_scatter | solution.py:255
  300.3 2.1 fusion.1
  (27 shorter events, 0.6 us)
Async XLA Ops:
  6.5 201.2 %copy-start = (bf16[8192,16]{0,1:T(8,128)(2,1)S(1)}, bf16[8192,16]{0,1:T(8,128)(2,1)}, u32[]{:S(2)}) copy-start(bf16[8192,16]{0,1:T(8,128)(2,1)} %param.27) | copy-start | bytes 786436
  6.5 39.1 %all-gather.10.cloned.1.call-start = ((), (), s32[]{:S(2)}) async-start(), calls=%async_computation.5 | async-start | bytes 1769472 | tf_op jit(solution)/shard_map/all_gather | solution.py:210
  18.3 70.8 %all-gather.6.cloned.1.call-start = ((), (), s32[]{:S(2)}) async-start(), calls=%async_computation.2 | async-start | bytes 4718592 | tf_op jit(solution)/shard_map/all_gather | solution.py:216
  98.4 6.0 %copy-start.3 = (s32[32,2]{0,1:T(2,128)S(1)}, s32[32,2]{0,1:T(2,128)}, u32[]{:S(2)}) copy-start(s32[32,2]{0,1:T(2,128)} %param.28) | copy-start | bytes 772
  98.4 34.1 %copy-start.1 = (bf16[32,8192]{1,0:T(8,128)(2,1)S(1)}, bf16[32,8192]{1,0:T(8,128)(2,1)}, u32[]{:S(2)}) copy-start(bf16[32,8192]{1,0:T(8,128)(2,1)} %param.25) | copy-start | bytes 1572868
  98.4 33.6 %all-to-all-start = ((bf16[32,32,1024]{2,1,0:T(8,128)(2,1)}), bf16[32,32,1024]{2,1,0:T(8,128)(2,1)S(1)}, u32[]{:S(2)}, u32[]{:S(2)}) async-start(bf16[32,32,1024]{2,1,0:T(8,128)(2,1)} %bitcast.37), calls=%async_computation | async-start | bytes 4194304 | tf_op jit(solution)/shard_map/all_to_all | solution.py:219
  104.4 28.5 %copy-start.2 = (f32[8192]{0:T(1024)S(1)}, f32[8192]{0:T(1024)}, u32[]{:S(2)}) copy-start(f32[8192]{0:T(1024)} %param.26) | copy-start | bytes 98308
  104.4 82.9 %all-gather.8.cloned.1.call-start = ((), (), s32[]{:S(2)}) async-start(), calls=%async_computation.3 | async-start | bytes 8650752 | tf_op jit(solution)/shard_map/all_gather | solution.py:254
  135.6 164.8 %reduce-scatter.2.cloned.1.call-start = ((), (), s32[]{:S(2)}) async-start(), calls=%async_computation.4 | async-start | bytes 8650752 | tf_op jit(solution)/shard_map/reduce_scatter | solution.py:255
Sparse Core Ops, SparseCore 0:
  18.5 27.1 all-gather.9
  57.0 32.1 all-gather.5
  135.7 51.5 all-gather.7
  207.8 92.4 reduce-scatter.1

commit v7 on v6

--- a/solution.py
+++ b/solution.py
@@ -76,30 +76,37 @@
     return jnp.concatenate([col] * (width // LANES), axis=1) if width > LANES else col
 
 
-def _end_kernel(step_ref, x_ref, decay_ref, b_ref, state_ref):
-    steps, width = step_ref.shape
+def _step_rows(raw_ref, bias_ref, base):
+    raw = raw_ref[pl.ds(base, ROWS_PER_LOAD), :].astype(jnp.float32)
+    return jax.nn.softplus(raw + bias_ref[...])
+
+
+def _end_kernel(raw_ref, bias_ref, x_ref, decay_ref, b_ref, state_ref):
+    steps, width = raw_ref.shape
     states = decay_ref.shape[0]
     rate = decay_ref[...]
 
-    def body(k, state):
+    def body(k, carry):
+        state, total = carry
         base = pl.multiple_of(k * ROWS_PER_LOAD, ROWS_PER_LOAD)
-        s_blk = step_ref[pl.ds(base, ROWS_PER_LOAD), :]
+        s_blk = _step_rows(raw_ref, bias_ref, base)
         x_blk = x_ref[pl.ds(base, ROWS_PER_LOAD), :].astype(jnp.float32)
         for i in range(ROWS_PER_LOAD):
             s_now = s_blk[i : i + 1]
             b_now = _lane_tile(b_ref[base + i], width)
             state = jnp.exp(-s_now * rate) * state + (s_now * x_blk[i : i + 1]) * b_now
-        return state
-
-    zero = jnp.zeros(rate.shape, jnp.float32)
-    state_ref[:states] = lax.fori_loop(0, steps // ROWS_PER_LOAD, body, zero)
-    state_ref[states:] = jnp.sum(step_ref[...], axis=0, keepdims=True)
+        return state, total + jnp.sum(s_blk, axis=0, keepdims=True)
+
+    zero = (jnp.zeros(rate.shape, jnp.float32), jnp.zeros((1, width), jnp.float32))
+    state, total = lax.fori_loop(0, steps // ROWS_PER_LOAD, body, zero)
+    state_ref[:states] = state
+    state_ref[states:] = total
 
 
 def _out_kernel(
-    mine_ref, stacked_ref, step_ref, x_ref, z_ref, decay_ref, b_ref, c_ref, skip_ref, gated_ref, y_ref
+    mine_ref, stacked_ref, raw_ref, bias_ref, x_ref, z_ref, decay_ref, b_ref, c_ref, skip_ref, gated_ref, y_ref
 ):
-    steps, width = step_ref.shape
+    steps, width = raw_ref.shape
     states = decay_ref.shape[0]
     rate = decay_ref[...]
     skip = skip_ref[...]
@@ -113,7 +120,7 @@
 
     def body(k, state):
         base = pl.multiple_of(k * ROWS_PER_LOAD, ROWS_PER_LOAD)
-        s_blk = step_ref[pl.ds(base, ROWS_PER_LOAD), :]
+        s_blk = _step_rows(raw_ref, bias_ref, base)
         x_blk = x_ref[pl.ds(base, ROWS_PER_LOAD), :].astype(jnp.float32)
         for i in range(ROWS_PER_LOAD):
             s_now = s_blk[i : i + 1]
@@ -138,14 +145,15 @@
     return pl.BlockSpec((None, steps, states, LANES), lambda j: (which, 0, 0, 0))
 
 
-def scan_end(step_size, x_in, decay_rate, columns, width=512):
-    steps, chans = step_size.shape
+def scan_end(step_raw, step_bias, x_in, decay_rate, columns, width=512):
+    steps, chans = step_raw.shape
     states = decay_rate.shape[0]
     return pl.pallas_call(
         _end_kernel,
         grid=(chans // width,),
         in_specs=[
             pl.BlockSpec((steps, width), lambda j: (0, j)),
+            pl.BlockSpec((1, width), lambda j: (0, j)),
             pl.BlockSpec((steps, width), lambda j: (0, j)),
             pl.BlockSpec((states, width), lambda j: (0, j)),
             _coef_spec(steps, states, 0),
@@ -155,11 +163,11 @@
         cost_estimate=pl.CostEstimate(
             flops=6 * steps * states * chans, transcendentals=steps * states * chans,
             bytes_accessed=steps * chans * 6 + states * chans * 8),
-    )(step_size, x_in, decay_rate, columns)
-
-
-def scan_gated(mine, stacked, step_size, x_in, z_in, decay_rate, columns, skip_gain, width=512):
-    steps, chans = step_size.shape
+    )(step_raw, step_bias[None, :], x_in, decay_rate, columns)
+
+
+def scan_gated(mine, stacked, step_raw, step_bias, x_in, z_in, decay_rate, columns, skip_gain, width=512):
+    steps, chans = step_raw.shape
     states = decay_rate.shape[0]
     count = stacked.shape[0]
     col = lambda j: (0, j)
@@ -170,6 +178,7 @@
             pl.BlockSpec(memory_space=pltpu.SMEM),
             pl.BlockSpec((count, states + 1, width), lambda j: (0, 0, j)),
             pl.BlockSpec((steps, width), col),
+            pl.BlockSpec((1, width), col),
             pl.BlockSpec((steps, width), col),
             pl.BlockSpec((steps, width), col),
             pl.BlockSpec((states, width), col),
@@ -183,7 +192,7 @@
         cost_estimate=pl.CostEstimate(
             flops=9 * steps * states * chans, transcendentals=steps * states * chans + steps * chans,
             bytes_accessed=steps * chans * 10 + count * states * chans * 4),
-    )(mine, stacked, step_size, x_in, z_in, decay_rate, columns, columns, skip_gain[None, :])
+    )(mine, stacked, step_raw, step_bias[None, :], x_in, z_in, decay_rate, columns, columns, skip_gain[None, :])
 
 
 def on_device(
@@ -204,12 +213,11 @@
     up_weight,
     down_weight,
 ):
-    step_size = jax.nn.softplus(step_raw.astype(jnp.float32) + step_bias[None, :])
     columns = _columns(b_coef, c_coef)
-    state_end = scan_end(step_size, x_in, decay_rate, columns)
+    state_end = scan_end(step_raw, step_bias, x_in, decay_rate, columns)
     stacked = lax.all_gather(state_end, "seq")
     mine = lax.axis_index("seq").astype(jnp.int32).reshape(1)
-    gated = scan_gated(mine, stacked, step_size, x_in, z_in, decay_rate, columns, skip_gain)
+    gated = scan_gated(mine, stacked, step_raw, step_bias, x_in, z_in, decay_rate, columns, skip_gain)
     seq_count = lax.axis_size("seq")
     expert_count = lax.axis_size("expert")
     rows = residual.shape[0]

time: 309 us -> 308 us (level)
  no operation moved by 1% of the time
where the time goes in v7:
time: 308 us
  waiting for transfers between devices  231 us (75%)
  Pallas kernels  39.6 us (13%)
  between operations  13.2 us (4%)
  matrix products  12.5 us (4%)
  starting transfers between devices  6.06 us (2%)
    reduce_scatter x1, waiting for transfers between devices, on_device(): lax.psum_scatter(expert_partial(inputs, gate_weight, up_weight, down_weig...  92.3 us
    all_gather x1, waiting for transfers between devices, on_device(): inputs = lax.all_gather(send_rows, ('seq', 'expert'), axis=0, tiled=True)  51.6 us
    all_gather x1, waiting for transfers between devices, on_device(): gathered = lax.all_gather(gated, 'seq', axis=0, tiled=True)  32.3 us
    all_to_all x1, waiting for transfers between devices, on_device(): lax.all_to_all(column_part, ('seq', 'expert'), split_axis=0, concat_axis=...  27.3 us
    all_gather x1, waiting for transfers between devices, on_device(): stacked = lax.all_gather(state_end, 'seq')  27.2 us
    pallas_call x1, Pallas kernels, expert_partial(): pl.pallas_call(lambda *refs: _expert_kernel(nk, *refs), grid=(nk + nn,),...  20.4 us
    pallas_call x1, Pallas kernels, scan_gated(): pl.pallas_call(_out_kernel, grid=(chans // width,), in_specs=[pl.BlockSpe...  11.9 us
    dot_general x1, matrix products, on_device(): jnp.dot(gathered, out_proj, preferred_element_type=jnp.float32)  9.28 us
  transfers between devices with their start and end apart: 5, of which 5 were waited for; matrix products, arithmetic and copies ran while one was open for 0% of the time, Pallas kernels for 0%

profile of v7, /device:TPU:0, one launch (start us, length us, event | category | flops | bytes accessed | tf_op | source)
XLA Modules:
  0.0 307.9 jit_solution(16079272529287423249)
XLA Ops:
  6.5 0.7 convert_bitcast_fusion
  7.3 0.1 copy.30
  7.4 2.0 broadcast_in_dim.22.b_ref.c_ref
  9.3 7.2 %shard_map.154 = f32[17,2048]{1,0:T(8,128)} custom-call(bf16[128,2048]{1,0:T(8,128)(2,1)} %raw_ref.3, f32[1,2048]{1,0:T(1,128)} %bitcast.42, bf16[128,2048]{1,0:T(8,128)(2,1)} %x_ref.3, f32[16,2048]{1,0:T(8,128)} %decay_ref.3, f32[2,128,16,128]{3,2,1,0:T(8,128)} %broadcast_in_dim.22.b_ref.c_ref), custom_call_target="tpu_custom_call" | custom-call | flops 25165824 | bytes 1835008 | tf_op jit(solution)/shard_map/pallas_call | solution.py:151
  16.7 27.2 %all-gather.10.cloned.1.call-done.stacked_ref = f32[8,17,2048]{2,1,0:T(8,128)} async-done(((f32[1,17,2048]{2,1,0:T(8,128)}), f32[8,17,2048]{2,1,0:T(8,128)}) %all-gather.10.cloned.1.call-update) | async-done | bytes 1114128 | tf_op jit(solution)/shard_map/all_gather | solution.py:218
  43.9 11.9 %shard_map.155 = bf16[128,2048]{1,0:T(8,128)(2,1)} custom-call(s32[1]{0:T(128)} %bitcast.mine_ref, f32[8,17,2048]{2,1,0:T(8,128)} %all-gather.10.cloned.1.call-done.stacked_ref, bf16[128,2048]{1,0:T(8,128)(2,1)} %raw_ref.3, f32[1,2048]{1,0:T(1,128)} %bitcast.43, bf16[128,2048]{1,0:T(8,128)(2,1)} %x_ref.3, bf16[128,2048]{1,0:T(8,128)(2,1)} %z_ref.1, ...), custom_call_target="tpu_custom_call" | custom-call | flops 37748736 | bytes 3670016 | tf_op jit(solution)/shard_map/pallas_call | solution.py:174
  55.8 32.3 %all-gather.6.cloned.1.call-done = bf16[1024,2048]{1,0:T(8,128)(2,1)} async-done(((bf16[128,2048]{1,0:T(8,128)(2,1)}), bf16[1024,2048]{1,0:T(8,128)(2,1)}) %all-gather.6.cloned.1.call-update) | async-done | bytes 4194320 | tf_op jit(solution)/shard_map/all_gather | solution.py:224
  88.2 9.3 %convolution_convert_fusion.1 = bf16[1024,1024]{1,0:T(8,128)(2,1)} fusion(bf16[1024,2048]{1,0:T(8,128)(2,1)} %all-gather.6.cloned.1.call-done, bf16[2048,1024]{1,0:T(8,128)(2,1)} %param.24), kind=kOutput, calls=%fused_computation.5 | convolution fusion | flops 4296015872 | bytes 10485760 | tf_op jit(solution)/shard_map/dot_general | solution.py:225
  97.4 5.9 %all-to-all-start = ((bf16[32,32,1024]{2,1,0:T(8,128)(2,1)}), bf16[32,32,1024]{2,1,0:T(8,128)(2,1)S(1)}, u32[]{:S(2)}, u32[]{:S(2)}) async-start(bf16[32,32,1024]{2,1,0:T(8,128)(2,1)} %bitcast.38), calls=%async_computation | async-start | bytes 4194304 | tf_op jit(solution)/shard_map/all_to_all | solution.py:227
  103.6 0.1 reduce.1
  103.7 27.3 %all-to-all-done = bf16[32,32,1024]{2,1,0:T(8,128)(2,1)S(1)} async-done(((bf16[32,32,1024]{2,1,0:T(8,128)(2,1)}), bf16[32,32,1024]{2,1,0:T(8,128)(2,1)S(1)}, u32[]{:S(2)}, u32[]{:S(2)}) %all-to-all-start) | async-done | bytes 2097184 | tf_op jit(solution)/shard_map/all_to_all | solution.py:227
  131.1 0.4 convert_reduce_fusion
  131.6 0.3 fusion.5
  131.9 0.2 fusion.9
  132.1 0.2 copy.34
  132.3 0.3 reduce_max.9
  132.6 0.3 div.38
  132.9 0.7 fusion.11
  133.6 0.9 convolution_convert_fusion
  134.6 51.6 %all-gather.8.cloned.1.call-done.refs_0_ = bf16[512,8192]{1,0:T(8,128)(2,1)} async-done(((bf16[16,8192]{1,0:T(8,128)(2,1)}), bf16[512,8192]{1,0:T(8,128)(2,1)}) %all-gather.8.cloned.1.call-update) | async-done | bytes 8388624 | tf_op jit(solution)/shard_map/all_gather | solution.py:262
  186.3 20.4 %shard_map.156 = bf16[512,8192]{1,0:T(8,128)(2,1)} custom-call(bf16[512,8192]{1,0:T(8,128)(2,1)} %all-gather.8.cloned.1.call-done.refs_0_, bf16[8192,384]{1,0:T(8,128)(2,1)} %refs_1_.1, bf16[8192,384]{1,0:T(8,128)(2,1)} %refs_2_.1, bf16[384,8192]{1,0:T(8,128)(2,1)} %refs_3_.1), custom_call_target="tpu_custom_call" | custom-call | flops 9663676416 | bytes 35651584 | tf_op jit(solution)/shard_map/pallas_call | solution.py:48
  206.7 0.3 fusion.4
  207.1 92.3 %reduce-scatter.2.cloned.1.call-done = bf16[16,8192]{1,0:T(8,128)(2,1)} async-done(((bf16[512,8192]{1,0:T(8,128)(2,1)}), bf16[16,8192]{1,0:T(8,128)(2,1)}) %reduce-scatter.2.cloned.1.call-update) | async-done | bytes 262160 | tf_op jit(solution)/shard_map/reduce_scatter | solution.py:263
  299.3 2.1 fusion.1
  (26 shorter events, 0.5 us)
Async XLA Ops:
  6.5 200.2 %copy-start = (bf16[8192,16]{0,1:T(8,128)(2,1)S(1)}, bf16[8192,16]{0,1:T(8,128)(2,1)}, u32[]{:S(2)}) copy-start(bf16[8192,16]{0,1:T(8,128)(2,1)} %param.27) | copy-start | bytes 786436
  6.5 37.4 %all-gather.10.cloned.1.call-start = ((), (), s32[]{:S(2)}) async-start(), calls=%async_computation.5 | async-start | bytes 1769472 | tf_op jit(solution)/shard_map/all_gather | solution.py:218
  16.6 71.5 %all-gather.6.cloned.1.call-start = ((), (), s32[]{:S(2)}) async-start(), calls=%async_computation.2 | async-start | bytes 4718592 | tf_op jit(solution)/shard_map/all_gather | solution.py:224
  97.4 6.0 %copy-start.3 = (s32[32,2]{0,1:T(2,128)S(1)}, s32[32,2]{0,1:T(2,128)}, u32[]{:S(2)}) copy-start(s32[32,2]{0,1:T(2,128)} %param.28) | copy-start | bytes 772
  97.4 34.1 %copy-start.1 = (bf16[32,8192]{1,0:T(8,128)(2,1)S(1)}, bf16[32,8192]{1,0:T(8,128)(2,1)}, u32[]{:S(2)}) copy-start(bf16[32,8192]{1,0:T(8,128)(2,1)} %param.25) | copy-start | bytes 1572868
  97.4 33.6 %all-to-all-start = ((bf16[32,32,1024]{2,1,0:T(8,128)(2,1)}), bf16[32,32,1024]{2,1,0:T(8,128)(2,1)S(1)}, u32[]{:S(2)}, u32[]{:S(2)}) async-start(bf16[32,32,1024]{2,1,0:T(8,128)(2,1)} %bitcast.38), calls=%async_computation | async-start | bytes 4194304 | tf_op jit(solution)/shard_map/all_to_all | solution.py:227
  103.4 28.5 %copy-start.2 = (f32[8192]{0:T(1024)S(1)}, f32[8192]{0:T(1024)}, u32[]{:S(2)}) copy-start(f32[8192]{0:T(1024)} %param.26) | copy-start | bytes 98308
  103.4 82.9 %all-gather.8.cloned.1.call-start = ((), (), s32[]{:S(2)}) async-start(), calls=%async_computation.3 | async-start | bytes 8650752 | tf_op jit(solution)/shard_map/all_gather | solution.py:262
  134.6 164.8 %reduce-scatter.2.cloned.1.call-start = ((), (), s32[]{:S(2)}) async-start(), calls=%async_computation.4 | async-start | bytes 8650752 | tf_op jit(solution)/shard_map/reduce_scatter | solution.py:263
Sparse Core Ops, SparseCore 0:
  16.7 27.1 all-gather.9
  56.0 32.1 all-gather.5
  134.7 51.5 all-gather.7
  206.8 92.4 reduce-scatter.1

commit v8 on v7

--- a/solution.py
+++ b/solution.py
@@ -70,6 +70,31 @@
             bytes_accessed=2 * (2 * slots * width + 3 * width * hidden),
         ),
     )(inputs, gate_weight, up_weight, down_weight)
+
+
+def _project_kernel(x_ref, w_ref, out_ref):
+    out_ref[...] = jnp.dot(x_ref[...], w_ref[...], preferred_element_type=jnp.float32).astype(
+        out_ref.dtype
+    )
+
+
+def project(gathered, out_proj, tile=512):
+    rows, inner = gathered.shape
+    cols = out_proj.shape[1]
+    return pl.pallas_call(
+        _project_kernel,
+        grid=(rows // tile, cols // tile),
+        in_specs=[
+            pl.BlockSpec((tile, inner), lambda i, j: (i, 0)),
+            pl.BlockSpec((inner, tile), lambda i, j: (0, j)),
+        ],
+        out_specs=pl.BlockSpec((tile, tile), lambda i, j: (i, j)),
+        out_shape=jax.ShapeDtypeStruct((rows, cols), jnp.bfloat16),
+        compiler_params=pltpu.CompilerParams(dimension_semantics=("arbitrary", "arbitrary")),
+        cost_estimate=pl.CostEstimate(
+            flops=2 * rows * inner * cols, transcendentals=0,
+            bytes_accessed=2 * (rows * inner + inner * cols + rows * cols)),
+    )(gathered, out_proj)
 
 
 def _lane_tile(col, width):
@@ -222,7 +247,7 @@
     expert_count = lax.axis_size("expert")
     rows = residual.shape[0]
     gathered = lax.all_gather(gated, "seq", axis=0, tiled=True)
-    column_part = jnp.dot(gathered, out_proj, preferred_element_type=jnp.float32).astype(jnp.bfloat16)
+    column_part = project(gathered, out_proj)
     column_part = column_part.reshape(seq_count * expert_count, rows, column_part.shape[1])
     swapped = lax.all_to_all(column_part, ("seq", "expert"), split_axis=0, concat_axis=0, tiled=True)
     swapped = swapped.reshape(seq_count, expert_count, rows, column_part.shape[2])

time: 308 us -> 308 us (level)
  Pallas kernels: 39.6 us -> 49.1 us
  matrix products: 12.5 us -> 3.25 us
    pallas_call x0 -> x1, Pallas kernels: none -> 9.47 us  [project(): pl.pallas_call(_project_kernel, grid=(rows // tile, cols // tile), in_spe...]
    dot_general x1 -> x0, matrix products: 9.28 us -> none  [on_device(): jnp.dot(gathered, out_proj, preferred_element_type=jnp.float32)]
where the time goes in v8:
time: 308 us
  waiting for transfers between devices  231 us (75%)
  Pallas kernels  49.1 us (16%)
  between operations  13.2 us (4%)
  starting transfers between devices  6.06 us (2%)
  matrix products  3.25 us (1%)
    reduce_scatter x1, waiting for transfers between devices, on_device(): lax.psum_scatter(expert_partial(inputs, gate_weight, up_weight, down_weig...  92.3 us
    all_gather x1, waiting for transfers between devices, on_device(): inputs = lax.all_gather(send_rows, ('seq', 'expert'), axis=0, tiled=True)  51.6 us
    all_gather x1, waiting for transfers between devices, on_device(): gathered = lax.all_gather(gated, 'seq', axis=0, tiled=True)  32.3 us
    all_to_all x1, waiting for transfers between devices, on_device(): lax.all_to_all(column_part, ('seq', 'expert'), split_axis=0, concat_axis=...  27.3 us
    all_gather x1, waiting for transfers between devices, on_device(): stacked = lax.all_gather(state_end, 'seq')  27.2 us
    pallas_call x1, Pallas kernels, expert_partial(): pl.pallas_call(lambda *refs: _expert_kernel(nk, *refs), grid=(nk + nn,),...  20.4 us
    pallas_call x1, Pallas kernels, scan_gated(): pl.pallas_call(_out_kernel, grid=(chans // width,), in_specs=[pl.BlockSpe...  11.9 us
    pallas_call x1, Pallas kernels, project(): pl.pallas_call(_project_kernel, grid=(rows // tile, cols // tile), in_spe...  9.47 us
  transfers between devices with their start and end apart: 5, of which 5 were waited for; matrix products, arithmetic and copies ran while one was open for 0% of the time, Pallas kernels for 0%

profile of v8, /device:TPU:0, one launch (start us, length us, event | category | flops | bytes accessed | tf_op | source)
XLA Modules:
  0.0 308.1 jit_solution(10909991522049839325)
XLA Ops:
  6.5 0.7 convert_bitcast_fusion
  7.3 0.1 copy.30
  7.4 2.0 broadcast_in_dim.22.b_ref.c_ref
  9.3 7.2 %shard_map.154 = f32[17,2048]{1,0:T(8,128)} custom-call(bf16[128,2048]{1,0:T(8,128)(2,1)} %raw_ref.3, f32[1,2048]{1,0:T(1,128)} %bitcast.40, bf16[128,2048]{1,0:T(8,128)(2,1)} %x_ref.3, f32[16,2048]{1,0:T(8,128)} %decay_ref.3, f32[2,128,16,128]{3,2,1,0:T(8,128)} %broadcast_in_dim.22.b_ref.c_ref), custom_call_target="tpu_custom_call" | custom-call | flops 25165824 | bytes 1835008 | tf_op jit(solution)/shard_map/pallas_call | solution.py:176
  16.7 27.2 %all-gather.10.cloned.1.call-done.stacked_ref = f32[8,17,2048]{2,1,0:T(8,128)} async-done(((f32[1,17,2048]{2,1,0:T(8,128)}), f32[8,17,2048]{2,1,0:T(8,128)}) %all-gather.10.cloned.1.call-update) | async-done | bytes 1114128 | tf_op jit(solution)/shard_map/all_gather | solution.py:243
  43.9 11.9 %shard_map.155 = bf16[128,2048]{1,0:T(8,128)(2,1)} custom-call(s32[1]{0:T(128)} %bitcast.mine_ref, f32[8,17,2048]{2,1,0:T(8,128)} %all-gather.10.cloned.1.call-done.stacked_ref, bf16[128,2048]{1,0:T(8,128)(2,1)} %raw_ref.3, f32[1,2048]{1,0:T(1,128)} %bitcast.41, bf16[128,2048]{1,0:T(8,128)(2,1)} %x_ref.3, bf16[128,2048]{1,0:T(8,128)(2,1)} %z_ref.1, ...), custom_call_target="tpu_custom_call" | custom-call | flops 37748736 | bytes 3670016 | tf_op jit(solution)/shard_map/pallas_call | solution.py:199
  55.8 32.3 %all-gather.6.cloned.1.call-done.x_ref = bf16[1024,2048]{1,0:T(8,128)(2,1)} async-done(((bf16[128,2048]{1,0:T(8,128)(2,1)}), bf16[1024,2048]{1,0:T(8,128)(2,1)}) %all-gather.6.cloned.1.call-update) | async-done | bytes 4194320 | tf_op jit(solution)/shard_map/all_gather | solution.py:249
  88.2 9.5 %shard_map.156 = bf16[1024,1024]{1,0:T(8,128)(2,1)} custom-call(bf16[1024,2048]{1,0:T(8,128)(2,1)} %all-gather.6.cloned.1.call-done.x_ref, bf16[2048,1024]{1,0:T(8,128)(2,1)} %w_ref.1), custom_call_target="tpu_custom_call" | custom-call | flops 4294967296 | bytes 10485760 | tf_op jit(solution)/shard_map/pallas_call | solution.py:84
  97.6 5.9 %all-to-all-start = ((bf16[32,32,1024]{2,1,0:T(8,128)(2,1)}), bf16[32,32,1024]{2,1,0:T(8,128)(2,1)S(1)}, u32[]{:S(2)}, u32[]{:S(2)}) async-start(bf16[32,32,1024]{2,1,0:T(8,128)(2,1)} %bitcast.36), calls=%async_computation | async-start | bytes 4194304 | tf_op jit(solution)/shard_map/all_to_all | solution.py:252
  103.8 0.1 reduce.1
  103.9 27.3 %all-to-all-done = bf16[32,32,1024]{2,1,0:T(8,128)(2,1)S(1)} async-done(((bf16[32,32,1024]{2,1,0:T(8,128)(2,1)}), bf16[32,32,1024]{2,1,0:T(8,128)(2,1)S(1)}, u32[]{:S(2)}, u32[]{:S(2)}) %all-to-all-start) | async-done | bytes 2097184 | tf_op jit(solution)/shard_map/all_to_all | solution.py:252
  131.2 0.4 convert_reduce_fusion
  131.7 0.3 fusion.5
  132.0 0.2 fusion.9
  132.2 0.2 copy.34
  132.4 0.3 reduce_max.9
  132.8 0.3 div.38
  133.1 0.6 fusion.11
  133.8 0.9 convolution_convert_fusion
  134.8 51.6 %all-gather.8.cloned.1.call-done.refs_0_ = bf16[512,8192]{1,0:T(8,128)(2,1)} async-done(((bf16[16,8192]{1,0:T(8,128)(2,1)}), bf16[512,8192]{1,0:T(8,128)(2,1)}) %all-gather.8.cloned.1.call-update) | async-done | bytes 8388624 | tf_op jit(solution)/shard_map/all_gather | solution.py:287
  186.4 20.4 %shard_map.157 = bf16[512,8192]{1,0:T(8,128)(2,1)} custom-call(bf16[512,8192]{1,0:T(8,128)(2,1)} %all-gather.8.cloned.1.call-done.refs_0_, bf16[8192,384]{1,0:T(8,128)(2,1)} %refs_1_.1, bf16[8192,384]{1,0:T(8,128)(2,1)} %refs_2_.1, bf16[384,8192]{1,0:T(8,128)(2,1)} %refs_3_.1), custom_call_target="tpu_custom_call" | custom-call | flops 9663676416 | bytes 35651584 | tf_op jit(solution)/shard_map/pallas_call | solution.py:48
  206.9 0.3 fusion.4
  207.2 92.3 %reduce-scatter.2.cloned.1.call-done = bf16[16,8192]{1,0:T(8,128)(2,1)} async-done(((bf16[512,8192]{1,0:T(8,128)(2,1)}), bf16[16,8192]{1,0:T(8,128)(2,1)}) %reduce-scatter.2.cloned.1.call-update) | async-done | bytes 262160 | tf_op jit(solution)/shard_map/reduce_scatter | solution.py:288
  299.5 2.1 fusion.1
  (26 shorter events, 0.5 us)
Async XLA Ops:
  6.5 200.3 %copy-start = (bf16[8192,16]{0,1:T(8,128)(2,1)S(1)}, bf16[8192,16]{0,1:T(8,128)(2,1)}, u32[]{:S(2)}) copy-start(bf16[8192,16]{0,1:T(8,128)(2,1)} %param.27) | copy-start | bytes 786436
  6.5 37.4 %all-gather.10.cloned.1.call-start = ((), (), s32[]{:S(2)}) async-start(), calls=%async_computation.5 | async-start | bytes 1769472 | tf_op jit(solution)/shard_map/all_gather | solution.py:243
  16.6 71.5 %all-gather.6.cloned.1.call-start = ((), (), s32[]{:S(2)}) async-start(), calls=%async_computation.2 | async-start | bytes 4718592 | tf_op jit(solution)/shard_map/all_gather | solution.py:249
  97.6 6.0 %copy-start.3 = (s32[32,2]{0,1:T(2,128)S(1)}, s32[32,2]{0,1:T(2,128)}, u32[]{:S(2)}) copy-start(s32[32,2]{0,1:T(2,128)} %param.28) | copy-start | bytes 772
  97.6 34.1 %copy-start.1 = (bf16[32,8192]{1,0:T(8,128)(2,1)S(1)}, bf16[32,8192]{1,0:T(8,128)(2,1)}, u32[]{:S(2)}) copy-start(bf16[32,8192]{1,0:T(8,128)(2,1)} %param.25) | copy-start | bytes 1572868
  97.6 33.6 %all-to-all-start = ((bf16[32,32,1024]{2,1,0:T(8,128)(2,1)}), bf16[32,32,1024]{2,1,0:T(8,128)(2,1)S(1)}, u32[]{:S(2)}, u32[]{:S(2)}) async-start(bf16[32,32,1024]{2,1,0:T(8,128)(2,1)} %bitcast.36), calls=%async_computation | async-start | bytes 4194304 | tf_op jit(solution)/shard_map/all_to_all | solution.py:252
  103.6 28.4 %copy-start.2 = (f32[8192]{0:T(1024)S(1)}, f32[8192]{0:T(1024)}, u32[]{:S(2)}) copy-start(f32[8192]{0:T(1024)} %param.26) | copy-start | bytes 98308
  103.6 82.8 %all-gather.8.cloned.1.call-start = ((), (), s32[]{:S(2)}) async-start(), calls=%async_computation.3 | async-start | bytes 8650752 | tf_op jit(solution)/shard_map/all_gather | solution.py:287
  134.7 164.8 %reduce-scatter.2.cloned.1.call-start = ((), (), s32[]{:S(2)}) async-start(), calls=%async_computation.4 | async-start | bytes 8650752 | tf_op jit(solution)/shard_map/reduce_scatter | solution.py:288
Sparse Core Ops, SparseCore 0:
  16.7 27.1 all-gather.9
  56.0 32.1 all-gather.5
  134.8 51.5 all-gather.7
  207.0 92.4 reduce-scatter.1

commit v9 on v7

--- a/solution.py
+++ b/solution.py
@@ -145,7 +145,7 @@
     return pl.BlockSpec((None, steps, states, LANES), lambda j: (which, 0, 0, 0))
 
 
-def scan_end(step_raw, step_bias, x_in, decay_rate, columns, width=512):
+def scan_end(step_raw, step_bias, x_in, decay_rate, columns, width=1024):
     steps, chans = step_raw.shape
     states = decay_rate.shape[0]
     return pl.pallas_call(
@@ -166,7 +166,7 @@
     )(step_raw, step_bias[None, :], x_in, decay_rate, columns)
 
 
-def scan_gated(mine, stacked, step_raw, step_bias, x_in, z_in, decay_rate, columns, skip_gain, width=512):
+def scan_gated(mine, stacked, step_raw, step_bias, x_in, z_in, decay_rate, columns, skip_gain, width=1024):
     steps, chans = step_raw.shape
     states = decay_rate.shape[0]
     count = stacked.shape[0]

time: 308 us -> 308 us (level)
  no operation moved by 1% of the time
where the time goes in v9:
time: 308 us
  waiting for transfers between devices  231 us (75%)
  Pallas kernels  39.8 us (13%)
  between operations  13.2 us (4%)
  matrix products  12.6 us (4%)
  starting transfers between devices  6.06 us (2%)
    reduce_scatter x1, waiting for transfers between devices, on_device(): lax.psum_scatter(expert_partial(inputs, gate_weight, up_weight, down_weig...  92.3 us
    all_gather x1, waiting for transfers between devices, on_device(): inputs = lax.all_gather(send_rows, ('seq', 'expert'), axis=0, tiled=True)  51.6 us
    all_gather x1, waiting for transfers between devices, on_device(): gathered = lax.all_gather(gated, 'seq', axis=0, tiled=True)  32.3 us
    all_to_all x1, waiting for transfers between devices, on_device(): lax.all_to_all(column_part, ('seq', 'expert'), split_axis=0, concat_axis=...  27.3 us
    all_gather x1, waiting for transfers between devices, on_device(): stacked = lax.all_gather(state_end, 'seq')  27.2 us
    pallas_call x1, Pallas kernels, expert_partial(): pl.pallas_call(lambda *refs: _expert_kernel(nk, *refs), grid=(nk + nn,),...  20.5 us
    pallas_call x1, Pallas kernels, scan_gated(): pl.pallas_call(_out_kernel, grid=(chans // width,), in_specs=[pl.BlockSpe...  12.1 us
    dot_general x1, matrix products, on_device(): jnp.dot(gathered, out_proj, preferred_element_type=jnp.float32)  9.28 us
  transfers between devices with their start and end apart: 5, of which 5 were waited for; matrix products, arithmetic and copies ran while one was open for 0% of the time, Pallas kernels for 0%

profile of v9, /device:TPU:0, one launch (start us, length us, event | category | flops | bytes accessed | tf_op | source)
XLA Modules:
  0.0 308.1 jit_solution(14576947464333306087)
XLA Ops:
  6.5 0.7 convert_bitcast_fusion
  7.3 0.1 copy.30
  7.4 2.0 broadcast_in_dim.22.b_ref.c_ref
  9.3 7.2 %shard_map.154 = f32[17,2048]{1,0:T(8,128)} custom-call(bf16[128,2048]{1,0:T(8,128)(2,1)} %raw_ref.3, f32[1,2048]{1,0:T(1,128)} %bitcast.42, bf16[128,2048]{1,0:T(8,128)(2,1)} %x_ref.3, f32[16,2048]{1,0:T(8,128)} %decay_ref.3, f32[2,128,16,128]{3,2,1,0:T(8,128)} %broadcast_in_dim.22.b_ref.c_ref), custom_call_target="tpu_custom_call" | custom-call | flops 25165824 | bytes 1835008 | tf_op jit(solution)/shard_map/pallas_call | solution.py:151
  16.6 27.2 %all-gather.10.cloned.1.call-done.stacked_ref = f32[8,17,2048]{2,1,0:T(8,128)} async-done(((f32[1,17,2048]{2,1,0:T(8,128)}), f32[8,17,2048]{2,1,0:T(8,128)}) %all-gather.10.cloned.1.call-update) | async-done | bytes 1114128 | tf_op jit(solution)/shard_map/all_gather | solution.py:218
  43.9 12.1 %shard_map.155 = bf16[128,2048]{1,0:T(8,128)(2,1)} custom-call(s32[1]{0:T(128)} %bitcast.mine_ref, f32[8,17,2048]{2,1,0:T(8,128)} %all-gather.10.cloned.1.call-done.stacked_ref, bf16[128,2048]{1,0:T(8,128)(2,1)} %raw_ref.3, f32[1,2048]{1,0:T(1,128)} %bitcast.43, bf16[128,2048]{1,0:T(8,128)(2,1)} %x_ref.3, bf16[128,2048]{1,0:T(8,128)(2,1)} %z_ref.1, ...), custom_call_target="tpu_custom_call" | custom-call | flops 37748736 | bytes 3670016 | tf_op jit(solution)/shard_map/pallas_call | solution.py:174
  56.0 32.3 %all-gather.6.cloned.1.call-done = bf16[1024,2048]{1,0:T(8,128)(2,1)} async-done(((bf16[128,2048]{1,0:T(8,128)(2,1)}), bf16[1024,2048]{1,0:T(8,128)(2,1)}) %all-gather.6.cloned.1.call-update) | async-done | bytes 4194320 | tf_op jit(solution)/shard_map/all_gather | solution.py:224
  88.3 9.3 %convolution_convert_fusion.1 = bf16[1024,1024]{1,0:T(8,128)(2,1)} fusion(bf16[1024,2048]{1,0:T(8,128)(2,1)} %all-gather.6.cloned.1.call-done, bf16[2048,1024]{1,0:T(8,128)(2,1)} %param.24), kind=kOutput, calls=%fused_computation.5 | convolution fusion | flops 4296015872 | bytes 10485760 | tf_op jit(solution)/shard_map/dot_general | solution.py:225
  97.6 5.9 %all-to-all-start = ((bf16[32,32,1024]{2,1,0:T(8,128)(2,1)}), bf16[32,32,1024]{2,1,0:T(8,128)(2,1)S(1)}, u32[]{:S(2)}, u32[]{:S(2)}) async-start(bf16[32,32,1024]{2,1,0:T(8,128)(2,1)} %bitcast.38), calls=%async_computation | async-start | bytes 4194304 | tf_op jit(solution)/shard_map/all_to_all | solution.py:227
  103.8 0.1 reduce.1
  103.9 27.3 %all-to-all-done = bf16[32,32,1024]{2,1,0:T(8,128)(2,1)S(1)} async-done(((bf16[32,32,1024]{2,1,0:T(8,128)(2,1)}), bf16[32,32,1024]{2,1,0:T(8,128)(2,1)S(1)}, u32[]{:S(2)}, u32[]{:S(2)}) %all-to-all-start) | async-done | bytes 2097184 | tf_op jit(solution)/shard_map/all_to_all | solution.py:227
  131.2 0.4 convert_reduce_fusion
  131.7 0.3 fusion.5
  132.0 0.2 fusion.9
  132.2 0.2 copy.34
  132.4 0.3 reduce_max.9
  132.8 0.3 div.38
  133.1 0.7 fusion.11
  133.8 0.9 convolution_convert_fusion
  134.8 51.6 %all-gather.8.cloned.1.call-done.refs_0_ = bf16[512,8192]{1,0:T(8,128)(2,1)} async-done(((bf16[16,8192]{1,0:T(8,128)(2,1)}), bf16[512,8192]{1,0:T(8,128)(2,1)}) %all-gather.8.cloned.1.call-update) | async-done | bytes 8388624 | tf_op jit(solution)/shard_map/all_gather | solution.py:262
  186.4 20.5 %shard_map.156 = bf16[512,8192]{1,0:T(8,128)(2,1)} custom-call(bf16[512,8192]{1,0:T(8,128)(2,1)} %all-gather.8.cloned.1.call-done.refs_0_, bf16[8192,384]{1,0:T(8,128)(2,1)} %refs_1_.1, bf16[8192,384]{1,0:T(8,128)(2,1)} %refs_2_.1, bf16[384,8192]{1,0:T(8,128)(2,1)} %refs_3_.1), custom_call_target="tpu_custom_call" | custom-call | flops 9663676416 | bytes 35651584 | tf_op jit(solution)/shard_map/pallas_call | solution.py:48
  206.9 0.3 fusion.4
  207.3 92.3 %reduce-scatter.2.cloned.1.call-done = bf16[16,8192]{1,0:T(8,128)(2,1)} async-done(((bf16[512,8192]{1,0:T(8,128)(2,1)}), bf16[16,8192]{1,0:T(8,128)(2,1)}) %reduce-scatter.2.cloned.1.call-update) | async-done | bytes 262160 | tf_op jit(solution)/shard_map/reduce_scatter | solution.py:263
  299.5 2.1 fusion.1
  (26 shorter events, 0.5 us)
Async XLA Ops:
  6.5 200.4 %copy-start = (bf16[8192,16]{0,1:T(8,128)(2,1)S(1)}, bf16[8192,16]{0,1:T(8,128)(2,1)}, u32[]{:S(2)}) copy-start(bf16[8192,16]{0,1:T(8,128)(2,1)} %param.27) | copy-start | bytes 786436
  6.5 37.3 %all-gather.10.cloned.1.call-start = ((), (), s32[]{:S(2)}) async-start(), calls=%async_computation.5 | async-start | bytes 1769472 | tf_op jit(solution)/shard_map/all_gather | solution.py:218
  16.6 71.8 %all-gather.6.cloned.1.call-start = ((), (), s32[]{:S(2)}) async-start(), calls=%async_computation.2 | async-start | bytes 4718592 | tf_op jit(solution)/shard_map/all_gather | solution.py:224
  97.6 6.0 %copy-start.3 = (s32[32,2]{0,1:T(2,128)S(1)}, s32[32,2]{0,1:T(2,128)}, u32[]{:S(2)}) copy-start(s32[32,2]{0,1:T(2,128)} %param.28) | copy-start | bytes 772
  97.6 34.1 %copy-start.1 = (bf16[32,8192]{1,0:T(8,128)(2,1)S(1)}, bf16[32,8192]{1,0:T(8,128)(2,1)}, u32[]{:S(2)}) copy-start(bf16[32,8192]{1,0:T(8,128)(2,1)} %param.25) | copy-start | bytes 1572868
  97.6 33.6 %all-to-all-start = ((bf16[32,32,1024]{2,1,0:T(8,128)(2,1)}), bf16[32,32,1024]{2,1,0:T(8,128)(2,1)S(1)}, u32[]{:S(2)}, u32[]{:S(2)}) async-start(bf16[32,32,1024]{2,1,0:T(8,128)(2,1)} %bitcast.38), calls=%async_computation | async-start | bytes 4194304 | tf_op jit(solution)/shard_map/all_to_all | solution.py:227
  103.6 28.5 %copy-start.2 = (f32[8192]{0:T(1024)S(1)}, f32[8192]{0:T(1024)}, u32[]{:S(2)}) copy-start(f32[8192]{0:T(1024)} %param.26) | copy-start | bytes 98308
  103.6 82.9 %all-gather.8.cloned.1.call-start = ((), (), s32[]{:S(2)}) async-start(), calls=%async_computation.3 | async-start | bytes 8650752 | tf_op jit(solution)/shard_map/all_gather | solution.py:262
  134.7 164.8 %reduce-scatter.2.cloned.1.call-start = ((), (), s32[]{:S(2)}) async-start(), calls=%async_computation.4 | async-start | bytes 8650752 | tf_op jit(solution)/shard_map/reduce_scatter | solution.py:263
Sparse Core Ops, SparseCore 0:
  16.7 27.1 all-gather.9
  56.1 32.1 all-gather.5
  134.9 51.5 all-gather.7
  207.0 92.4 reduce-scatter.1

commit v10 on v7

--- a/solution.py
+++ b/solution.py
@@ -41,17 +41,17 @@
 def expert_partial(inputs, gate_weight, up_weight, down_weight):
     slots, width = inputs.shape
     hidden = gate_weight.shape[1]
-    tile = EXPERT_TILE
-    nk, nn = width // tile, down_weight.shape[1] // tile
+    tile, k_tile = EXPERT_TILE, EXPERT_TILE // 2
+    nk, nn = width // k_tile, down_weight.shape[1] // tile
     k_of = lambda i: jnp.minimum(i, nk - 1)
     n_of = lambda i: jnp.maximum(i - nk, 0)
     return pl.pallas_call(
         lambda *refs: _expert_kernel(nk, *refs),
         grid=(nk + nn,),
         in_specs=[
-            pl.BlockSpec((slots, tile), lambda i: (0, k_of(i))),
-            pl.BlockSpec((tile, hidden), lambda i: (k_of(i), 0)),
-            pl.BlockSpec((tile, hidden), lambda i: (k_of(i), 0)),
+            pl.BlockSpec((slots, k_tile), lambda i: (0, k_of(i))),
+            pl.BlockSpec((k_tile, hidden), lambda i: (k_of(i), 0)),
+            pl.BlockSpec((k_tile, hidden), lambda i: (k_of(i), 0)),
             pl.BlockSpec((hidden, tile), lambda i: (0, n_of(i))),
         ],
         out_specs=pl.BlockSpec((slots, tile), lambda i: (0, n_of(i))),

time: 308 us -> 310 us (level)
  no operation moved by 1% of the time
where the time goes in v10:
time: 310 us; the launch traced here: 309 us
  waiting for transfers between devices  231 us (75%)
  Pallas kernels  40.9 us (13%)
  between operations  13.2 us (4%)
  matrix products  12.5 us (4%)
  starting transfers between devices  6.06 us (2%)
    reduce_scatter x1, waiting for transfers between devices, on_device(): lax.psum_scatter(expert_partial(inputs, gate_weight, up_weight, down_weig...  92.3 us
    all_gather x1, waiting for transfers between devices, on_device(): inputs = lax.all_gather(send_rows, ('seq', 'expert'), axis=0, tiled=True)  51.6 us
    all_gather x1, waiting for transfers between devices, on_device(): gathered = lax.all_gather(gated, 'seq', axis=0, tiled=True)  32.3 us
    all_to_all x1, waiting for transfers between devices, on_device(): lax.all_to_all(column_part, ('seq', 'expert'), split_axis=0, concat_axis=...  27.3 us
    all_gather x1, waiting for transfers between devices, on_device(): stacked = lax.all_gather(state_end, 'seq')  27.2 us
    pallas_call x1, Pallas kernels, expert_partial(): pl.pallas_call(lambda *refs: _expert_kernel(nk, *refs), grid=(nk + nn,),...  21.7 us
    pallas_call x1, Pallas kernels, scan_gated(): pl.pallas_call(_out_kernel, grid=(chans // width,), in_specs=[pl.BlockSpe...  11.9 us
    dot_general x1, matrix products, on_device(): jnp.dot(gathered, out_proj, preferred_element_type=jnp.float32)  9.28 us
  transfers between devices with their start and end apart: 5, of which 5 were waited for; matrix products, arithmetic and copies ran while one was open for 0% of the time, Pallas kernels for 0%

profile of v10, /device:TPU:0, one launch (start us, length us, event | category | flops | bytes accessed | tf_op | source)
XLA Modules:
  0.0 309.2 jit_solution(6972011224200090780)
XLA Ops:
  6.5 0.7 convert_bitcast_fusion
  7.3 0.1 copy.30
  7.4 2.0 broadcast_in_dim.22.b_ref.c_ref
  9.3 7.2 %shard_map.154 = f32[17,2048]{1,0:T(8,128)} custom-call(bf16[128,2048]{1,0:T(8,128)(2,1)} %raw_ref.3, f32[1,2048]{1,0:T(1,128)} %bitcast.42, bf16[128,2048]{1,0:T(8,128)(2,1)} %x_ref.3, f32[16,2048]{1,0:T(8,128)} %decay_ref.3, f32[2,128,16,128]{3,2,1,0:T(8,128)} %broadcast_in_dim.22.b_ref.c_ref), custom_call_target="tpu_custom_call" | custom-call | flops 25165824 | bytes 1835008 | tf_op jit(solution)/shard_map/pallas_call | solution.py:151
  16.7 27.2 %all-gather.10.cloned.1.call-done.stacked_ref = f32[8,17,2048]{2,1,0:T(8,128)} async-done(((f32[1,17,2048]{2,1,0:T(8,128)}), f32[8,17,2048]{2,1,0:T(8,128)}) %all-gather.10.cloned.1.call-update) | async-done | bytes 1114128 | tf_op jit(solution)/shard_map/all_gather | solution.py:218
  43.9 11.9 %shard_map.155 = bf16[128,2048]{1,0:T(8,128)(2,1)} custom-call(s32[1]{0:T(128)} %bitcast.mine_ref, f32[8,17,2048]{2,1,0:T(8,128)} %all-gather.10.cloned.1.call-done.stacked_ref, bf16[128,2048]{1,0:T(8,128)(2,1)} %raw_ref.3, f32[1,2048]{1,0:T(1,128)} %bitcast.43, bf16[128,2048]{1,0:T(8,128)(2,1)} %x_ref.3, bf16[128,2048]{1,0:T(8,128)(2,1)} %z_ref.1, ...), custom_call_target="tpu_custom_call" | custom-call | flops 37748736 | bytes 3670016 | tf_op jit(solution)/shard_map/pallas_call | solution.py:174
  55.8 32.3 %all-gather.6.cloned.1.call-done = bf16[1024,2048]{1,0:T(8,128)(2,1)} async-done(((bf16[128,2048]{1,0:T(8,128)(2,1)}), bf16[1024,2048]{1,0:T(8,128)(2,1)}) %all-gather.6.cloned.1.call-update) | async-done | bytes 4194320 | tf_op jit(solution)/shard_map/all_gather | solution.py:224
  88.2 9.3 %convolution_convert_fusion.1 = bf16[1024,1024]{1,0:T(8,128)(2,1)} fusion(bf16[1024,2048]{1,0:T(8,128)(2,1)} %all-gather.6.cloned.1.call-done, bf16[2048,1024]{1,0:T(8,128)(2,1)} %param.24), kind=kOutput, calls=%fused_computation.5 | convolution fusion | flops 4296015872 | bytes 10485760 | tf_op jit(solution)/shard_map/dot_general | solution.py:225
  97.4 5.9 %all-to-all-start = ((bf16[32,32,1024]{2,1,0:T(8,128)(2,1)}), bf16[32,32,1024]{2,1,0:T(8,128)(2,1)S(1)}, u32[]{:S(2)}, u32[]{:S(2)}) async-start(bf16[32,32,1024]{2,1,0:T(8,128)(2,1)} %bitcast.38), calls=%async_computation | async-start | bytes 4194304 | tf_op jit(solution)/shard_map/all_to_all | solution.py:227
  103.6 0.1 reduce.1
  103.7 27.3 %all-to-all-done = bf16[32,32,1024]{2,1,0:T(8,128)(2,1)S(1)} async-done(((bf16[32,32,1024]{2,1,0:T(8,128)(2,1)}), bf16[32,32,1024]{2,1,0:T(8,128)(2,1)S(1)}, u32[]{:S(2)}, u32[]{:S(2)}) %all-to-all-start) | async-done | bytes 2097184 | tf_op jit(solution)/shard_map/all_to_all | solution.py:227
  131.1 0.4 convert_reduce_fusion
  131.6 0.3 fusion.5
  131.9 0.2 fusion.9
  132.1 0.2 copy.34
  132.3 0.3 reduce_max.9
  132.6 0.3 div.38
  132.9 0.7 fusion.11
  133.6 0.9 convolution_convert_fusion
  134.6 51.6 %all-gather.8.cloned.1.call-done.refs_0_ = bf16[512,8192]{1,0:T(8,128)(2,1)} async-done(((bf16[16,8192]{1,0:T(8,128)(2,1)}), bf16[512,8192]{1,0:T(8,128)(2,1)}) %all-gather.8.cloned.1.call-update) | async-done | bytes 8388624 | tf_op jit(solution)/shard_map/all_gather | solution.py:262
  186.3 21.7 %shard_map.156 = bf16[512,8192]{1,0:T(8,128)(2,1)} custom-call(bf16[512,8192]{1,0:T(8,128)(2,1)} %all-gather.8.cloned.1.call-done.refs_0_, bf16[8192,384]{1,0:T(8,128)(2,1)} %refs_1_.1, bf16[8192,384]{1,0:T(8,128)(2,1)} %refs_2_.1, bf16[384,8192]{1,0:T(8,128)(2,1)} %refs_3_.1), custom_call_target="tpu_custom_call" | custom-call | flops 9663676416 | bytes 35651584 | tf_op jit(solution)/shard_map/pallas_call | solution.py:48
  208.0 0.3 fusion.4
  208.4 92.3 %reduce-scatter.2.cloned.1.call-done = bf16[16,8192]{1,0:T(8,128)(2,1)} async-done(((bf16[512,8192]{1,0:T(8,128)(2,1)}), bf16[16,8192]{1,0:T(8,128)(2,1)}) %reduce-scatter.2.cloned.1.call-update) | async-done | bytes 262160 | tf_op jit(solution)/shard_map/reduce_scatter | solution.py:263
  300.6 2.1 fusion.1
  (26 shorter events, 0.5 us)
Async XLA Ops:
  6.5 201.5 %copy-start = (bf16[8192,16]{0,1:T(8,128)(2,1)S(1)}, bf16[8192,16]{0,1:T(8,128)(2,1)}, u32[]{:S(2)}) copy-start(bf16[8192,16]{0,1:T(8,128)(2,1)} %param.27) | copy-start | bytes 786436
  6.5 37.4 %all-gather.10.cloned.1.call-start = ((), (), s32[]{:S(2)}) async-start(), calls=%async_computation.5 | async-start | bytes 1769472 | tf_op jit(solution)/shard_map/all_gather | solution.py:218
  16.6 71.5 %all-gather.6.cloned.1.call-start = ((), (), s32[]{:S(2)}) async-start(), calls=%async_computation.2 | async-start | bytes 4718592 | tf_op jit(solution)/shard_map/all_gather | solution.py:224
  97.4 6.0 %copy-start.3 = (s32[32,2]{0,1:T(2,128)S(1)}, s32[32,2]{0,1:T(2,128)}, u32[]{:S(2)}) copy-start(s32[32,2]{0,1:T(2,128)} %param.28) | copy-start | bytes 772
  97.4 34.1 %copy-start.1 = (bf16[32,8192]{1,0:T(8,128)(2,1)S(1)}, bf16[32,8192]{1,0:T(8,128)(2,1)}, u32[]{:S(2)}) copy-start(bf16[32,8192]{1,0:T(8,128)(2,1)} %param.25) | copy-start | bytes 1572868
  97.4 33.6 %all-to-all-start = ((bf16[32,32,1024]{2,1,0:T(8,128)(2,1)}), bf16[32,32,1024]{2,1,0:T(8,128)(2,1)S(1)}, u32[]{:S(2)}, u32[]{:S(2)}) async-start(bf16[32,32,1024]{2,1,0:T(8,128)(2,1)} %bitcast.38), calls=%async_computation | async-start | bytes 4194304 | tf_op jit(solution)/shard_map/all_to_all | solution.py:227
  103.4 28.5 %copy-start.2 = (f32[8192]{0:T(1024)S(1)}, f32[8192]{0:T(1024)}, u32[]{:S(2)}) copy-start(f32[8192]{0:T(1024)} %param.26) | copy-start | bytes 98308
  103.4 82.9 %all-gather.8.cloned.1.call-start = ((), (), s32[]{:S(2)}) async-start(), calls=%async_computation.3 | async-start | bytes 8650752 | tf_op jit(solution)/shard_map/all_gather | solution.py:262
  134.6 166.1 %reduce-scatter.2.cloned.1.call-start = ((), (), s32[]{:S(2)}) async-start(), calls=%async_computation.4 | async-start | bytes 8650752 | tf_op jit(solution)/shard_map/reduce_scatter | solution.py:263
Sparse Core Ops, SparseCore 0:
  16.7 27.1 all-gather.9
  56.0 32.1 all-gather.5
  134.7 51.5 all-gather.7
  208.1 92.4 reduce-scatter.1

commit v11 on v10

--- a/solution.py
+++ b/solution.py
@@ -41,7 +41,7 @@
 def expert_partial(inputs, gate_weight, up_weight, down_weight):
     slots, width = inputs.shape
     hidden = gate_weight.shape[1]
-    tile, k_tile = EXPERT_TILE, EXPERT_TILE // 2
+    tile, k_tile = EXPERT_TILE, EXPERT_TILE * 2
     nk, nn = width // k_tile, down_weight.shape[1] // tile
     k_of = lambda i: jnp.minimum(i, nk - 1)
     n_of = lambda i: jnp.maximum(i - nk, 0)

time: 310 us -> 309 us (level)
  no operation moved by 1% of the time
where the time goes in v11:
time: 309 us
  waiting for transfers between devices  231 us (75%)
  Pallas kernels  40.5 us (13%)
  between operations  13.2 us (4%)
  matrix products  12.6 us (4%)
  starting transfers between devices  6.24 us (2%)
    reduce_scatter x1, waiting for transfers between devices, on_device(): lax.psum_scatter(expert_partial(inputs, gate_weight, up_weight, down_weig...  92.3 us
    all_gather x1, waiting for transfers between devices, on_device(): inputs = lax.all_gather(send_rows, ('seq', 'expert'), axis=0, tiled=True)  51.5 us
    all_gather x1, waiting for transfers between devices, on_device(): gathered = lax.all_gather(gated, 'seq', axis=0, tiled=True)  32.3 us
    all_to_all x1, waiting for transfers between devices, on_device(): lax.all_to_all(column_part, ('seq', 'expert'), split_axis=0, concat_axis=...  27.3 us
    all_gather x1, waiting for transfers between devices, on_device(): stacked = lax.all_gather(state_end, 'seq')  27.2 us
    pallas_call x1, Pallas kernels, expert_partial(): pl.pallas_call(lambda *refs: _expert_kernel(nk, *refs), grid=(nk + nn,),...  21.4 us
    pallas_call x1, Pallas kernels, scan_gated(): pl.pallas_call(_out_kernel, grid=(chans // width,), in_specs=[pl.BlockSpe...  11.9 us
    dot_general x1, matrix products, on_device(): jnp.dot(gathered, out_proj, preferred_element_type=jnp.float32)  9.28 us
  transfers between devices with their start and end apart: 5, of which 5 were waited for; matrix products, arithmetic and copies ran while one was open for 0% of the time, Pallas kernels for 0%

profile of v11, /device:TPU:0, one launch (start us, length us, event | category | flops | bytes accessed | tf_op | source)
XLA Modules:
  0.0 308.9 jit_solution(11070819082532582009)
XLA Ops:
  6.5 0.7 convert_bitcast_fusion
  7.4 2.0 broadcast_in_dim.22.b_ref.c_ref
  9.3 7.2 %shard_map.154 = f32[17,2048]{1,0:T(8,128)} custom-call(bf16[128,2048]{1,0:T(8,128)(2,1)} %raw_ref.3, f32[1,2048]{1,0:T(1,128)} %bitcast.42, bf16[128,2048]{1,0:T(8,128)(2,1)} %x_ref.3, f32[16,2048]{1,0:T(8,128)} %decay_ref.3, f32[2,128,16,128]{3,2,1,0:T(8,128)} %broadcast_in_dim.22.b_ref.c_ref), custom_call_target="tpu_custom_call" | custom-call | flops 25165824 | bytes 1835008 | tf_op jit(solution)/shard_map/pallas_call | solution.py:151
  16.7 27.2 %all-gather.10.cloned.1.call-done.stacked_ref = f32[8,17,2048]{2,1,0:T(8,128)} async-done(((f32[1,17,2048]{2,1,0:T(8,128)}), f32[8,17,2048]{2,1,0:T(8,128)}) %all-gather.10.cloned.1.call-update) | async-done | bytes 1114128 | tf_op jit(solution)/shard_map/all_gather | solution.py:218
  43.9 11.9 %shard_map.155 = bf16[128,2048]{1,0:T(8,128)(2,1)} custom-call(s32[1]{0:T(128)} %bitcast.mine_ref, f32[8,17,2048]{2,1,0:T(8,128)} %all-gather.10.cloned.1.call-done.stacked_ref, bf16[128,2048]{1,0:T(8,128)(2,1)} %raw_ref.3, f32[1,2048]{1,0:T(1,128)} %bitcast.43, bf16[128,2048]{1,0:T(8,128)(2,1)} %x_ref.3, bf16[128,2048]{1,0:T(8,128)(2,1)} %z_ref.1, ...), custom_call_target="tpu_custom_call" | custom-call | flops 37748736 | bytes 3670016 | tf_op jit(solution)/shard_map/pallas_call | solution.py:174
  55.8 32.3 %all-gather.6.cloned.1.call-done = bf16[1024,2048]{1,0:T(8,128)(2,1)} async-done(((bf16[128,2048]{1,0:T(8,128)(2,1)}), bf16[1024,2048]{1,0:T(8,128)(2,1)}) %all-gather.6.cloned.1.call-update) | async-done | bytes 4194320 | tf_op jit(solution)/shard_map/all_gather | solution.py:224
  88.2 9.3 %convolution_convert_fusion.1 = bf16[1024,1024]{1,0:T(8,128)(2,1)} fusion(bf16[1024,2048]{1,0:T(8,128)(2,1)} %all-gather.6.cloned.1.call-done, bf16[2048,1024]{1,0:T(8,128)(2,1)} %param.24), kind=kOutput, calls=%fused_computation.5 | convolution fusion | flops 4296015872 | bytes 10485760 | tf_op jit(solution)/shard_map/dot_general | solution.py:225
  97.4 5.9 %all-to-all-start = ((bf16[32,32,1024]{2,1,0:T(8,128)(2,1)}), bf16[32,32,1024]{2,1,0:T(8,128)(2,1)S(1)}, u32[]{:S(2)}, u32[]{:S(2)}) async-start(bf16[32,32,1024]{2,1,0:T(8,128)(2,1)} %bitcast.38), calls=%async_computation | async-start | bytes 4194304 | tf_op jit(solution)/shard_map/all_to_all | solution.py:227
  103.6 0.1 reduce.1
  103.7 27.3 %all-to-all-done = bf16[32,32,1024]{2,1,0:T(8,128)(2,1)S(1)} async-done(((bf16[32,32,1024]{2,1,0:T(8,128)(2,1)}), bf16[32,32,1024]{2,1,0:T(8,128)(2,1)S(1)}, u32[]{:S(2)}, u32[]{:S(2)}) %all-to-all-start) | async-done | bytes 2097184 | tf_op jit(solution)/shard_map/all_to_all | solution.py:227
  131.1 0.4 convert_reduce_fusion
  131.6 0.3 fusion.5
  131.9 0.2 fusion.9
  132.1 0.2 copy.34
  132.3 0.3 reduce_max.9
  132.6 0.3 div.38
  132.9 0.7 fusion.11
  133.6 0.9 convolution_convert_fusion
  134.6 0.2 reduce-scatter.2.cloned.1.call-start
  134.8 51.5 %all-gather.8.cloned.1.call-done.refs_0_ = bf16[512,8192]{1,0:T(8,128)(2,1)} async-done(((bf16[16,8192]{1,0:T(8,128)(2,1)}), bf16[512,8192]{1,0:T(8,128)(2,1)}) %all-gather.8.cloned.1.call-update) | async-done | bytes 8388624 | tf_op jit(solution)/shard_map/all_gather | solution.py:262
  186.3 21.4 %shard_map.156 = bf16[512,8192]{1,0:T(8,128)(2,1)} custom-call(bf16[512,8192]{1,0:T(8,128)(2,1)} %all-gather.8.cloned.1.call-done.refs_0_, bf16[8192,384]{1,0:T(8,128)(2,1)} %refs_1_.1, bf16[8192,384]{1,0:T(8,128)(2,1)} %refs_2_.1, bf16[384,8192]{1,0:T(8,128)(2,1)} %refs_3_.1), custom_call_target="tpu_custom_call" | custom-call | flops 9663676416 | bytes 35651584 | tf_op jit(solution)/shard_map/pallas_call | solution.py:48
  207.6 0.3 fusion.4
  208.0 92.3 %reduce-scatter.2.cloned.1.call-done = bf16[16,8192]{1,0:T(8,128)(2,1)} async-done(((bf16[512,8192]{1,0:T(8,128)(2,1)}), bf16[16,8192]{1,0:T(8,128)(2,1)}) %reduce-scatter.2.cloned.1.call-update) | async-done | bytes 262160 | tf_op jit(solution)/shard_map/reduce_scatter | solution.py:263
  300.2 2.1 fusion.1
  (26 shorter events, 0.6 us)
Async XLA Ops:
  6.5 201.1 %copy-start = (bf16[8192,16]{0,1:T(8,128)(2,1)S(1)}, bf16[8192,16]{0,1:T(8,128)(2,1)}, u32[]{:S(2)}) copy-start(bf16[8192,16]{0,1:T(8,128)(2,1)} %param.27) | copy-start | bytes 786436
  6.5 37.4 %all-gather.10.cloned.1.call-start = ((), (), s32[]{:S(2)}) async-start(), calls=%async_computation.5 | async-start | bytes 1769472 | tf_op jit(solution)/shard_map/all_gather | solution.py:218
  16.6 71.5 %all-gather.6.cloned.1.call-start = ((), (), s32[]{:S(2)}) async-start(), calls=%async_computation.2 | async-start | bytes 4718592 | tf_op jit(solution)/shard_map/all_gather | solution.py:224
  97.4 6.0 %copy-start.3 = (s32[32,2]{0,1:T(2,128)S(1)}, s32[32,2]{0,1:T(2,128)}, u32[]{:S(2)}) copy-start(s32[32,2]{0,1:T(2,128)} %param.28) | copy-start | bytes 772
  97.4 34.1 %copy-start.1 = (bf16[32,8192]{1,0:T(8,128)(2,1)S(1)}, bf16[32,8192]{1,0:T(8,128)(2,1)}, u32[]{:S(2)}) copy-start(bf16[32,8192]{1,0:T(8,128)(2,1)} %param.25) | copy-start | bytes 1572868
  97.4 33.6 %all-to-all-start = ((bf16[32,32,1024]{2,1,0:T(8,128)(2,1)}), bf16[32,32,1024]{2,1,0:T(8,128)(2,1)S(1)}, u32[]{:S(2)}, u32[]{:S(2)}) async-start(bf16[32,32,1024]{2,1,0:T(8,128)(2,1)} %bitcast.38), calls=%async_computation | async-start | bytes 4194304 | tf_op jit(solution)/shard_map/all_to_all | solution.py:227
  103.4 28.5 %copy-start.2 = (f32[8192]{0:T(1024)S(1)}, f32[8192]{0:T(1024)}, u32[]{:S(2)}) copy-start(f32[8192]{0:T(1024)} %param.26) | copy-start | bytes 98308
  103.4 82.9 %all-gather.8.cloned.1.call-start = ((), (), s32[]{:S(2)}) async-start(), calls=%async_computation.3 | async-start | bytes 8650752 | tf_op jit(solution)/shard_map/all_gather | solution.py:262
  134.6 165.7 %reduce-scatter.2.cloned.1.call-start = ((), (), s32[]{:S(2)}) async-start(), calls=%async_computation.4 | async-start | bytes 8650752 | tf_op jit(solution)/shard_map/reduce_scatter | solution.py:263
Sparse Core Ops, SparseCore 0:
  16.7 27.1 all-gather.9
  56.0 32.1 all-gather.5
  134.7 51.5 all-gather.7
  207.8 92.4 reduce-scatter.1

commit v12 on v7

--- a/solution.py
+++ b/solution.py
@@ -7,7 +7,7 @@
 
 BLOCK = 128
 LANES = 128
-ROWS_PER_LOAD = 16
+ROWS_PER_LOAD = 32
 
 EXPERT_TILE = 2048
 

time: 308 us -> 308 us (level)
  no operation moved by 1% of the time
where the time goes in v12:
time: 308 us
  waiting for transfers between devices  231 us (75%)
  Pallas kernels  39.5 us (13%)
  between operations  13.2 us (4%)
  matrix products  12.6 us (4%)
  starting transfers between devices  6.05 us (2%)
    reduce_scatter x1, waiting for transfers between devices, on_device(): lax.psum_scatter(expert_partial(inputs, gate_weight, up_weight, down_weig...  92.3 us
    all_gather x1, waiting for transfers between devices, on_device(): inputs = lax.all_gather(send_rows, ('seq', 'expert'), axis=0, tiled=True)  51.6 us
    all_gather x1, waiting for transfers between devices, on_device(): gathered = lax.all_gather(gated, 'seq', axis=0, tiled=True)  32.3 us
    all_to_all x1, waiting for transfers between devices, on_device(): lax.all_to_all(column_part, ('seq', 'expert'), split_axis=0, concat_axis=...  27.3 us
    all_gather x1, waiting for transfers between devices, on_device(): stacked = lax.all_gather(state_end, 'seq')  27.2 us
    pallas_call x1, Pallas kernels, expert_partial(): pl.pallas_call(lambda *refs: _expert_kernel(nk, *refs), grid=(nk + nn,),...  20.4 us
    pallas_call x1, Pallas kernels, scan_gated(): pl.pallas_call(_out_kernel, grid=(chans // width,), in_specs=[pl.BlockSpe...  12 us
    dot_general x1, matrix products, on_device(): jnp.dot(gathered, out_proj, preferred_element_type=jnp.float32)  9.29 us
  transfers between devices with their start and end apart: 5, of which 5 were waited for; matrix products, arithmetic and copies ran while one was open for 0% of the time, Pallas kernels for 0%

profile of v12, /device:TPU:0, one launch (start us, length us, event | category | flops | bytes accessed | tf_op | source)
XLA Modules:
  0.0 307.8 jit_solution(1548882114338853067)
XLA Ops:
  6.5 0.7 convert_bitcast_fusion
  7.3 0.1 copy.30
  7.4 2.0 broadcast_in_dim.22.b_ref.c_ref
  9.3 7.0 %shard_map.154 = f32[17,2048]{1,0:T(8,128)} custom-call(bf16[128,2048]{1,0:T(8,128)(2,1)} %raw_ref.3, f32[1,2048]{1,0:T(1,128)} %bitcast.42, bf16[128,2048]{1,0:T(8,128)(2,1)} %x_ref.3, f32[16,2048]{1,0:T(8,128)} %decay_ref.3, f32[2,128,16,128]{3,2,1,0:T(8,128)} %broadcast_in_dim.22.b_ref.c_ref), custom_call_target="tpu_custom_call" | custom-call | flops 25165824 | bytes 1835008 | tf_op jit(solution)/shard_map/pallas_call | solution.py:151
  16.4 27.2 %all-gather.10.cloned.1.call-done.stacked_ref = f32[8,17,2048]{2,1,0:T(8,128)} async-done(((f32[1,17,2048]{2,1,0:T(8,128)}), f32[8,17,2048]{2,1,0:T(8,128)}) %all-gather.10.cloned.1.call-update) | async-done | bytes 1114128 | tf_op jit(solution)/shard_map/all_gather | solution.py:218
  43.7 12.0 %shard_map.155 = bf16[128,2048]{1,0:T(8,128)(2,1)} custom-call(s32[1]{0:T(128)} %bitcast.mine_ref, f32[8,17,2048]{2,1,0:T(8,128)} %all-gather.10.cloned.1.call-done.stacked_ref, bf16[128,2048]{1,0:T(8,128)(2,1)} %raw_ref.3, f32[1,2048]{1,0:T(1,128)} %bitcast.43, bf16[128,2048]{1,0:T(8,128)(2,1)} %x_ref.3, bf16[128,2048]{1,0:T(8,128)(2,1)} %z_ref.1, ...), custom_call_target="tpu_custom_call" | custom-call | flops 37748736 | bytes 3670016 | tf_op jit(solution)/shard_map/pallas_call | solution.py:174
  55.7 32.3 %all-gather.6.cloned.1.call-done = bf16[1024,2048]{1,0:T(8,128)(2,1)} async-done(((bf16[128,2048]{1,0:T(8,128)(2,1)}), bf16[1024,2048]{1,0:T(8,128)(2,1)}) %all-gather.6.cloned.1.call-update) | async-done | bytes 4194320 | tf_op jit(solution)/shard_map/all_gather | solution.py:224
  88.0 9.3 %convolution_convert_fusion.1 = bf16[1024,1024]{1,0:T(8,128)(2,1)} fusion(bf16[1024,2048]{1,0:T(8,128)(2,1)} %all-gather.6.cloned.1.call-done, bf16[2048,1024]{1,0:T(8,128)(2,1)} %param.24), kind=kOutput, calls=%fused_computation.5 | convolution fusion | flops 4296015872 | bytes 10485760 | tf_op jit(solution)/shard_map/dot_general | solution.py:225
  97.3 5.9 %all-to-all-start = ((bf16[32,32,1024]{2,1,0:T(8,128)(2,1)}), bf16[32,32,1024]{2,1,0:T(8,128)(2,1)S(1)}, u32[]{:S(2)}, u32[]{:S(2)}) async-start(bf16[32,32,1024]{2,1,0:T(8,128)(2,1)} %bitcast.38), calls=%async_computation | async-start | bytes 4194304 | tf_op jit(solution)/shard_map/all_to_all | solution.py:227
  103.5 0.1 reduce.1
  103.6 27.3 %all-to-all-done = bf16[32,32,1024]{2,1,0:T(8,128)(2,1)S(1)} async-done(((bf16[32,32,1024]{2,1,0:T(8,128)(2,1)}), bf16[32,32,1024]{2,1,0:T(8,128)(2,1)S(1)}, u32[]{:S(2)}, u32[]{:S(2)}) %all-to-all-start) | async-done | bytes 2097184 | tf_op jit(solution)/shard_map/all_to_all | solution.py:227
  130.9 0.4 convert_reduce_fusion
  131.4 0.3 fusion.5
  131.7 0.2 fusion.9
  131.9 0.2 copy.34
  132.1 0.3 reduce_max.9
  132.5 0.3 div.38
  132.8 0.7 fusion.11
  133.5 0.9 convolution_convert_fusion
  134.5 51.6 %all-gather.8.cloned.1.call-done.refs_0_ = bf16[512,8192]{1,0:T(8,128)(2,1)} async-done(((bf16[16,8192]{1,0:T(8,128)(2,1)}), bf16[512,8192]{1,0:T(8,128)(2,1)}) %all-gather.8.cloned.1.call-update) | async-done | bytes 8388624 | tf_op jit(solution)/shard_map/all_gather | solution.py:262
  186.1 20.4 %shard_map.156 = bf16[512,8192]{1,0:T(8,128)(2,1)} custom-call(bf16[512,8192]{1,0:T(8,128)(2,1)} %all-gather.8.cloned.1.call-done.refs_0_, bf16[8192,384]{1,0:T(8,128)(2,1)} %refs_1_.1, bf16[8192,384]{1,0:T(8,128)(2,1)} %refs_2_.1, bf16[384,8192]{1,0:T(8,128)(2,1)} %refs_3_.1), custom_call_target="tpu_custom_call" | custom-call | flops 9663676416 | bytes 35651584 | tf_op jit(solution)/shard_map/pallas_call | solution.py:48
  206.6 0.3 fusion.4
  206.9 92.3 %reduce-scatter.2.cloned.1.call-done = bf16[16,8192]{1,0:T(8,128)(2,1)} async-done(((bf16[512,8192]{1,0:T(8,128)(2,1)}), bf16[16,8192]{1,0:T(8,128)(2,1)}) %reduce-scatter.2.cloned.1.call-update) | async-done | bytes 262160 | tf_op jit(solution)/shard_map/reduce_scatter | solution.py:263
  299.2 2.1 fusion.1
  (26 shorter events, 0.5 us)
Async XLA Ops:
  6.5 200.1 %copy-start = (bf16[8192,16]{0,1:T(8,128)(2,1)S(1)}, bf16[8192,16]{0,1:T(8,128)(2,1)}, u32[]{:S(2)}) copy-start(bf16[8192,16]{0,1:T(8,128)(2,1)} %param.27) | copy-start | bytes 786436
  6.5 37.1 %all-gather.10.cloned.1.call-start = ((), (), s32[]{:S(2)}) async-start(), calls=%async_computation.5 | async-start | bytes 1769472 | tf_op jit(solution)/shard_map/all_gather | solution.py:218
  16.4 71.7 %all-gather.6.cloned.1.call-start = ((), (), s32[]{:S(2)}) async-start(), calls=%async_computation.2 | async-start | bytes 4718592 | tf_op jit(solution)/shard_map/all_gather | solution.py:224
  97.3 6.0 %copy-start.3 = (s32[32,2]{0,1:T(2,128)S(1)}, s32[32,2]{0,1:T(2,128)}, u32[]{:S(2)}) copy-start(s32[32,2]{0,1:T(2,128)} %param.28) | copy-start | bytes 772
  97.3 34.1 %copy-start.1 = (bf16[32,8192]{1,0:T(8,128)(2,1)S(1)}, bf16[32,8192]{1,0:T(8,128)(2,1)}, u32[]{:S(2)}) copy-start(bf16[32,8192]{1,0:T(8,128)(2,1)} %param.25) | copy-start | bytes 1572868
  97.3 33.6 %all-to-all-start = ((bf16[32,32,1024]{2,1,0:T(8,128)(2,1)}), bf16[32,32,1024]{2,1,0:T(8,128)(2,1)S(1)}, u32[]{:S(2)}, u32[]{:S(2)}) async-start(bf16[32,32,1024]{2,1,0:T(8,128)(2,1)} %bitcast.38), calls=%async_computation | async-start | bytes 4194304 | tf_op jit(solution)/shard_map/all_to_all | solution.py:227
  103.2 28.5 %copy-start.2 = (f32[8192]{0:T(1024)S(1)}, f32[8192]{0:T(1024)}, u32[]{:S(2)}) copy-start(f32[8192]{0:T(1024)} %param.26) | copy-start | bytes 98308
  103.3 82.9 %all-gather.8.cloned.1.call-start = ((), (), s32[]{:S(2)}) async-start(), calls=%async_computation.3 | async-start | bytes 8650752 | tf_op jit(solution)/shard_map/all_gather | solution.py:262
  134.4 164.8 %reduce-scatter.2.cloned.1.call-start = ((), (), s32[]{:S(2)}) async-start(), calls=%async_computation.4 | async-start | bytes 8650752 | tf_op jit(solution)/shard_map/reduce_scatter | solution.py:263
Sparse Core Ops, SparseCore 0:
  16.5 27.1 all-gather.9
  55.8 32.1 all-gather.5
  134.5 51.5 all-gather.7
  206.7 92.4 reduce-scatter.1
